TPU v7x, 256 devices: a whole 4x4x8 slice. The times are simulated.
256 devices in a mesh: uly: 16 (over y, x), blk: 16 (over z, core).
Axes of the slice: x: 4, y: 4, z: 8, core: 2. Of those that a mesh axis runs over, the one named last changes fastest.
Arguments:
- query_rows: bfloat16 [98304, 2048], P(('uly', 'blk')), may hold values from -8 to 8
- key_rows: bfloat16 [98304, 2048], P(('uly', 'blk')), may hold values from -8 to 8
- value_rows: bfloat16 [98304, 2048], P(('uly', 'blk')), may hold values from -6 to 6
- kept_tiles: int32 [256, 6], replicated, may hold values from -1 to 255, as said below
Outputs:
- attended: bfloat16 [98304, 2048], P(('uly', 'blk'))
Inputs may be any that keep to these rules, and one draw needn't show every extreme that they name: `kept_tiles`: tile t = p * 16 + a with p = b * 4 + c has coordinates (b, a, c) with 0 <= b < 4, 0 <= a < 16, 0 <= c < 4; slab a is the tiles with that a, and p is a tile's position in its slab. Row t lists distinct tiles, t itself first, then the others, then -1 in the unused entries; every listed tile differs from t by at most 1 in each coordinate. For every slab a and each of the slabs a - 1 and a + 1, the tiles of that neighbouring slab listed by queries of slab a lie within 8 consecutive positions. Some row fills all 6 entries.
All inputs are finite; a program needn't handle non-finite values.
Results may differ from a plain program's by a relative error of at most 0.0047.
Values may be sent and summed in bfloat16 or wider, within the bound.
No kernel may reach another device: no remote copies, remote signals or barrier semaphores. Data moves between devices by JAX's collectives and lax.ppermute only.
A program may use at most 64 MiB of HBM per device.

v0:
```python
import jax
import jax.numpy as jnp
from jax import lax
from jax.sharding import PartitionSpec as P

HEAD_DIM = 128
TILE = 384
KEEP = 6


def passed_along(block, axis, distance):
    devices = range(lax.axis_size(axis))
    route = [(i - distance, i) for i in devices if i - distance in devices]
    return lax.ppermute(block, axis, route)


def tile_place(tile_ids, n_blk):
    slab_of = tile_ids % n_blk
    position = tile_ids // n_blk
    return (slab_of, position)


def slab_kept(kept_tiles, slab_index, n_blk, slab_tiles):
    position = jnp.arange(slab_tiles, dtype=jnp.int32)
    tile_ids = position * n_blk + slab_index
    return jnp.take(kept_tiles, tile_ids, axis=0)


def body(query_rows, key_rows, value_rows, kept_tiles):
    query_local, key_local, value_local = (
        lax.all_to_all(query_rows, "uly", split_axis=1, concat_axis=0, tiled=True),
        lax.all_to_all(key_rows, "uly", split_axis=1, concat_axis=0, tiled=True),
        lax.all_to_all(value_rows, "uly", split_axis=1, concat_axis=0, tiled=True),
    )
    n_uly = lax.axis_size("uly")
    n_blk = lax.axis_size("blk")
    feat_width = query_local.shape[1]
    head_dev = feat_width // HEAD_DIM
    slab_now = lax.axis_index("blk")
    score_scale = HEAD_DIM ** (-0.5)
    listed = slab_kept(kept_tiles, slab_now, n_blk, n_uly)
    is_live = listed >= 0
    slab_of, position = tile_place(jnp.where(is_live, listed, 0), n_blk)
    relative = slab_of - slab_now
    key_tiles = key_local.reshape(n_uly, TILE, feat_width)
    value_tiles = value_local.reshape(n_uly, TILE, feat_width)
    left_key, left_value = passed_along((key_tiles, value_tiles), "blk", 1)
    right_key, right_value = passed_along((key_tiles, value_tiles), "blk", -1)
    key_buffer = jnp.concatenate([left_key, key_tiles, right_key], axis=0)
    value_buffer = jnp.concatenate([left_value, value_tiles, right_value], axis=0)
    buffer_slot = (relative + 1) * n_uly + position
    buffer_slot = jnp.where(is_live, buffer_slot, 0)
    key_buffer = key_buffer.reshape(-1, TILE, head_dev, HEAD_DIM)
    value_buffer = value_buffer.reshape(-1, TILE, head_dev, HEAD_DIM)
    tile_group = 1
    while tile_group * TILE < 512 and n_uly % (tile_group * 2) == 0:
        tile_group = tile_group * 2
    block_count = n_uly // tile_group
    query_blocks = query_local.reshape(block_count, tile_group, TILE, head_dev, HEAD_DIM)
    slot_blocks = buffer_slot.reshape(block_count, tile_group, KEEP)
    live_blocks = is_live.reshape(block_count, tile_group, KEEP)

    def attend_block(block_args):
        query_block, slot_block, live_block = block_args
        key_gather = key_buffer[slot_block].reshape(tile_group, KEEP * TILE, head_dev, HEAD_DIM)
        value_gather = value_buffer[slot_block].reshape(tile_group, KEEP * TILE, head_dev, HEAD_DIM)
        scores = (
            jnp.einsum(
                "gihd,gjhd->ghij", query_block, key_gather, preferred_element_type=jnp.float32
            )
            * score_scale
        )
        live_cols = jnp.repeat(live_block, TILE, axis=1)
        scores = jnp.where(live_cols[:, None, None, :], scores, -jnp.inf)
        row_max = jnp.max(scores, axis=3, keepdims=True)
        weights = jnp.exp(scores - row_max)
        totals = jnp.sum(weights, axis=3)
        weights_low = weights.astype(jnp.bfloat16)
        mixed = jnp.einsum(
            "ghij,gjhd->gihd", weights_low, value_gather, preferred_element_type=jnp.float32
        )
        mixed = mixed / jnp.transpose(totals, (0, 2, 1))[:, :, :, None]
        return mixed.astype(jnp.bfloat16)

    attended = lax.map(attend_block, (query_blocks, slot_blocks, live_blocks))
    attended = attended.reshape(n_uly * TILE, feat_width)
    return lax.all_to_all(attended, "uly", split_axis=0, concat_axis=1, tiled=True)


def solution(mesh):
    placed = (P(("uly", "blk"), None), P(("uly", "blk"), None), P(("uly", "blk"), None), P())
    return jax.shard_map(
        body, mesh=mesh, in_specs=placed, out_specs=P(("uly", "blk"), None), check_vma=False
    )
```

profile of v0, /device:TPU:192, one launch (start us, length us, event | category | flops | bytes accessed | tf_op | source)
XLA Modules:
  0.0 268.4 jit_solution(9262955187034925305)
XLA Ops:
  0.0 2.7 %copy.30 = bf16[384,2048]{0,1:T(8,128)(2,1)} copy(bf16[384,2048]{1,0:T(8,128)(2,1)} %param.7) | data formatting | bytes 3145728 | tf_op args[1]
  2.7 7.0 %all-to-all-start.2 = ((bf16[384,16,128]{0,2,1:T(8,128)(2,1)}), bf16[384,16,128]{0,2,1:T(8,128)(2,1)S(1)}, u32[]{:S(2)}, u32[]{:S(2)}) async-start(bf16[384,16,128]{0,2,1:T(8,128)(2,1)} %bitcast.92), calls=%async_computation.2 | async-start | bytes 3145728 | tf_op jit(solution)/shard_map/all_to_all | solution.py:32
  9.8 2.6 copy.27
  12.4 21.9 %all-to-all-done.2 = bf16[384,16,128]{0,2,1:T(8,128)(2,1)S(1)} async-done(((bf16[384,16,128]{0,2,1:T(8,128)(2,1)}), bf16[384,16,128]{0,2,1:T(8,128)(2,1)S(1)}, u32[]{:S(2)}, u32[]{:S(2)}) %all-to-all-start.2) | async-done | bytes 1572896 | tf_op jit(solution)/shard_map/all_to_all | solution.py:32
  35.5 3.7 %all-to-all-start = ((bf16[384,16,128]{0,2,1:T(8,128)(2,1)}), bf16[384,16,128]{0,2,1:T(8,128)(2,1)S(1)}, u32[]{:S(2)}, u32[]{:S(2)}) async-start(bf16[384,16,128]{0,2,1:T(8,128)(2,1)} %bitcast.91), calls=%async_computation | async-start | bytes 3145728 | tf_op jit(solution)/shard_map/all_to_all | solution.py:33
  41.1 3.6 %collective-permute-start.3 = (bf16[16,384,128]{1,2,0:T(8,128)(2,1)}, bf16[16,384,128]{1,2,0:T(8,128)(2,1)}, u32[]{:S(2)}, u32[]{:S(2)}) collective-permute-start(bf16[16,384,128]{1,2,0:T(8,128)(2,1)} %bitcast.89), channel_id=1, source_target_pairs={{1,0},{2,1},{3,2},{4,3},{5,4},{6,5},{7,6},{8,7},{9,8},{10,9},{11,1... | collective-permute-start | bytes 4718600 | tf_op jit(solution)/shard_map/ppermute | solution.py:14
  44.8 17.7 %all-to-all-done = bf16[384,16,128]{0,2,1:T(8,128)(2,1)S(1)} async-done(((bf16[384,16,128]{0,2,1:T(8,128)(2,1)}), bf16[384,16,128]{0,2,1:T(8,128)(2,1)S(1)}, u32[]{:S(2)}, u32[]{:S(2)}) %all-to-all-start) | async-done | bytes 1572896 | tf_op jit(solution)/shard_map/all_to_all | solution.py:33
  64.4 3.6 %collective-permute-start.1 = (bf16[16,384,128]{1,2,0:T(8,128)(2,1)S(1)}, bf16[16,384,128]{1,2,0:T(8,128)(2,1)}, u32[]{:S(2)}, u32[]{:S(2)}) collective-permute-start(bf16[16,384,128]{1,2,0:T(8,128)(2,1)S(1)} %bitcast.86), channel_id=1, source_target_pairs={{1,0},{2,1},{3,2},{4,3},{5,4},{6,5},{7,6},{8,7},{9,8},{10,9},{11,1... | collective-permute-start | bytes 4718600 | tf_op jit(solution)/shard_map/ppermute | solution.py:14
  69.6 4.5 %all-to-all-start.1 = ((bf16[384,16,128]{2,0,1:T(8,128)(2,1)}), bf16[384,16,128]{2,0,1:T(8,128)(2,1)}, u32[]{:S(2)}, u32[]{:S(2)}) async-start(bf16[384,16,128]{2,0,1:T(8,128)(2,1)} %copy_bitcast_fusion), calls=%async_computation.1 | async-start | bytes 3145728 | tf_op jit(solution)/shard_map/all_to_all | solution.py:31
  75.2 4.1 %pad_maximum_fusion.1 = bf16[48,384,128]{1,2,0:T(8,128)(2,1)} fusion(bf16[16,384,128]{1,2,0:T(8,128)(2,1)} %collective-permute-done.3, bf16[16,384,128]{1,2,0:T(8,128)(2,1)} %bitcast.90, bf16[16,384,128]{1,2,0:T(8,128)(2,1)} %collective-permute-done.2), kind=kLoop, calls=%fused_computation.26 | loop fusion | flops 4718592 | bytes 9437184 | tf_op jit(solution)/shard_map/concatenate | solution.py:49
  79.3 6.7 %copy.31 = bf16[48,384,128]{2,1,0:T(8,128)(2,1)} copy(bf16[48,384,128]{1,2,0:T(8,128)(2,1)} %pad_maximum_fusion.1) | data formatting | bytes 9437184 | tf_op jit(solution)/shard_map/concatenate | solution.py:49
  86.0 3.9 %pad_maximum_fusion = bf16[48,384,128]{1,2,0:T(8,128)(2,1)} fusion(bf16[16,384,128]{1,2,0:T(8,128)(2,1)} %collective-permute-done.1, bf16[16,384,128]{1,2,0:T(8,128)(2,1)S(1)} %bitcast.87, bf16[16,384,128]{1,2,0:T(8,128)(2,1)} %collective-permute-done), kind=kLoop, calls=%fused_computation.25 | loop fusion | flops 4718592 | bytes 9437184 | tf_op jit(solution)/shard_map/concatenate | solution.py:50
  89.9 6.7 %copy.28 = bf16[48,384,128]{2,1,0:T(8,128)(2,1)} copy(bf16[48,384,128]{1,2,0:T(8,128)(2,1)} %pad_maximum_fusion) | data formatting | bytes 9437184 | tf_op jit(solution)/shard_map/concatenate | solution.py:50
  98.5 138.4 %while.10 = (s32[]{:T(128)}, bf16[8,2,384,1,128]{4,2,1,0,3:T(8,128)(2,1)}, s32[8,2,6]{2,1,0:T(2,128)S(1)}, bf16[48,384,1,128]{3,1,0,2:T(8,128)(2,1)}, pred[8,2,6...) while((s32[]{:T(128)}, ...), condition=%wide.region_3.4_spmd, body=%wide.region_0.3_spmd.sunk | while | flops 925629952 | bytes 57851372 | solution.py:85
  98.6 3.1 %gather_fusion.1 = bf16[12,384,128]{2,1,0:T(8,128)(2,1)S(1)} fusion(bf16[48,384,128]{2,1,0:T(8,128)(2,1)} %bitcast.82, s32[1024]{0:T(1024)S(1)} %pad_clamp_fusion.3), kind=kCustom, calls=%fused_computation.1.clone.1 | custom fusion | bytes 2359344 | tf_op jit(solution)/shard_map/while/body/eval_jaxpr/gather | solution.py:65
  101.8 2.2 fusion.44
  106.9 3.1 %gather_fusion = bf16[12,384,128]{2,1,0:T(8,128)(2,1)S(1)} fusion(bf16[48,384,128]{2,1,0:T(8,128)(2,1)} %bitcast.84, s32[1024]{0:T(1024)S(1)} %pad_clamp_fusion.3), kind=kCustom, calls=%fused_computation.clone.1 | custom fusion | bytes 2359344 | tf_op jit(solution)/shard_map/while/body/eval_jaxpr/gather | solution.py:66
  110.0 4.9 %fusion.46 = bf16[1,2,384,1,128]{2,4,1,3,0:T(8,128)(2,1)S(1)} fusion(bf16[2,2304,128]{2,1,0:T(8,128)(2,1)S(1)} %bitcast.80, f32[2,384,2304]{2,1,0:T(8,128)} %copy-done.1, f32[2,384]{1,0:T(2,128)S(1)} %get-tuple-element.105, pred[2,2304]{1,0:T(4,128)(4,1)S(1)} %bitcast.96, f32[2,384]{1,0:T(2,128)S(1)} %fusion.45), kind=kOutput, calls=%fused_computation.13.clone.1 | convolution fusion | flops 460259328 | bytes 8464896 | tf_op jit(solution)/shard_map/while/body/eval_jaxpr/ghij,gjhd->gihd/dot_general | solution.py:79
  115.9 3.1 %gather_fusion.1 = bf16[12,384,128]{2,1,0:T(8,128)(2,1)S(1)} fusion(bf16[48,384,128]{2,1,0:T(8,128)(2,1)} %bitcast.82, s32[1024]{0:T(1024)S(1)} %pad_clamp_fusion.3), kind=kCustom, calls=%fused_computation.1.clone.1 | custom fusion | bytes 2359344 | tf_op jit(solution)/shard_map/while/body/eval_jaxpr/gather | solution.py:65
  119.1 2.2 fusion.44
  124.2 3.1 %gather_fusion = bf16[12,384,128]{2,1,0:T(8,128)(2,1)S(1)} fusion(bf16[48,384,128]{2,1,0:T(8,128)(2,1)} %bitcast.84, s32[1024]{0:T(1024)S(1)} %pad_clamp_fusion.3), kind=kCustom, calls=%fused_computation.clone.1 | custom fusion | bytes 2359344 | tf_op jit(solution)/shard_map/while/body/eval_jaxpr/gather | solution.py:66
  127.3 4.9 %fusion.46 = bf16[1,2,384,1,128]{2,4,1,3,0:T(8,128)(2,1)S(1)} fusion(bf16[2,2304,128]{2,1,0:T(8,128)(2,1)S(1)} %bitcast.80, f32[2,384,2304]{2,1,0:T(8,128)} %copy-done.1, f32[2,384]{1,0:T(2,128)S(1)} %get-tuple-element.105, pred[2,2304]{1,0:T(4,128)(4,1)S(1)} %bitcast.96, f32[2,384]{1,0:T(2,128)S(1)} %fusion.45), kind=kOutput, calls=%fused_computation.13.clone.1 | convolution fusion | flops 460259328 | bytes 8464896 | tf_op jit(solution)/shard_map/while/body/eval_jaxpr/ghij,gjhd->gihd/dot_general | solution.py:79
  133.2 3.1 %gather_fusion.1 = bf16[12,384,128]{2,1,0:T(8,128)(2,1)S(1)} fusion(bf16[48,384,128]{2,1,0:T(8,128)(2,1)} %bitcast.82, s32[1024]{0:T(1024)S(1)} %pad_clamp_fusion.3), kind=kCustom, calls=%fused_computation.1.clone.1 | custom fusion | bytes 2359344 | tf_op jit(solution)/shard_map/while/body/eval_jaxpr/gather | solution.py:65
  136.4 2.2 fusion.44
  141.5 3.1 %gather_fusion = bf16[12,384,128]{2,1,0:T(8,128)(2,1)S(1)} fusion(bf16[48,384,128]{2,1,0:T(8,128)(2,1)} %bitcast.84, s32[1024]{0:T(1024)S(1)} %pad_clamp_fusion.3), kind=kCustom, calls=%fused_computation.clone.1 | custom fusion | bytes 2359344 | tf_op jit(solution)/shard_map/while/body/eval_jaxpr/gather | solution.py:66
  144.6 4.9 %fusion.46 = bf16[1,2,384,1,128]{2,4,1,3,0:T(8,128)(2,1)S(1)} fusion(bf16[2,2304,128]{2,1,0:T(8,128)(2,1)S(1)} %bitcast.80, f32[2,384,2304]{2,1,0:T(8,128)} %copy-done.1, f32[2,384]{1,0:T(2,128)S(1)} %get-tuple-element.105, pred[2,2304]{1,0:T(4,128)(4,1)S(1)} %bitcast.96, f32[2,384]{1,0:T(2,128)S(1)} %fusion.45), kind=kOutput, calls=%fused_computation.13.clone.1 | convolution fusion | flops 460259328 | bytes 8464896 | tf_op jit(solution)/shard_map/while/body/eval_jaxpr/ghij,gjhd->gihd/dot_general | solution.py:79
  150.5 3.1 %gather_fusion.1 = bf16[12,384,128]{2,1,0:T(8,128)(2,1)S(1)} fusion(bf16[48,384,128]{2,1,0:T(8,128)(2,1)} %bitcast.82, s32[1024]{0:T(1024)S(1)} %pad_clamp_fusion.3), kind=kCustom, calls=%fused_computation.1.clone.1 | custom fusion | bytes 2359344 | tf_op jit(solution)/shard_map/while/body/eval_jaxpr/gather | solution.py:65
  153.7 2.2 fusion.44
  158.8 3.1 %gather_fusion = bf16[12,384,128]{2,1,0:T(8,128)(2,1)S(1)} fusion(bf16[48,384,128]{2,1,0:T(8,128)(2,1)} %bitcast.84, s32[1024]{0:T(1024)S(1)} %pad_clamp_fusion.3), kind=kCustom, calls=%fused_computation.clone.1 | custom fusion | bytes 2359344 | tf_op jit(solution)/shard_map/while/body/eval_jaxpr/gather | solution.py:66
  161.9 4.9 %fusion.46 = bf16[1,2,384,1,128]{2,4,1,3,0:T(8,128)(2,1)S(1)} fusion(bf16[2,2304,128]{2,1,0:T(8,128)(2,1)S(1)} %bitcast.80, f32[2,384,2304]{2,1,0:T(8,128)} %copy-done.1, f32[2,384]{1,0:T(2,128)S(1)} %get-tuple-element.105, pred[2,2304]{1,0:T(4,128)(4,1)S(1)} %bitcast.96, f32[2,384]{1,0:T(2,128)S(1)} %fusion.45), kind=kOutput, calls=%fused_computation.13.clone.1 | convolution fusion | flops 460259328 | bytes 8464896 | tf_op jit(solution)/shard_map/while/body/eval_jaxpr/ghij,gjhd->gihd/dot_general | solution.py:79
  167.8 3.1 %gather_fusion.1 = bf16[12,384,128]{2,1,0:T(8,128)(2,1)S(1)} fusion(bf16[48,384,128]{2,1,0:T(8,128)(2,1)} %bitcast.82, s32[1024]{0:T(1024)S(1)} %pad_clamp_fusion.3), kind=kCustom, calls=%fused_computation.1.clone.1 | custom fusion | bytes 2359344 | tf_op jit(solution)/shard_map/while/body/eval_jaxpr/gather | solution.py:65
  171.0 2.2 fusion.44
  176.1 3.1 %gather_fusion = bf16[12,384,128]{2,1,0:T(8,128)(2,1)S(1)} fusion(bf16[48,384,128]{2,1,0:T(8,128)(2,1)} %bitcast.84, s32[1024]{0:T(1024)S(1)} %pad_clamp_fusion.3), kind=kCustom, calls=%fused_computation.clone.1 | custom fusion | bytes 2359344 | tf_op jit(solution)/shard_map/while/body/eval_jaxpr/gather | solution.py:66
  179.2 4.9 %fusion.46 = bf16[1,2,384,1,128]{2,4,1,3,0:T(8,128)(2,1)S(1)} fusion(bf16[2,2304,128]{2,1,0:T(8,128)(2,1)S(1)} %bitcast.80, f32[2,384,2304]{2,1,0:T(8,128)} %copy-done.1, f32[2,384]{1,0:T(2,128)S(1)} %get-tuple-element.105, pred[2,2304]{1,0:T(4,128)(4,1)S(1)} %bitcast.96, f32[2,384]{1,0:T(2,128)S(1)} %fusion.45), kind=kOutput, calls=%fused_computation.13.clone.1 | convolution fusion | flops 460259328 | bytes 8464896 | tf_op jit(solution)/shard_map/while/body/eval_jaxpr/ghij,gjhd->gihd/dot_general | solution.py:79
  185.1 3.1 %gather_fusion.1 = bf16[12,384,128]{2,1,0:T(8,128)(2,1)S(1)} fusion(bf16[48,384,128]{2,1,0:T(8,128)(2,1)} %bitcast.82, s32[1024]{0:T(1024)S(1)} %pad_clamp_fusion.3), kind=kCustom, calls=%fused_computation.1.clone.1 | custom fusion | bytes 2359344 | tf_op jit(solution)/shard_map/while/body/eval_jaxpr/gather | solution.py:65
  188.3 2.2 fusion.44
  193.4 3.1 %gather_fusion = bf16[12,384,128]{2,1,0:T(8,128)(2,1)S(1)} fusion(bf16[48,384,128]{2,1,0:T(8,128)(2,1)} %bitcast.84, s32[1024]{0:T(1024)S(1)} %pad_clamp_fusion.3), kind=kCustom, calls=%fused_computation.clone.1 | custom fusion | bytes 2359344 | tf_op jit(solution)/shard_map/while/body/eval_jaxpr/gather | solution.py:66
  196.5 4.9 %fusion.46 = bf16[1,2,384,1,128]{2,4,1,3,0:T(8,128)(2,1)S(1)} fusion(bf16[2,2304,128]{2,1,0:T(8,128)(2,1)S(1)} %bitcast.80, f32[2,384,2304]{2,1,0:T(8,128)} %copy-done.1, f32[2,384]{1,0:T(2,128)S(1)} %get-tuple-element.105, pred[2,2304]{1,0:T(4,128)(4,1)S(1)} %bitcast.96, f32[2,384]{1,0:T(2,128)S(1)} %fusion.45), kind=kOutput, calls=%fused_computation.13.clone.1 | convolution fusion | flops 460259328 | bytes 8464896 | tf_op jit(solution)/shard_map/while/body/eval_jaxpr/ghij,gjhd->gihd/dot_general | solution.py:79
  202.4 3.1 %gather_fusion.1 = bf16[12,384,128]{2,1,0:T(8,128)(2,1)S(1)} fusion(bf16[48,384,128]{2,1,0:T(8,128)(2,1)} %bitcast.82, s32[1024]{0:T(1024)S(1)} %pad_clamp_fusion.3), kind=kCustom, calls=%fused_computation.1.clone.1 | custom fusion | bytes 2359344 | tf_op jit(solution)/shard_map/while/body/eval_jaxpr/gather | solution.py:65
  205.6 2.2 fusion.44
  210.7 3.1 %gather_fusion = bf16[12,384,128]{2,1,0:T(8,128)(2,1)S(1)} fusion(bf16[48,384,128]{2,1,0:T(8,128)(2,1)} %bitcast.84, s32[1024]{0:T(1024)S(1)} %pad_clamp_fusion.3), kind=kCustom, calls=%fused_computation.clone.1 | custom fusion | bytes 2359344 | tf_op jit(solution)/shard_map/while/body/eval_jaxpr/gather | solution.py:66
  213.8 4.9 %fusion.46 = bf16[1,2,384,1,128]{2,4,1,3,0:T(8,128)(2,1)S(1)} fusion(bf16[2,2304,128]{2,1,0:T(8,128)(2,1)S(1)} %bitcast.80, f32[2,384,2304]{2,1,0:T(8,128)} %copy-done.1, f32[2,384]{1,0:T(2,128)S(1)} %get-tuple-element.105, pred[2,2304]{1,0:T(4,128)(4,1)S(1)} %bitcast.96, f32[2,384]{1,0:T(2,128)S(1)} %fusion.45), kind=kOutput, calls=%fused_computation.13.clone.1 | convolution fusion | flops 460259328 | bytes 8464896 | tf_op jit(solution)/shard_map/while/body/eval_jaxpr/ghij,gjhd->gihd/dot_general | solution.py:79
  219.7 3.1 %gather_fusion.1 = bf16[12,384,128]{2,1,0:T(8,128)(2,1)S(1)} fusion(bf16[48,384,128]{2,1,0:T(8,128)(2,1)} %bitcast.82, s32[1024]{0:T(1024)S(1)} %pad_clamp_fusion.3), kind=kCustom, calls=%fused_computation.1.clone.1 | custom fusion | bytes 2359344 | tf_op jit(solution)/shard_map/while/body/eval_jaxpr/gather | solution.py:65
  222.9 2.2 fusion.44
  228.0 3.1 %gather_fusion = bf16[12,384,128]{2,1,0:T(8,128)(2,1)S(1)} fusion(bf16[48,384,128]{2,1,0:T(8,128)(2,1)} %bitcast.84, s32[1024]{0:T(1024)S(1)} %pad_clamp_fusion.3), kind=kCustom, calls=%fused_computation.clone.1 | custom fusion | bytes 2359344 | tf_op jit(solution)/shard_map/while/body/eval_jaxpr/gather | solution.py:66
  231.1 4.9 %fusion.46 = bf16[1,2,384,1,128]{2,4,1,3,0:T(8,128)(2,1)S(1)} fusion(bf16[2,2304,128]{2,1,0:T(8,128)(2,1)S(1)} %bitcast.80, f32[2,384,2304]{2,1,0:T(8,128)} %copy-done.1, f32[2,384]{1,0:T(2,128)S(1)} %get-tuple-element.105, pred[2,2304]{1,0:T(4,128)(4,1)S(1)} %bitcast.96, f32[2,384]{1,0:T(2,128)S(1)} %fusion.45), kind=kOutput, calls=%fused_computation.13.clone.1 | convolution fusion | flops 460259328 | bytes 8464896 | tf_op jit(solution)/shard_map/while/body/eval_jaxpr/ghij,gjhd->gihd/dot_general | solution.py:79
  236.9 27.4 %all_to_all.67 = bf16[16,384,128]{2,1,0:T(8,128)(2,1)S(1)} all-to-all(bf16[16,384,128]{2,1,0:T(8,128)(2,1)} %bitcast.97), channel_id=1, replica_groups=mesh['uly'=16,'blk'=16] {'uly'}, dimensions={0} | all-to-all | bytes 3145728 | tf_op jit(solution)/shard_map/all_to_all | solution.py:87
  265.9 2.6 copy.34
  (111 shorter events, 42.8 us)
Async XLA Ops:
  0.0 68.0 %copy-start = (bf16[384,2048]{1,0:T(8,128)(2,1)S(1)}, bf16[384,2048]{1,0:T(8,128)(2,1)}, u32[]{:S(2)}) copy-start(bf16[384,2048]{1,0:T(8,128)(2,1)} %param.6) | copy-start | bytes 4718596
  2.7 31.6 %all-to-all-start.2 = ((bf16[384,16,128]{0,2,1:T(8,128)(2,1)}), bf16[384,16,128]{0,2,1:T(8,128)(2,1)S(1)}, u32[]{:S(2)}, u32[]{:S(2)}) async-start(bf16[384,16,128]{0,2,1:T(8,128)(2,1)} %bitcast.92), calls=%async_computation.2 | async-start | bytes 3145728 | tf_op jit(solution)/shard_map/all_to_all | solution.py:32
  34.3 1.2 copy-start.2
  35.5 27.0 %all-to-all-start = ((bf16[384,16,128]{0,2,1:T(8,128)(2,1)}), bf16[384,16,128]{0,2,1:T(8,128)(2,1)S(1)}, u32[]{:S(2)}, u32[]{:S(2)}) async-start(bf16[384,16,128]{0,2,1:T(8,128)(2,1)} %bitcast.91), calls=%async_computation | async-start | bytes 3145728 | tf_op jit(solution)/shard_map/all_to_all | solution.py:33
  39.2 35.9 %collective-permute-start.2 = (bf16[16,384,128]{1,2,0:T(8,128)(2,1)}, bf16[16,384,128]{1,2,0:T(8,128)(2,1)}, u32[]{:S(2)}, u32[]{:S(2)}) collective-permute-start(bf16[16,384,128]{1,2,0:T(8,128)(2,1)} %bitcast.88), channel_id=1, source_target_pairs={{0,1},{1,2},{2,3},{3,4},{4,5},{5,6},{6,7},{7,8},{8,9},{9,10},{10,1... | collective-permute-start | bytes 4718600 | tf_op jit(solution)/shard_map/ppermute | solution.py:14
  41.1 34.0 %collective-permute-start.3 = (bf16[16,384,128]{1,2,0:T(8,128)(2,1)}, bf16[16,384,128]{1,2,0:T(8,128)(2,1)}, u32[]{:S(2)}, u32[]{:S(2)}) collective-permute-start(bf16[16,384,128]{1,2,0:T(8,128)(2,1)} %bitcast.89), channel_id=1, source_target_pairs={{1,0},{2,1},{3,2},{4,3},{5,4},{6,5},{7,6},{8,7},{9,8},{10,9},{11,1... | collective-permute-start | bytes 4718600 | tf_op jit(solution)/shard_map/ppermute | solution.py:14
  62.4 23.6 %collective-permute-start = (bf16[16,384,128]{1,2,0:T(8,128)(2,1)S(1)}, bf16[16,384,128]{1,2,0:T(8,128)(2,1)}, u32[]{:S(2)}, u32[]{:S(2)}) collective-permute-start(bf16[16,384,128]{1,2,0:T(8,128)(2,1)S(1)} %bitcast.85), channel_id=1, source_target_pairs={{0,1},{1,2},{2,3},{3,4},{4,5},{5,6},{6,7},{7,8},{8,9},{9,10},{10,1... | collective-permute-start | bytes 4718600 | tf_op jit(solution)/shard_map/ppermute | solution.py:14
  64.4 21.7 %collective-permute-start.1 = (bf16[16,384,128]{1,2,0:T(8,128)(2,1)S(1)}, bf16[16,384,128]{1,2,0:T(8,128)(2,1)}, u32[]{:S(2)}, u32[]{:S(2)}) collective-permute-start(bf16[16,384,128]{1,2,0:T(8,128)(2,1)S(1)} %bitcast.86), channel_id=1, source_target_pairs={{1,0},{2,1},{3,2},{4,3},{5,4},{6,5},{7,6},{8,7},{9,8},{10,9},{11,1... | collective-permute-start | bytes 4718600 | tf_op jit(solution)/shard_map/ppermute | solution.py:14
  69.6 4.6 %copy-start.3 = (s32[256,6]{0,1:T(8,128)S(1)}, s32[256,6]{0,1:T(8,128)}, u32[]{:S(2)}) copy-start(s32[256,6]{0,1:T(8,128)} %param.9) | copy-start | bytes 18436
  69.6 28.9 %all-to-all-start.1 = ((bf16[384,16,128]{2,0,1:T(8,128)(2,1)}), bf16[384,16,128]{2,0,1:T(8,128)(2,1)}, u32[]{:S(2)}, u32[]{:S(2)}) async-start(bf16[384,16,128]{2,0,1:T(8,128)(2,1)} %copy_bitcast_fusion), calls=%async_computation.1 | async-start | bytes 3145728 | tf_op jit(solution)/shard_map/all_to_all | solution.py:31
  104.0 2.9 %copy-start.1 = (f32[2,384,2304]{2,1,0:T(8,128)}, f32[2,384,2304]{2,1,0:T(8,128)S(1)}, u32[]{:S(2)}) copy-start(f32[2,384,2304]{2,1,0:T(8,128)S(1)} %get-tuple-element.104) | copy-start | bytes 21233668 | tf_op jit(solution)/shard_map/while
  121.3 2.9 %copy-start.1 = (f32[2,384,2304]{2,1,0:T(8,128)}, f32[2,384,2304]{2,1,0:T(8,128)S(1)}, u32[]{:S(2)}) copy-start(f32[2,384,2304]{2,1,0:T(8,128)S(1)} %get-tuple-element.104) | copy-start | bytes 21233668 | tf_op jit(solution)/shard_map/while
  138.6 2.9 %copy-start.1 = (f32[2,384,2304]{2,1,0:T(8,128)}, f32[2,384,2304]{2,1,0:T(8,128)S(1)}, u32[]{:S(2)}) copy-start(f32[2,384,2304]{2,1,0:T(8,128)S(1)} %get-tuple-element.104) | copy-start | bytes 21233668 | tf_op jit(solution)/shard_map/while
  155.9 2.9 %copy-start.1 = (f32[2,384,2304]{2,1,0:T(8,128)}, f32[2,384,2304]{2,1,0:T(8,128)S(1)}, u32[]{:S(2)}) copy-start(f32[2,384,2304]{2,1,0:T(8,128)S(1)} %get-tuple-element.104) | copy-start | bytes 21233668 | tf_op jit(solution)/shard_map/while
  173.2 2.9 %copy-start.1 = (f32[2,384,2304]{2,1,0:T(8,128)}, f32[2,384,2304]{2,1,0:T(8,128)S(1)}, u32[]{:S(2)}) copy-start(f32[2,384,2304]{2,1,0:T(8,128)S(1)} %get-tuple-element.104) | copy-start | bytes 21233668 | tf_op jit(solution)/shard_map/while
  190.5 2.9 %copy-start.1 = (f32[2,384,2304]{2,1,0:T(8,128)}, f32[2,384,2304]{2,1,0:T(8,128)S(1)}, u32[]{:S(2)}) copy-start(f32[2,384,2304]{2,1,0:T(8,128)S(1)} %get-tuple-element.104) | copy-start | bytes 21233668 | tf_op jit(solution)/shard_map/while
  207.8 2.9 %copy-start.1 = (f32[2,384,2304]{2,1,0:T(8,128)}, f32[2,384,2304]{2,1,0:T(8,128)S(1)}, u32[]{:S(2)}) copy-start(f32[2,384,2304]{2,1,0:T(8,128)S(1)} %get-tuple-element.104) | copy-start | bytes 21233668 | tf_op jit(solution)/shard_map/while
  225.1 2.9 %copy-start.1 = (f32[2,384,2304]{2,1,0:T(8,128)}, f32[2,384,2304]{2,1,0:T(8,128)S(1)}, u32[]{:S(2)}) copy-start(f32[2,384,2304]{2,1,0:T(8,128)S(1)} %get-tuple-element.104) | copy-start | bytes 21233668 | tf_op jit(solution)/shard_map/while
where the time goes:
time: 273 us; the launch traced here: 268 us
  local copies, waits for them, and re-layouts  94.7 us (35%)
  matrix products  56.5 us (21%)
  waiting for transfers between devices  41.5 us (15%)
  blocking collectives  27.4 us (10%)
  starting transfers between devices  26.4 us (10%)
  other arithmetic  21.4 us (8%)
    dot_general x8, matrix products, attend_block(): jnp.einsum('ghij,gjhd->gihd', weights_low, value_gather, preferred_elemen...  39.2 us
    all_to_all x1, blocking collectives, body(): lax.all_to_all(attended, 'uly', split_axis=0, concat_axis=1, tiled=True)  27.4 us
    gather x8, local copies, waits for them, and re-layouts, attend_block(): key_buffer[slot_block].reshape(tile_group, KEEP * TILE, head_dev, HEAD_DIM)  24.9 us
    gather x8, local copies, waits for them, and re-layouts, attend_block(): value_buffer[slot_block]  24.9 us
    all_to_all x1, waiting for transfers between devices, body(): lax.all_to_all(key_rows, 'uly', split_axis=1, concat_axis=0, tiled=True)  21.9 us
    all_to_all x1, waiting for transfers between devices, body(): lax.all_to_all(value_rows, 'uly', split_axis=1, concat_axis=0, tiled=True)  17.7 us
    dot_general x8, matrix products, attend_block(): jnp.einsum('gihd,gjhd->ghij', query_block, key_gather, preferred_element_...  17.3 us
    reduce_sum x8, other arithmetic, attend_block(): totals = jnp.sum(weights, axis=3)  13.1 us
  transfers between devices with their start and end apart: 7, of which 3 were waited for; matrix products, arithmetic and copies ran while one was open for 10% of the time, Pallas kernels for 0%

commit v1 on v0

v1 whole, which is shorter than its diff:
```python
import functools

import jax
import jax.numpy as jnp
from jax import lax
from jax.experimental import pallas as pl
from jax.experimental.pallas import tpu as pltpu
from jax.sharding import PartitionSpec as P

HEAD_DIM = 128
TILE = 384
KEEP = 6
USED = 8


def passed_along(block, axis, distance):
    devices = range(lax.axis_size(axis))
    route = [(i - distance, i) for i in devices if i - distance in devices]
    return lax.ppermute(block, axis, route)


def run_starts(kept_tiles, n_blk, slab_tiles):
    rows = kept_tiles.shape[0]
    row_slab = (jnp.arange(rows, dtype=jnp.int32) % n_blk)[:, None]
    live = kept_tiles >= 0
    entry_slab = jnp.where(live, kept_tiles % n_blk, -5)
    entry_pos = kept_tiles // n_blk
    slabs = jnp.arange(n_blk, dtype=jnp.int32)
    big = jnp.int32(slab_tiles + 1)

    def start_for(shift):
        hit = (row_slab[None] == slabs[:, None, None]) & (
            entry_slab[None] == slabs[:, None, None] + shift
        )
        low = jnp.min(jnp.where(hit, entry_pos[None], big), axis=(1, 2))
        return jnp.where(low == big, 0, jnp.minimum(low, slab_tiles - USED))

    return start_for(-1), start_for(1)


def attend_kernel(which_ref, index_ref, count_ref, q_ref, kl_ref, kc_ref, kr_ref,
                  vl_ref, vc_ref, vr_ref, o_ref, s_scr, m_scr, l_scr, acc_scr):
    i = pl.program_id(0)
    n = count_ref[i]
    score_scale = HEAD_DIM ** (-0.5)
    q = q_ref[0]

    def pick(l_ref, c_ref, r_ref, j):
        w = which_ref[i * KEEP + j]
        x = index_ref[i * KEEP + j]
        side = l_ref.shape[0] - 1
        own = c_ref.shape[0] - 1
        a = l_ref[jnp.clip(x, 0, side)]
        b = c_ref[jnp.clip(x, 0, own)]
        c = r_ref[jnp.clip(x, 0, side)]
        return jnp.where(w == 0, a, jnp.where(w == 1, b, c))

    for j in range(KEEP):
        @pl.when(j < n)
        def _():
            k = pick(kl_ref, kc_ref, kr_ref, j)
            s = lax.dot_general(q, k, (((1,), (1,)), ((), ())),
                                preferred_element_type=jnp.float32) * score_scale
            s_scr[j] = s
            mj = jnp.max(s, axis=1, keepdims=True)
            if j == 0:
                m_scr[...] = mj
            else:
                m_scr[...] = jnp.maximum(m_scr[...], mj)

    m = m_scr[...]
    for j in range(KEEP):
        @pl.when(j < n)
        def _():
            p = jnp.exp(s_scr[j] - m)
            lsum = jnp.sum(p, axis=1, keepdims=True)
            v = pick(vl_ref, vc_ref, vr_ref, j)
            pv = jnp.dot(p.astype(jnp.bfloat16), v, preferred_element_type=jnp.float32)
            if j == 0:
                l_scr[...] = lsum
                acc_scr[...] = pv
            else:
                l_scr[...] = l_scr[...] + lsum
                acc_scr[...] = acc_scr[...] + pv

    o_ref[0] = (acc_scr[...] / l_scr[...]).astype(o_ref.dtype)


def attend(which, index, count, q, kl, kc, kr, vl, vc, vr):
    n_q, tile, width = q.shape
    side = kl.shape[0]
    own = kc.shape[0]
    whole_side = pl.BlockSpec((side, tile, width), lambda i, *_: (0, 0, 0))
    whole_own = pl.BlockSpec((own, tile, width), lambda i, *_: (0, 0, 0))
    one = pl.BlockSpec((1, tile, width), lambda i, *_: (i, 0, 0))
    grid_spec = pltpu.PrefetchScalarGridSpec(
        num_scalar_prefetch=3,
        grid=(n_q,),
        in_specs=[one, whole_side, whole_own, whole_side, whole_side, whole_own, whole_side],
        out_specs=one,
        scratch_shapes=[
            pltpu.VMEM((KEEP, tile, tile), jnp.float32),
            pltpu.VMEM((tile, 1), jnp.float32),
            pltpu.VMEM((tile, 1), jnp.float32),
            pltpu.VMEM((tile, width), jnp.float32),
        ],
    )
    flops = n_q * KEEP * tile * tile * width * 4
    cost = pl.CostEstimate(
        flops=flops,
        transcendentals=n_q * KEEP * tile * tile,
        bytes_accessed=2 * (q.size * 2 + (kl.size + kc.size + kr.size) * 2),
    )
    return pl.pallas_call(
        attend_kernel,
        grid_spec=grid_spec,
        out_shape=jax.ShapeDtypeStruct(q.shape, q.dtype),
        compiler_params=pltpu.CompilerParams(dimension_semantics=("arbitrary",)),
        cost_estimate=cost,
    )(which, index, count, q, kl, kc, kr, vl, vc, vr)


def body(query_rows, key_rows, value_rows, kept_tiles):
    query_local, key_local, value_local = (
        lax.all_to_all(query_rows, "uly", split_axis=1, concat_axis=0, tiled=True),
        lax.all_to_all(key_rows, "uly", split_axis=1, concat_axis=0, tiled=True),
        lax.all_to_all(value_rows, "uly", split_axis=1, concat_axis=0, tiled=True),
    )
    n_uly = lax.axis_size("uly")
    n_blk = lax.axis_size("blk")
    feat_width = query_local.shape[1]
    slab_now = lax.axis_index("blk")

    from_left, from_right = run_starts(kept_tiles, n_blk, n_uly)
    key_tiles = key_local.reshape(n_uly, TILE, feat_width)
    value_tiles = value_local.reshape(n_uly, TILE, feat_width)
    query_tiles = query_local.reshape(n_uly, TILE, feat_width)

    to_next = from_left[jnp.minimum(slab_now + 1, n_blk - 1)]
    to_prev = from_right[jnp.maximum(slab_now - 1, 0)]
    run_next = (
        lax.dynamic_slice_in_dim(key_tiles, to_next, USED, 0),
        lax.dynamic_slice_in_dim(value_tiles, to_next, USED, 0),
    )
    run_prev = (
        lax.dynamic_slice_in_dim(key_tiles, to_prev, USED, 0),
        lax.dynamic_slice_in_dim(value_tiles, to_prev, USED, 0),
    )
    left_key, left_value = passed_along(run_next, "blk", 1)
    right_key, right_value = passed_along(run_prev, "blk", -1)

    position = jnp.arange(n_uly, dtype=jnp.int32)
    listed = jnp.take(kept_tiles, position * n_blk + slab_now, axis=0)
    is_live = listed >= 0
    safe = jnp.where(is_live, listed, 0)
    relative = safe % n_blk - slab_now
    tile_pos = safe // n_blk
    which = (relative + 1).astype(jnp.int32)
    index = jnp.where(
        relative == 0,
        tile_pos,
        jnp.where(relative < 0, tile_pos - from_left[slab_now], tile_pos - from_right[slab_now]),
    ).astype(jnp.int32)
    index = jnp.where(is_live, index, 0)
    which = jnp.where(is_live, which, 1)
    count = jnp.sum(is_live.astype(jnp.int32), axis=1)

    attended = attend(
        which.reshape(-1), index.reshape(-1), count,
        query_tiles, left_key, key_tiles, right_key, left_value, value_tiles, right_value,
    )
    attended = attended.reshape(n_uly * TILE, feat_width)
    return lax.all_to_all(attended, "uly", split_axis=0, concat_axis=1, tiled=True)


def solution(mesh):
    placed = (P(("uly", "blk"), None), P(("uly", "blk"), None), P(("uly", "blk"), None), P())
    return jax.shard_map(
        body, mesh=mesh, in_specs=placed, out_specs=P(("uly", "blk"), None), check_vma=False
    )
```

time: 273 us -> 194 us (0.71); the launches traced: 268 us -> 192 us
  local copies, waits for them, and re-layouts: 94.7 us -> 18.2 us
  Pallas kernels: 0 us -> 69.7 us
  matrix products: 56.5 us -> 0 us
  other arithmetic: 21.4 us -> 2.74 us
  waiting for transfers between devices: 41.5 us -> 50.2 us
  blocking collectives: 27.4 us -> 22.9 us
  between operations: 0.15 us -> 3.94 us
    pallas_call x0 -> x1, Pallas kernels: none -> 69.7 us  [attend(): pl.pallas_call(attend_kernel, grid_spec=grid_spec, out_shape=jax.ShapeDty...]
    dot_general x16 -> x0, matrix products: 56.5 us -> none  [the longest x8 39.2 us: attend_block(): jnp.einsum('ghij,gjhd->gihd', weights_low, value_gather, preferred_elemen...]
    gather x17 -> x1, local copies, waits for them, and re-layouts: 50.3 us -> 0.56 us  [body(): listed = jnp.take(kept_tiles, position * n_blk + slab_now, axis=0)]
    concatenate x2 -> x0, local copies, waits for them, and re-layouts: 13.4 us -> none  [the longest x1 6.72 us: body(): key_buffer = jnp.concatenate([left_key, key_tiles, right_key], axis=0)]
    reduce_sum x8 -> x1, other arithmetic: 13.1 us -> 0.67 us  [body(): count = jnp.sum(is_live.astype(jnp.int32), axis=1)]
    while x32 -> x0, local copies, waits for them, and re-layouts: 10.9 us -> none
    concatenate x2 -> x0, other arithmetic: 8.01 us -> none  [the longest x1 4.13 us: body(): key_buffer = jnp.concatenate([left_key, key_tiles, right_key], axis=0)]
    ppermute x4, waiting for transfers between devices: 0.01 us -> 7.99 us  [passed_along(): return lax.ppermute(block, axis, route)]
  transfers between devices with their start and end apart: 7 -> 7, of which waited for: 3 -> 5; matrix products, arithmetic and copies ran while one was open for 10% -> 8% of each run, Pallas kernels for 0% -> 0%
where the time goes in v1:
time: 194 us; the launch traced here: 192 us
  Pallas kernels  69.7 us (36%)
  waiting for transfers between devices  50.2 us (26%)
  starting transfers between devices  24.5 us (13%)
  blocking collectives  22.9 us (12%)
  local copies, waits for them, and re-layouts  18.2 us (9%)
  between operations  3.94 us (2%)
  other arithmetic  2.74 us (1%)
    pallas_call x1, Pallas kernels, attend(): pl.pallas_call(attend_kernel, grid_spec=grid_spec, out_shape=jax.ShapeDty...  69.7 us
    all_to_all x1, blocking collectives, body(): lax.all_to_all(attended, 'uly', split_axis=0, concat_axis=1, tiled=True)  22.9 us
    all_to_all x1, waiting for transfers between devices, body(): lax.all_to_all(key_rows, 'uly', split_axis=1, concat_axis=0, tiled=True)  21 us
    all_to_all x1, waiting for transfers between devices, body(): lax.all_to_all(value_rows, 'uly', split_axis=1, concat_axis=0, tiled=True)  18 us
    ppermute x4, starting transfers between devices, passed_along(): return lax.ppermute(block, axis, route)  9.39 us
    ppermute x4, waiting for transfers between devices, passed_along(): return lax.ppermute(block, axis, route)  7.99 us
    all_to_all x1, starting transfers between devices, body(): lax.all_to_all(key_rows, 'uly', split_axis=1, concat_axis=0, tiled=True)  7.03 us
    unnamed x12, local copies, waits for them, and re-layouts  6.47 us
  transfers between devices with their start and end apart: 7, of which 5 were waited for; matrix products, arithmetic and copies ran while one was open for 8% of the time, Pallas kernels for 0%

profile of v1, /device:TPU:192, one launch (start us, length us, event | category | flops | bytes accessed | tf_op | source)
XLA Modules:
  0.0 192.3 jit_solution(18024587604975872578)
XLA Ops:
  0.0 1.9 copy.22
  1.9 1.6 copy.23
  3.5 7.0 %all-to-all-start.1 = ((bf16[384,16,128]{2,0,1:T(8,128)(2,1)}), bf16[384,16,128]{2,0,1:T(8,128)(2,1)S(1)}, u32[]{:S(2)}, u32[]{:S(2)}) async-start(bf16[384,16,128]{2,0,1:T(8,128)(2,1)} %copy.23), calls=%async_computation.1 | async-start | bytes 3145728 | tf_op jit(solution)/shard_map/all_to_all | solution.py:126
  10.5 1.9 copy.24
  12.4 1.6 copy.25
  14.1 21.0 %all-to-all-done.1 = bf16[384,16,128]{2,0,1:T(8,128)(2,1)S(1)} async-done(((bf16[384,16,128]{2,0,1:T(8,128)(2,1)}), bf16[384,16,128]{2,0,1:T(8,128)(2,1)S(1)}, u32[]{:S(2)}, u32[]{:S(2)}) %all-to-all-start.1) | async-done | bytes 1572896 | tf_op jit(solution)/shard_map/all_to_all | solution.py:126
  35.1 0.0 copy-start
  35.1 3.7 %all-to-all-start.2 = ((bf16[384,16,128]{2,0,1:T(8,128)(2,1)}), bf16[384,16,128]{2,0,1:T(8,128)(2,1)S(1)}, u32[]{:S(2)}, u32[]{:S(2)}) async-start(bf16[384,16,128]{2,0,1:T(8,128)(2,1)} %copy.25), calls=%async_computation.2 | async-start | bytes 3145728 | tf_op jit(solution)/shard_map/all_to_all | solution.py:127
  38.8 2.6 %copy.20 = bf16[384,2048]{0,1:T(8,128)(2,1)} copy(bf16[384,2048]{1,0:T(8,128)(2,1)} %param.4) | data formatting | bytes 3145728 | tf_op args[0]
  41.4 0.0 copy-start.2
  41.4 2.6 %copy.21 = bf16[384,16,128]{2,0,1:T(8,128)(2,1)} copy(bf16[384,16,128]{0,2,1:T(8,128)(2,1)} %bitcast.28) | data formatting | bytes 3145728 | tf_op jit(solution)/shard_map/all_to_all | solution.py:125
  44.0 0.0 copy-done.2
  44.0 18.0 %all-to-all-done.2 = bf16[384,16,128]{2,0,1:T(8,128)(2,1)S(1)} async-done(((bf16[384,16,128]{2,0,1:T(8,128)(2,1)}), bf16[384,16,128]{2,0,1:T(8,128)(2,1)S(1)}, u32[]{:S(2)}, u32[]{:S(2)}) %all-to-all-start.2) | async-done | bytes 1572896 | tf_op jit(solution)/shard_map/all_to_all | solution.py:127
  62.0 0.0 copy-start.1
  62.0 4.4 %all-to-all-start = ((bf16[384,16,128]{2,0,1:T(8,128)(2,1)}), bf16[384,16,128]{2,0,1:T(8,128)(2,1)}, u32[]{:S(2)}, u32[]{:S(2)}) async-start(bf16[384,16,128]{2,0,1:T(8,128)(2,1)} %copy.21), calls=%async_computation | async-start | bytes 3145728 | tf_op jit(solution)/shard_map/all_to_all | solution.py:125
  66.5 0.2 select_reduce_fusion.1
  66.7 0.7 fusion.5
  68.6 0.6 fusion.6
  71.7 0.0 copy-done.1
  71.8 1.4 dynamic-slice_bitcast_fusion
  73.1 1.9 collective-permute-start.3
  75.0 2.4 %collective-permute-start.2 = (bf16[8,384,128]{2,1,0:T(8,128)(2,1)}, bf16[8,384,128]{2,1,0:T(8,128)(2,1)}, u32[]{:S(2)}, u32[]{:S(2)}) collective-permute-start(bf16[8,384,128]{2,1,0:T(8,128)(2,1)} %get-tuple-element.10), channel_id=1, source_target_pairs={{0,1},{1,2},{2,3},{3,4},{4,5},{5,6},{6,7},{7,8},{8,9},{9,10},{10,1... | collective-permute-start | bytes 2359304 | tf_op jit(solution)/shard_map/ppermute | solution.py:19
  77.4 0.0 copy-done
  77.5 0.1 dynamic-slice_bitcast_fusion.2
  77.6 3.2 %collective-permute-start.1 = (bf16[8,384,128]{2,1,0:T(8,128)(2,1)S(1)}, bf16[8,384,128]{2,1,0:T(8,128)(2,1)S(1)}, u32[]{:S(2)}, u32[]{:S(2)}) collective-permute-start(bf16[8,384,128]{2,1,0:T(8,128)(2,1)S(1)} %get-tuple-element.11), channel_id=1, source_target_pairs={{1,0},{2,1},{3,2},{4,3},{5,4},{6,5},{7,6},{8,7},{9,8},{10,9},{11,1... | collective-permute-start | bytes 2359304 | tf_op jit(solution)/shard_map/ppermute | solution.py:19
  80.7 1.9 collective-permute-start
  82.7 0.1 copy.19
  82.8 0.6 gather_fusion
  83.4 0.7 convert_reduce_fusion
  84.1 0.1 select_n.122
  84.2 1.8 compare_select_fusion.9
  85.9 3.1 %all-to-all-done = bf16[384,16,128]{2,0,1:T(8,128)(2,1)} async-done(((bf16[384,16,128]{2,0,1:T(8,128)(2,1)}), bf16[384,16,128]{2,0,1:T(8,128)(2,1)}, u32[]{:S(2)}, u32[]{:S(2)}) %all-to-all-start) | async-done | bytes 1572896 | tf_op jit(solution)/shard_map/all_to_all | solution.py:125
  89.1 0.0 collective-permute-done.3.vr_ref
  89.1 0.0 collective-permute-done.2.vl_ref
  89.1 4.1 %collective-permute-done.1.kr_ref = bf16[8,384,128]{2,1,0:T(8,128)(2,1)S(1)} collective-permute-done((bf16[8,384,128]{2,1,0:T(8,128)(2,1)S(1)}, bf16[8,384,128]{2,1,0:T(8,128)(2,1)S(1)}, u32[]{:S(2)}, u32[]{:S(2)}) %collective-permute-start.1) | collective-permute-done | bytes 786464 | tf_op jit(solution)/shard_map/ppermute | solution.py:19
  93.1 0.0 copy-start.3
  93.2 3.9 %collective-permute-done.kl_ref = bf16[8,384,128]{2,1,0:T(8,128)(2,1)} collective-permute-done((bf16[8,384,128]{2,1,0:T(8,128)(2,1)S(1)}, bf16[8,384,128]{2,1,0:T(8,128)(2,1)}, u32[]{:S(2)}, u32[]{:S(2)}) %collective-permute-start) | collective-permute-done | bytes 786464 | tf_op jit(solution)/shard_map/ppermute | solution.py:19
  97.1 0.0 copy-done.3
  97.1 69.7 %shard_map.46 = bf16[16,384,128]{2,1,0:T(8,128)(2,1)} custom-call(s32[96]{0:T(128)} %get-tuple-element.20.which_ref, s32[96]{0:T(128)} %get-tuple-element.19.index_ref, s32[16]{0:T(128)} %get-tuple-element.7.count_ref, bf16[16,384,128]{2,1,0:T(8,128)(2,1)} %bitcast.4.q_ref, bf16[8,384,128]{2,1,0:T(8,128)(2,1)} %collective-permute-done.kl_ref, ...), custom_call_target="tpu_custom_call" | custom-call | flops 7247757312 | bytes 9437184 | tf_op jit(solution)/shard_map/pallas_call | solution.py:114
  166.8 22.9 %all_to_all.64 = bf16[16,384,128]{2,1,0:T(8,128)(2,1)S(1)} all-to-all(bf16[16,384,128]{2,1,0:T(8,128)(2,1)} %shard_map.46), channel_id=1, replica_groups=mesh['uly'=16,'blk'=16] {'uly'}, dimensions={0} | all-to-all | bytes 3145728 | tf_op jit(solution)/shard_map/all_to_all | solution.py:173
  189.8 0.9 copy.26
  190.6 1.6 copy.27
  (9 shorter events, 0.1 us)
Async XLA Ops:
  3.5 31.6 %all-to-all-start.1 = ((bf16[384,16,128]{2,0,1:T(8,128)(2,1)}), bf16[384,16,128]{2,0,1:T(8,128)(2,1)S(1)}, u32[]{:S(2)}, u32[]{:S(2)}) async-start(bf16[384,16,128]{2,0,1:T(8,128)(2,1)} %copy.23), calls=%async_computation.1 | async-start | bytes 3145728 | tf_op jit(solution)/shard_map/all_to_all | solution.py:126
  35.1 42.4 %copy-start = (bf16[384,16,128]{2,0,1:T(8,128)(2,1)}, bf16[384,16,128]{2,0,1:T(8,128)(2,1)S(1)}, u32[]{:S(2)}) copy-start(bf16[384,16,128]{2,0,1:T(8,128)(2,1)S(1)} %all-to-all-done.1) | copy-start | bytes 4718596
  35.1 27.0 %all-to-all-start.2 = ((bf16[384,16,128]{2,0,1:T(8,128)(2,1)}), bf16[384,16,128]{2,0,1:T(8,128)(2,1)S(1)}, u32[]{:S(2)}, u32[]{:S(2)}) async-start(bf16[384,16,128]{2,0,1:T(8,128)(2,1)} %copy.25), calls=%async_computation.2 | async-start | bytes 3145728 | tf_op jit(solution)/shard_map/all_to_all | solution.py:127
  41.4 2.6 %copy-start.2 = (s32[256,6]{0,1:T(8,128)S(1)}, s32[256,6]{0,1:T(8,128)}, u32[]{:S(2)}) copy-start(s32[256,6]{0,1:T(8,128)} %param.7) | copy-start | bytes 18436
  62.0 9.7 %copy-start.1 = (bf16[384,16,128]{2,0,1:T(8,128)(2,1)}, bf16[384,16,128]{2,0,1:T(8,128)(2,1)S(1)}, u32[]{:S(2)}) copy-start(bf16[384,16,128]{2,0,1:T(8,128)(2,1)S(1)} %all-to-all-done.2) | copy-start | bytes 4718596
  62.0 27.0 %all-to-all-start = ((bf16[384,16,128]{2,0,1:T(8,128)(2,1)}), bf16[384,16,128]{2,0,1:T(8,128)(2,1)}, u32[]{:S(2)}, u32[]{:S(2)}) async-start(bf16[384,16,128]{2,0,1:T(8,128)(2,1)} %copy.21), calls=%async_computation | async-start | bytes 3145728 | tf_op jit(solution)/shard_map/all_to_all | solution.py:125
  73.1 16.0 %collective-permute-start.3 = (bf16[8,384,128]{2,1,0:T(8,128)(2,1)}, bf16[8,384,128]{2,1,0:T(8,128)(2,1)}, u32[]{:S(2)}, u32[]{:S(2)}) collective-permute-start(bf16[8,384,128]{2,1,0:T(8,128)(2,1)} %get-tuple-element.9), channel_id=1, source_target_pairs={{1,0},{2,1},{3,2},{4,3},{5,4},{6,5},{7,6},{8,7},{9,8},{10,9},{11,1... | collective-permute-start | bytes 2359304 | tf_op jit(solution)/shard_map/ppermute | solution.py:19
  75.0 14.1 %collective-permute-start.2 = (bf16[8,384,128]{2,1,0:T(8,128)(2,1)}, bf16[8,384,128]{2,1,0:T(8,128)(2,1)}, u32[]{:S(2)}, u32[]{:S(2)}) collective-permute-start(bf16[8,384,128]{2,1,0:T(8,128)(2,1)} %get-tuple-element.10), channel_id=1, source_target_pairs={{0,1},{1,2},{2,3},{3,4},{4,5},{5,6},{6,7},{7,8},{8,9},{9,10},{10,1... | collective-permute-start | bytes 2359304 | tf_op jit(solution)/shard_map/ppermute | solution.py:19
  77.6 15.6 %collective-permute-start.1 = (bf16[8,384,128]{2,1,0:T(8,128)(2,1)S(1)}, bf16[8,384,128]{2,1,0:T(8,128)(2,1)S(1)}, u32[]{:S(2)}, u32[]{:S(2)}) collective-permute-start(bf16[8,384,128]{2,1,0:T(8,128)(2,1)S(1)} %get-tuple-element.11), channel_id=1, source_target_pairs={{1,0},{2,1},{3,2},{4,3},{5,4},{6,5},{7,6},{8,7},{9,8},{10,9},{11,1... | collective-permute-start | bytes 2359304 | tf_op jit(solution)/shard_map/ppermute | solution.py:19
  80.7 16.3 %collective-permute-start = (bf16[8,384,128]{2,1,0:T(8,128)(2,1)S(1)}, bf16[8,384,128]{2,1,0:T(8,128)(2,1)}, u32[]{:S(2)}, u32[]{:S(2)}) collective-permute-start(bf16[8,384,128]{2,1,0:T(8,128)(2,1)S(1)} %get-tuple-element.12), channel_id=1, source_target_pairs={{0,1},{1,2},{2,3},{3,4},{4,5},{5,6},{6,7},{7,8},{8,9},{9,10},{10,1... | collective-permute-start | bytes 2359304 | tf_op jit(solution)/shard_map/ppermute | solution.py:19
  93.1 3.9 %copy-start.3 = (bf16[8,384,128]{2,1,0:T(8,128)(2,1)}, bf16[8,384,128]{2,1,0:T(8,128)(2,1)S(1)}, u32[]{:S(2)}) copy-start(bf16[8,384,128]{2,1,0:T(8,128)(2,1)S(1)} %collective-permute-done.1.kr_ref) | copy-start | bytes 2359300

commit v2 on v1

--- a/solution.py
+++ b/solution.py
@@ -11,6 +11,8 @@
 TILE = 384
 KEEP = 6
 USED = 8
+CHUNKS = 2
+LOG2_E = 1.4426950408889634
 
 
 def passed_along(block, axis, distance):
@@ -39,10 +41,10 @@
 
 
 def attend_kernel(which_ref, index_ref, count_ref, q_ref, kl_ref, kc_ref, kr_ref,
-                  vl_ref, vc_ref, vr_ref, o_ref, s_scr, m_scr, l_scr, acc_scr):
+                  vl_ref, vc_ref, vr_ref, o_ref, s_scr, mx_scr, lacc_scr, acc_scr):
     i = pl.program_id(0)
     n = count_ref[i]
-    score_scale = HEAD_DIM ** (-0.5)
+    score_scale = (HEAD_DIM ** (-0.5)) * LOG2_E
     q = q_ref[0]
 
     def pick(l_ref, c_ref, r_ref, j):
@@ -62,36 +64,36 @@
             s = lax.dot_general(q, k, (((1,), (1,)), ((), ())),
                                 preferred_element_type=jnp.float32) * score_scale
             s_scr[j] = s
-            mj = jnp.max(s, axis=1, keepdims=True)
             if j == 0:
-                m_scr[...] = mj
+                mx_scr[...] = s
             else:
-                m_scr[...] = jnp.maximum(m_scr[...], mj)
+                mx_scr[...] = jnp.maximum(mx_scr[...], s)
 
-    m = m_scr[...]
+    m = jnp.max(mx_scr[...], axis=1, keepdims=True)
     for j in range(KEEP):
         @pl.when(j < n)
         def _():
-            p = jnp.exp(s_scr[j] - m)
-            lsum = jnp.sum(p, axis=1, keepdims=True)
+            p = jnp.exp2(s_scr[j] - m)
             v = pick(vl_ref, vc_ref, vr_ref, j)
             pv = jnp.dot(p.astype(jnp.bfloat16), v, preferred_element_type=jnp.float32)
             if j == 0:
-                l_scr[...] = lsum
+                lacc_scr[...] = p
                 acc_scr[...] = pv
             else:
-                l_scr[...] = l_scr[...] + lsum
+                lacc_scr[...] = lacc_scr[...] + p
                 acc_scr[...] = acc_scr[...] + pv
 
-    o_ref[0] = (acc_scr[...] / l_scr[...]).astype(o_ref.dtype)
+    total = jnp.sum(lacc_scr[...], axis=1, keepdims=True)
+    o_ref[0] = (acc_scr[...] / total).astype(o_ref.dtype)
 
 
 def attend(which, index, count, q, kl, kc, kr, vl, vc, vr):
     n_q, tile, width = q.shape
     side = kl.shape[0]
     own = kc.shape[0]
-    whole_side = pl.BlockSpec((side, tile, width), lambda i, *_: (0, 0, 0))
-    whole_own = pl.BlockSpec((own, tile, width), lambda i, *_: (0, 0, 0))
+    key_tile = kc.shape[1]
+    whole_side = pl.BlockSpec((side, key_tile, width), lambda i, *_: (0, 0, 0))
+    whole_own = pl.BlockSpec((own, key_tile, width), lambda i, *_: (0, 0, 0))
     one = pl.BlockSpec((1, tile, width), lambda i, *_: (i, 0, 0))
     grid_spec = pltpu.PrefetchScalarGridSpec(
         num_scalar_prefetch=3,
@@ -99,16 +101,16 @@
         in_specs=[one, whole_side, whole_own, whole_side, whole_side, whole_own, whole_side],
         out_specs=one,
         scratch_shapes=[
-            pltpu.VMEM((KEEP, tile, tile), jnp.float32),
-            pltpu.VMEM((tile, 1), jnp.float32),
-            pltpu.VMEM((tile, 1), jnp.float32),
+            pltpu.VMEM((KEEP, tile, key_tile), jnp.float32),
+            pltpu.VMEM((tile, key_tile), jnp.float32),
+            pltpu.VMEM((tile, key_tile), jnp.float32),
             pltpu.VMEM((tile, width), jnp.float32),
         ],
     )
-    flops = n_q * KEEP * tile * tile * width * 4
+    flops = n_q * KEEP * tile * key_tile * width * 4
     cost = pl.CostEstimate(
         flops=flops,
-        transcendentals=n_q * KEEP * tile * tile,
+        transcendentals=n_q * KEEP * tile * key_tile,
         bytes_accessed=2 * (q.size * 2 + (kl.size + kc.size + kr.size) * 2),
     )
     return pl.pallas_call(
@@ -121,20 +123,20 @@
 
 
 def body(query_rows, key_rows, value_rows, kept_tiles):
-    query_local, key_local, value_local = (
-        lax.all_to_all(query_rows, "uly", split_axis=1, concat_axis=0, tiled=True),
+    key_local, value_local = (
         lax.all_to_all(key_rows, "uly", split_axis=1, concat_axis=0, tiled=True),
         lax.all_to_all(value_rows, "uly", split_axis=1, concat_axis=0, tiled=True),
     )
     n_uly = lax.axis_size("uly")
     n_blk = lax.axis_size("blk")
-    feat_width = query_local.shape[1]
+    feat_width = key_local.shape[1]
     slab_now = lax.axis_index("blk")
+    rows = query_rows.shape[0]
+    chunk = rows // CHUNKS
 
     from_left, from_right = run_starts(kept_tiles, n_blk, n_uly)
     key_tiles = key_local.reshape(n_uly, TILE, feat_width)
     value_tiles = value_local.reshape(n_uly, TILE, feat_width)
-    query_tiles = query_local.reshape(n_uly, TILE, feat_width)
 
     to_next = from_left[jnp.minimum(slab_now + 1, n_blk - 1)]
     to_prev = from_right[jnp.maximum(slab_now - 1, 0)]
@@ -165,12 +167,18 @@
     which = jnp.where(is_live, which, 1)
     count = jnp.sum(is_live.astype(jnp.int32), axis=1)
 
-    attended = attend(
-        which.reshape(-1), index.reshape(-1), count,
-        query_tiles, left_key, key_tiles, right_key, left_value, value_tiles, right_value,
-    )
-    attended = attended.reshape(n_uly * TILE, feat_width)
-    return lax.all_to_all(attended, "uly", split_axis=0, concat_axis=1, tiled=True)
+    pieces = []
+    for c in range(CHUNKS):
+        query_part = lax.all_to_all(
+            query_rows[c * chunk:(c + 1) * chunk], "uly", split_axis=1, concat_axis=0, tiled=True
+        ).reshape(n_uly, chunk, feat_width)
+        attended = attend(
+            which.reshape(-1), index.reshape(-1), count,
+            query_part, left_key, key_tiles, right_key, left_value, value_tiles, right_value,
+        )
+        attended = attended.reshape(n_uly * chunk, feat_width)
+        pieces.append(lax.all_to_all(attended, "uly", split_axis=0, concat_axis=1, tiled=True))
+    return jnp.concatenate(pieces, axis=0)
 
 
 def solution(mesh):

time: 194 us -> 227 us (1.17)
  Pallas kernels: 69.7 us -> 101 us
  blocking collectives: 22.9 us -> 0 us
  starting transfers between devices: 24.5 us -> 46 us
  waiting for transfers between devices: 50.2 us -> 53.8 us
    pallas_call x1 -> x2, Pallas kernels: 69.7 us -> 101 us  [attend(): pl.pallas_call(attend_kernel, grid_spec=grid_spec, out_shape=jax.ShapeDty...]
    all_to_all x1 -> x0, blocking collectives: 22.9 us -> none  [body(): lax.all_to_all(attended, 'uly', split_axis=0, concat_axis=1, tiled=True)]
    all_to_all x1 -> x4, starting transfers between devices: 4.4 us -> 25.7 us  [the longest x2 14.3 us: body(): lax.all_to_all(attended, 'uly', split_axis=0, concat_axis=1, tiled=True)]
    all_to_all x1 -> x4, waiting for transfers between devices: 3.14 us -> 11.5 us  [the longest x2 11.5 us: body(): lax.all_to_all(attended, 'uly', split_axis=0, concat_axis=1, tiled=True)]
    ppermute x4, waiting for transfers between devices: 7.99 us -> 1.88 us  [passed_along(): return lax.ppermute(block, axis, route)]
    unnamed x12 -> x14, local copies, waits for them, and re-layouts: 6.47 us -> 6.35 us
  transfers between devices with their start and end apart: 7 -> 10, of which waited for: 5 -> 4; matrix products, arithmetic and copies ran while one was open for 8% -> 7% of each run, Pallas kernels for 0% -> 45%
where the time goes in v2:
time: 227 us; the launch traced here: 225 us
  Pallas kernels  101 us (44%)
  waiting for transfers between devices  53.8 us (24%)
  starting transfers between devices  46 us (20%)
  local copies, waits for them, and re-layouts  16.4 us (7%)
  other arithmetic  4.07 us (2%)
  between operations  4.02 us (2%)
    pallas_call x2, Pallas kernels, attend(): pl.pallas_call(attend_kernel, grid_spec=grid_spec, out_shape=jax.ShapeDty...  101 us
    all_to_all x1, waiting for transfers between devices, body(): lax.all_to_all(key_rows, 'uly', split_axis=1, concat_axis=0, tiled=True)  21 us
    all_to_all x1, waiting for transfers between devices, body(): lax.all_to_all(value_rows, 'uly', split_axis=1, concat_axis=0, tiled=True)  19.4 us
    all_to_all x2, starting transfers between devices, body(): lax.all_to_all(attended, 'uly', split_axis=0, concat_axis=1, tiled=True)  14.3 us
    all_to_all x2, waiting for transfers between devices, body(): lax.all_to_all(attended, 'uly', split_axis=0, concat_axis=1, tiled=True)  11.5 us
    all_to_all x2, starting transfers between devices, body(): lax.all_to_all(query_rows[c * chunk:(c + 1) * chunk], 'uly', split_axis=1...  11.4 us
    ppermute x4, starting transfers between devices, passed_along(): return lax.ppermute(block, axis, route)  9.52 us
    all_to_all x1, starting transfers between devices, body(): lax.all_to_all(key_rows, 'uly', split_axis=1, concat_axis=0, tiled=True)  7.03 us
  transfers between devices with their start and end apart: 10, of which 4 were waited for; matrix products, arithmetic and copies ran while one was open for 7% of the time, Pallas kernels for 45%

profile of v2, /device:TPU:192, one launch (start us, length us, event | category | flops | bytes accessed | tf_op | source)
XLA Modules:
  0.0 225.0 jit_solution(8714128613591635583)
XLA Ops:
  0.0 1.9 copy.21
  1.9 1.6 copy.22
  3.5 7.0 %all-to-all-start.1 = ((bf16[384,16,128]{2,0,1:T(8,128)(2,1)}), bf16[384,16,128]{2,0,1:T(8,128)(2,1)S(1)}, u32[]{:S(2)}, u32[]{:S(2)}) async-start(bf16[384,16,128]{2,0,1:T(8,128)(2,1)} %copy.22), calls=%async_computation.1 | async-start | bytes 3145728 | tf_op jit(solution)/shard_map/all_to_all | solution.py:127
  10.5 1.9 copy.23
  12.4 1.7 copy.24
  14.1 21.0 %all-to-all-done.1 = bf16[384,16,128]{2,0,1:T(8,128)(2,1)S(1)} async-done(((bf16[384,16,128]{2,0,1:T(8,128)(2,1)}), bf16[384,16,128]{2,0,1:T(8,128)(2,1)S(1)}, u32[]{:S(2)}, u32[]{:S(2)}) %all-to-all-start.1) | async-done | bytes 1572896 | tf_op jit(solution)/shard_map/all_to_all | solution.py:127
  35.1 3.7 %all-to-all-start.2 = ((bf16[384,16,128]{2,0,1:T(8,128)(2,1)}), bf16[384,16,128]{2,0,1:T(8,128)(2,1)S(1)}, u32[]{:S(2)}, u32[]{:S(2)}) async-start(bf16[384,16,128]{2,0,1:T(8,128)(2,1)} %copy.24), calls=%async_computation.2 | async-start | bytes 3145728 | tf_op jit(solution)/shard_map/all_to_all | solution.py:128
  38.8 2.5 %slice_bitcast_fusion.1 = (bf16[24,16,8,128]{3,2,1,0:T(8,128)(2,1)S(1)}, bf16[24,16,8,128]{3,2,1,0:T(8,128)(2,1)}) fusion(bf16[384,2048]{1,0:T(8,128)(2,1)} %param.4), kind=kLoop, calls=%fused_computation.11 | loop fusion | bytes 3145728
  41.2 1.1 copy.37
  42.4 0.0 copy-done.4
  42.4 0.2 select_reduce_fusion.1
  42.6 19.4 %all-to-all-done.2 = bf16[384,16,128]{2,0,1:T(8,128)(2,1)S(1)} async-done(((bf16[384,16,128]{2,0,1:T(8,128)(2,1)}), bf16[384,16,128]{2,0,1:T(8,128)(2,1)S(1)}, u32[]{:S(2)}, u32[]{:S(2)}) %all-to-all-start.2) | async-done | bytes 1572896 | tf_op jit(solution)/shard_map/all_to_all | solution.py:128
  62.0 4.3 %all-to-all-start = ((bf16[192,16,128]{2,0,1:T(8,128)(2,1)}), bf16[192,16,128]{2,0,1:T(8,128)(2,1)}, u32[]{:S(2)}, u32[]{:S(2)}) async-start(bf16[192,16,128]{2,0,1:T(8,128)(2,1)} %bitcast.48), calls=%async_computation | async-start | bytes 1572864 | tf_op jit(solution)/shard_map/all_to_all | solution.py:172
  66.4 0.6 fusion.5
  68.2 0.7 fusion.6
  71.4 1.4 dynamic-slice_bitcast_fusion
  72.8 0.0 copy-done.1
  72.8 1.9 collective-permute-start.3
  74.7 0.0 copy-start.2
  74.7 2.5 %collective-permute-start.2 = (bf16[8,384,128]{2,1,0:T(8,128)(2,1)}, bf16[8,384,128]{2,1,0:T(8,128)(2,1)}, u32[]{:S(2)}, u32[]{:S(2)}) collective-permute-start(bf16[8,384,128]{2,1,0:T(8,128)(2,1)} %get-tuple-element.12), channel_id=1, source_target_pairs={{0,1},{1,2},{2,3},{3,4},{4,5},{5,6},{6,7},{7,8},{8,9},{9,10},{10,1... | collective-permute-start | bytes 2359304 | tf_op jit(solution)/shard_map/ppermute | solution.py:21
  77.3 0.0 copy-done
  77.3 1.1 dynamic-slice_bitcast_fusion.2
  78.4 3.1 %collective-permute-start.1 = (bf16[8,384,128]{2,1,0:T(8,128)(2,1)}, bf16[8,384,128]{2,1,0:T(8,128)(2,1)}, u32[]{:S(2)}, u32[]{:S(2)}) collective-permute-start(bf16[8,384,128]{2,1,0:T(8,128)(2,1)} %get-tuple-element.13), channel_id=1, source_target_pairs={{1,0},{2,1},{3,2},{4,3},{5,4},{6,5},{7,6},{8,7},{9,8},{10,9},{11,1... | collective-permute-start | bytes 2359304 | tf_op jit(solution)/shard_map/ppermute | solution.py:21
  81.5 1.9 collective-permute-start
  83.4 0.1 copy.19
  83.6 0.0 copy-done.2
  83.6 1.1 copy.36
  84.7 0.6 gather_fusion
  85.3 0.0 all-to-all-done
  85.3 7.1 %all-to-all-start.4 = ((bf16[192,16,128]{2,0,1:T(8,128)(2,1)}), bf16[192,16,128]{2,0,1:T(8,128)(2,1)S(1)}, u32[]{:S(2)}, u32[]{:S(2)}) async-start(bf16[192,16,128]{2,0,1:T(8,128)(2,1)} %bitcast.40), calls=%async_computation.4 | async-start | bytes 1572864 | tf_op jit(solution)/shard_map/all_to_all | solution.py:172
  92.4 0.7 convert_reduce_fusion
  93.1 0.1 select_n.122
  93.2 1.8 compare_select_fusion.9
  95.0 0.0 collective-permute-done.3.vr_ref
  95.0 0.0 collective-permute-done.2.vl_ref
  95.0 0.0 collective-permute-done.1.kr_ref
  95.0 1.9 collective-permute-done.kl_ref
  96.9 50.4 %shard_map.46 = bf16[16,192,128]{2,1,0:T(8,128)(2,1)} custom-call(s32[96]{0:T(128)} %get-tuple-element.22.which_ref, s32[96]{0:T(128)} %get-tuple-element.21.index_ref, s32[16]{0:T(128)} %get-tuple-element.7.count_ref, bf16[16,192,128]{2,1,0:T(8,128)(2,1)} %bitcast.3.q_ref, bf16[8,384,128]{2,1,0:T(8,128)(2,1)} %collective-permute-done.kl_ref, ...), custom_call_target="tpu_custom_call" | custom-call | flops 3623878656 | bytes 7864320 | tf_op jit(solution)/shard_map/pallas_call | solution.py:116
  147.3 0.0 all-to-all-done.4
  147.3 7.1 %all-to-all-start.3 = ((bf16[16,192,128]{2,1,0:T(8,128)(2,1)}), bf16[16,192,128]{2,1,0:T(8,128)(2,1)S(1)}, u32[]{:S(2)}, u32[]{:S(2)}) async-start(bf16[16,192,128]{2,1,0:T(8,128)(2,1)} %shard_map.46), calls=%async_computation.3 | async-start | bytes 1572864 | tf_op jit(solution)/shard_map/all_to_all | solution.py:180
  154.4 0.0 copy-done.3
  154.4 50.4 %shard_map.47 = bf16[16,192,128]{2,1,0:T(8,128)(2,1)} custom-call(s32[96]{0:T(128)} %get-tuple-element.22.which_ref, s32[96]{0:T(128)} %get-tuple-element.21.index_ref, s32[16]{0:T(128)} %get-tuple-element.7.count_ref, bf16[16,192,128]{2,1,0:T(8,128)(2,1)} %bitcast.49, bf16[8,384,128]{2,1,0:T(8,128)(2,1)} %collective-permute-done.kl_ref, ...), custom_call_target="tpu_custom_call" | custom-call | flops 3623878656 | bytes 7864320 | tf_op jit(solution)/shard_map/pallas_call | solution.py:116
  204.8 0.0 all-to-all-done.3
  204.8 7.2 %all-to-all-start.5 = ((bf16[16,192,128]{2,1,0:T(8,128)(2,1)}), bf16[16,192,128]{2,1,0:T(8,128)(2,1)S(1)}, u32[]{:S(2)}, u32[]{:S(2)}) async-start(bf16[16,192,128]{2,1,0:T(8,128)(2,1)} %shard_map.47), calls=%async_computation.5 | async-start | bytes 1572864 | tf_op jit(solution)/shard_map/all_to_all | solution.py:180
  212.0 0.1 copy_bitcast_fusion.1
  212.1 11.5 %all-to-all-done.5 = bf16[16,192,128]{2,1,0:T(8,128)(2,1)S(1)} async-done(((bf16[16,192,128]{2,1,0:T(8,128)(2,1)}), bf16[16,192,128]{2,1,0:T(8,128)(2,1)S(1)}, u32[]{:S(2)}, u32[]{:S(2)}) %all-to-all-start.5) | async-done | bytes 786464 | tf_op jit(solution)/shard_map/all_to_all | solution.py:180
  223.6 0.1 copy_bitcast_fusion
  223.7 1.2 pad_maximum_fusion
  (13 shorter events, 0.1 us)
Async XLA Ops:
  3.5 31.6 %all-to-all-start.1 = ((bf16[384,16,128]{2,0,1:T(8,128)(2,1)}), bf16[384,16,128]{2,0,1:T(8,128)(2,1)S(1)}, u32[]{:S(2)}, u32[]{:S(2)}) async-start(bf16[384,16,128]{2,0,1:T(8,128)(2,1)} %copy.22), calls=%async_computation.1 | async-start | bytes 3145728 | tf_op jit(solution)/shard_map/all_to_all | solution.py:127
  35.1 42.2 %copy-start = (bf16[384,16,128]{2,0,1:T(8,128)(2,1)}, bf16[384,16,128]{2,0,1:T(8,128)(2,1)S(1)}, u32[]{:S(2)}) copy-start(bf16[384,16,128]{2,0,1:T(8,128)(2,1)S(1)} %all-to-all-done.1) | copy-start | bytes 4718596
  35.1 27.0 %all-to-all-start.2 = ((bf16[384,16,128]{2,0,1:T(8,128)(2,1)}), bf16[384,16,128]{2,0,1:T(8,128)(2,1)S(1)}, u32[]{:S(2)}, u32[]{:S(2)}) async-start(bf16[384,16,128]{2,0,1:T(8,128)(2,1)} %copy.24), calls=%async_computation.2 | async-start | bytes 3145728 | tf_op jit(solution)/shard_map/all_to_all | solution.py:128
  41.2 1.1 copy-start.4
  62.0 10.8 %copy-start.1 = (bf16[384,16,128]{2,0,1:T(8,128)(2,1)}, bf16[384,16,128]{2,0,1:T(8,128)(2,1)S(1)}, u32[]{:S(2)}) copy-start(bf16[384,16,128]{2,0,1:T(8,128)(2,1)S(1)} %all-to-all-done.2) | copy-start | bytes 4718596
  62.0 23.3 %all-to-all-start = ((bf16[192,16,128]{2,0,1:T(8,128)(2,1)}), bf16[192,16,128]{2,0,1:T(8,128)(2,1)}, u32[]{:S(2)}, u32[]{:S(2)}) async-start(bf16[192,16,128]{2,0,1:T(8,128)(2,1)} %bitcast.48), calls=%async_computation | async-start | bytes 1572864 | tf_op jit(solution)/shard_map/all_to_all | solution.py:172
  72.8 22.2 %collective-permute-start.3 = (bf16[8,384,128]{2,1,0:T(8,128)(2,1)}, bf16[8,384,128]{2,1,0:T(8,128)(2,1)}, u32[]{:S(2)}, u32[]{:S(2)}) collective-permute-start(bf16[8,384,128]{2,1,0:T(8,128)(2,1)} %get-tuple-element.11), channel_id=1, source_target_pairs={{1,0},{2,1},{3,2},{4,3},{5,4},{6,5},{7,6},{8,7},{9,8},{10,9},{11,1... | collective-permute-start | bytes 2359304 | tf_op jit(solution)/shard_map/ppermute | solution.py:21
  74.7 8.9 %copy-start.2 = (bf16[24,16,8,128]{3,2,1,0:T(8,128)(2,1)S(1)}, bf16[24,16,8,128]{3,2,1,0:T(8,128)(2,1)}, u32[]{:S(2)}) copy-start(bf16[24,16,8,128]{3,2,1,0:T(8,128)(2,1)} %get-tuple-element.10) | copy-start | bytes 2359300
  74.7 20.3 %collective-permute-start.2 = (bf16[8,384,128]{2,1,0:T(8,128)(2,1)}, bf16[8,384,128]{2,1,0:T(8,128)(2,1)}, u32[]{:S(2)}, u32[]{:S(2)}) collective-permute-start(bf16[8,384,128]{2,1,0:T(8,128)(2,1)} %get-tuple-element.12), channel_id=1, source_target_pairs={{0,1},{1,2},{2,3},{3,4},{4,5},{5,6},{6,7},{7,8},{8,9},{9,10},{10,1... | collective-permute-start | bytes 2359304 | tf_op jit(solution)/shard_map/ppermute | solution.py:21
  78.4 16.7 %collective-permute-start.1 = (bf16[8,384,128]{2,1,0:T(8,128)(2,1)}, bf16[8,384,128]{2,1,0:T(8,128)(2,1)}, u32[]{:S(2)}, u32[]{:S(2)}) collective-permute-start(bf16[8,384,128]{2,1,0:T(8,128)(2,1)} %get-tuple-element.13), channel_id=1, source_target_pairs={{1,0},{2,1},{3,2},{4,3},{5,4},{6,5},{7,6},{8,7},{9,8},{10,9},{11,1... | collective-permute-start | bytes 2359304 | tf_op jit(solution)/shard_map/ppermute | solution.py:21
  81.5 15.4 %collective-permute-start = (bf16[8,384,128]{2,1,0:T(8,128)(2,1)S(1)}, bf16[8,384,128]{2,1,0:T(8,128)(2,1)}, u32[]{:S(2)}, u32[]{:S(2)}) collective-permute-start(bf16[8,384,128]{2,1,0:T(8,128)(2,1)S(1)} %get-tuple-element.14), channel_id=1, source_target_pairs={{0,1},{1,2},{2,3},{3,4},{4,5},{5,6},{6,7},{7,8},{8,9},{9,10},{10,1... | collective-permute-start | bytes 2359304 | tf_op jit(solution)/shard_map/ppermute | solution.py:21
  85.3 62.0 %all-to-all-start.4 = ((bf16[192,16,128]{2,0,1:T(8,128)(2,1)}), bf16[192,16,128]{2,0,1:T(8,128)(2,1)S(1)}, u32[]{:S(2)}, u32[]{:S(2)}) async-start(bf16[192,16,128]{2,0,1:T(8,128)(2,1)} %bitcast.40), calls=%async_computation.4 | async-start | bytes 1572864 | tf_op jit(solution)/shard_map/all_to_all | solution.py:172
  147.3 7.1 %copy-start.3 = (bf16[192,16,128]{2,0,1:T(8,128)(2,1)}, bf16[192,16,128]{2,0,1:T(8,128)(2,1)S(1)}, u32[]{:S(2)}) copy-start(bf16[192,16,128]{2,0,1:T(8,128)(2,1)S(1)} %all-to-all-done.4) | copy-start | bytes 2359300
  147.3 57.5 %all-to-all-start.3 = ((bf16[16,192,128]{2,1,0:T(8,128)(2,1)}), bf16[16,192,128]{2,1,0:T(8,128)(2,1)S(1)}, u32[]{:S(2)}, u32[]{:S(2)}) async-start(bf16[16,192,128]{2,1,0:T(8,128)(2,1)} %shard_map.46), calls=%async_computation.3 | async-start | bytes 1572864 | tf_op jit(solution)/shard_map/all_to_all | solution.py:180
  204.8 18.8 %all-to-all-start.5 = ((bf16[16,192,128]{2,1,0:T(8,128)(2,1)}), bf16[16,192,128]{2,1,0:T(8,128)(2,1)S(1)}, u32[]{:S(2)}, u32[]{:S(2)}) async-start(bf16[16,192,128]{2,1,0:T(8,128)(2,1)} %shard_map.47), calls=%async_computation.5 | async-start | bytes 1572864 | tf_op jit(solution)/shard_map/all_to_all | solution.py:180

commit v3 on v2

--- a/solution.py
+++ b/solution.py
@@ -11,7 +11,7 @@
 TILE = 384
 KEEP = 6
 USED = 8
-CHUNKS = 2
+CHUNKS = 1
 LOG2_E = 1.4426950408889634
 
 
@@ -41,7 +41,7 @@
 
 
 def attend_kernel(which_ref, index_ref, count_ref, q_ref, kl_ref, kc_ref, kr_ref,
-                  vl_ref, vc_ref, vr_ref, o_ref, s_scr, mx_scr, lacc_scr, acc_scr):
+                  vl_ref, vc_ref, vr_ref, o_ref):
     i = pl.program_id(0)
     n = count_ref[i]
     score_scale = (HEAD_DIM ** (-0.5)) * LOG2_E
@@ -57,59 +57,45 @@
         c = r_ref[jnp.clip(x, 0, side)]
         return jnp.where(w == 0, a, jnp.where(w == 1, b, c))
 
+    scores = []
+    top = None
     for j in range(KEEP):
-        @pl.when(j < n)
-        def _():
-            k = pick(kl_ref, kc_ref, kr_ref, j)
-            s = lax.dot_general(q, k, (((1,), (1,)), ((), ())),
-                                preferred_element_type=jnp.float32) * score_scale
-            s_scr[j] = s
-            if j == 0:
-                mx_scr[...] = s
-            else:
-                mx_scr[...] = jnp.maximum(mx_scr[...], s)
+        s = jnp.dot(q, pick(kl_ref, kc_ref, kr_ref, j),
+                    preferred_element_type=jnp.float32) * score_scale
+        if j > 0:
+            s = jnp.where(j < n, s, -jnp.inf)
+        scores.append(s)
+        top = s if top is None else jnp.maximum(top, s)
+    m = jnp.max(top, axis=1, keepdims=True)
 
-    m = jnp.max(mx_scr[...], axis=1, keepdims=True)
+    spread = None
+    acc = None
     for j in range(KEEP):
-        @pl.when(j < n)
-        def _():
-            p = jnp.exp2(s_scr[j] - m)
-            v = pick(vl_ref, vc_ref, vr_ref, j)
-            pv = jnp.dot(p.astype(jnp.bfloat16), v, preferred_element_type=jnp.float32)
-            if j == 0:
-                lacc_scr[...] = p
-                acc_scr[...] = pv
-            else:
-                lacc_scr[...] = lacc_scr[...] + p
-                acc_scr[...] = acc_scr[...] + pv
-
-    total = jnp.sum(lacc_scr[...], axis=1, keepdims=True)
-    o_ref[0] = (acc_scr[...] / total).astype(o_ref.dtype)
+        p = jnp.exp2(scores[j] - m)
+        pv = jnp.dot(p.astype(jnp.bfloat16), pick(vl_ref, vc_ref, vr_ref, j),
+                     preferred_element_type=jnp.float32)
+        spread = p if spread is None else spread + p
+        acc = pv if acc is None else acc + pv
+    total = jnp.sum(spread, axis=1, keepdims=True)
+    o_ref[0] = (acc / total).astype(o_ref.dtype)
 
 
 def attend(which, index, count, q, kl, kc, kr, vl, vc, vr):
     n_q, tile, width = q.shape
-    side = kl.shape[0]
-    own = kc.shape[0]
-    key_tile = kc.shape[1]
-    whole_side = pl.BlockSpec((side, key_tile, width), lambda i, *_: (0, 0, 0))
-    whole_own = pl.BlockSpec((own, key_tile, width), lambda i, *_: (0, 0, 0))
+    key_tile = vc.shape[1]
+
+    def whole(x):
+        return pl.BlockSpec(x.shape, lambda i, *_: (0, 0, 0))
+
     one = pl.BlockSpec((1, tile, width), lambda i, *_: (i, 0, 0))
     grid_spec = pltpu.PrefetchScalarGridSpec(
         num_scalar_prefetch=3,
         grid=(n_q,),
-        in_specs=[one, whole_side, whole_own, whole_side, whole_side, whole_own, whole_side],
+        in_specs=[one] + [whole(x) for x in (kl, kc, kr, vl, vc, vr)],
         out_specs=one,
-        scratch_shapes=[
-            pltpu.VMEM((KEEP, tile, key_tile), jnp.float32),
-            pltpu.VMEM((tile, key_tile), jnp.float32),
-            pltpu.VMEM((tile, key_tile), jnp.float32),
-            pltpu.VMEM((tile, width), jnp.float32),
-        ],
     )
-    flops = n_q * KEEP * tile * key_tile * width * 4
     cost = pl.CostEstimate(
-        flops=flops,
+        flops=n_q * KEEP * tile * key_tile * width * 4,
         transcendentals=n_q * KEEP * tile * key_tile,
         bytes_accessed=2 * (q.size * 2 + (kl.size + kc.size + kr.size) * 2),
     )
@@ -135,7 +121,7 @@
     chunk = rows // CHUNKS
 
     from_left, from_right = run_starts(kept_tiles, n_blk, n_uly)
-    key_tiles = key_local.reshape(n_uly, TILE, feat_width)
+    key_tiles = jnp.swapaxes(key_local.reshape(n_uly, TILE, feat_width), 1, 2)
     value_tiles = value_local.reshape(n_uly, TILE, feat_width)
 
     to_next = from_left[jnp.minimum(slab_now + 1, n_blk - 1)]

time: 227 us -> 163 us (0.72)
  Pallas kernels: 101 us -> 32.8 us
  blocking collectives: 0 us -> 29.1 us
  starting transfers between devices: 46 us -> 24.5 us
  waiting for transfers between devices: 53.8 us -> 50.1 us
    pallas_call x2 -> x1, Pallas kernels: 101 us -> 32.8 us  [attend(): pl.pallas_call(attend_kernel, grid_spec=grid_spec, out_shape=jax.ShapeDty...]
    all_to_all x0 -> x1, blocking collectives: none -> 29.1 us  [body(): lax.all_to_all(attended, 'uly', split_axis=0, concat_axis=1, tiled=True)]
    all_to_all x2 -> x0, starting transfers between devices: 14.3 us -> none  [body(): lax.all_to_all(attended, 'uly', split_axis=0, concat_axis=1, tiled=True)]
    all_to_all x2 -> x0, waiting for transfers between devices: 11.5 us -> none  [body(): lax.all_to_all(attended, 'uly', split_axis=0, concat_axis=1, tiled=True)]
    all_to_all x2 -> x1, starting transfers between devices: 11.4 us -> 4.4 us  [body(): lax.all_to_all(query_rows[c * chunk:(c + 1) * chunk], 'uly', split_axis=1...]
    ppermute x4, waiting for transfers between devices: 1.88 us -> 7.99 us  [passed_along(): return lax.ppermute(block, axis, route)]
    all_to_all x2 -> x1, waiting for transfers between devices: 0.01 us -> 3.06 us  [body(): lax.all_to_all(query_rows[c * chunk:(c + 1) * chunk], 'uly', split_axis=1...]
    unnamed x14 -> x12, local copies, waits for them, and re-layouts: 6.35 us -> 7.18 us
  transfers between devices with their start and end apart: 10 -> 7, of which waited for: 4 -> 5; matrix products, arithmetic and copies ran while one was open for 7% -> 9% of each run, Pallas kernels for 45% -> 0%
where the time goes in v3:
time: 163 us; the launch traced here: 161 us
  waiting for transfers between devices  50.1 us (31%)
  Pallas kernels  32.8 us (20%)
  blocking collectives  29.1 us (18%)
  starting transfers between devices  24.5 us (15%)
  local copies, waits for them, and re-layouts  17.4 us (11%)
  between operations  3.93 us (2%)
  other arithmetic  2.74 us (2%)
    pallas_call x1, Pallas kernels, attend(): pl.pallas_call(attend_kernel, grid_spec=grid_spec, out_shape=jax.ShapeDty...  32.8 us
    all_to_all x1, blocking collectives, body(): lax.all_to_all(attended, 'uly', split_axis=0, concat_axis=1, tiled=True)  29.1 us
    all_to_all x1, waiting for transfers between devices, body(): lax.all_to_all(key_rows, 'uly', split_axis=1, concat_axis=0, tiled=True)  21 us
    all_to_all x1, waiting for transfers between devices, body(): lax.all_to_all(value_rows, 'uly', split_axis=1, concat_axis=0, tiled=True)  18 us
    ppermute x4, starting transfers between devices, passed_along(): return lax.ppermute(block, axis, route)  9.39 us
    ppermute x4, waiting for transfers between devices, passed_along(): return lax.ppermute(block, axis, route)  7.99 us
    unnamed x12, local copies, waits for them, and re-layouts  7.18 us
    all_to_all x1, starting transfers between devices, body(): lax.all_to_all(key_rows, 'uly', split_axis=1, concat_axis=0, tiled=True)  7.03 us
  transfers between devices with their start and end apart: 7, of which 5 were waited for; matrix products, arithmetic and copies ran while one was open for 9% of the time, Pallas kernels for 0%

profile of v3, /device:TPU:192, one launch (start us, length us, event | category | flops | bytes accessed | tf_op | source)
XLA Modules:
  0.0 160.6 jit_solution(9320445256840533620)
XLA Ops:
  0.0 2.6 %copy.22 = bf16[384,2048]{0,1:T(8,128)(2,1)} copy(bf16[384,2048]{1,0:T(8,128)(2,1)} %param.5) | data formatting | bytes 3145728 | tf_op args[1]
  2.6 7.0 %all-to-all-start.1 = ((bf16[384,16,128]{0,2,1:T(8,128)(2,1)}), bf16[384,16,128]{0,2,1:T(8,128)(2,1)S(1)}, u32[]{:S(2)}, u32[]{:S(2)}) async-start(bf16[384,16,128]{0,2,1:T(8,128)(2,1)} %bitcast.5), calls=%async_computation.1 | async-start | bytes 3145728 | tf_op jit(solution)/shard_map/all_to_all | solution.py:113
  9.6 1.9 %copy.23 = bf16[384,2048]{0,1:T(8,128)(2,1)S(1)} copy(bf16[384,2048]{1,0:T(8,128)(2,1)} %param.6) | data formatting | bytes 3145728 | tf_op args[2]
  11.5 1.6 %copy.24 = bf16[384,16,128]{2,0,1:T(8,128)(2,1)} copy(bf16[384,16,128]{0,2,1:T(8,128)(2,1)S(1)} %bitcast.26) | data formatting | bytes 3145728 | tf_op jit(solution)/shard_map/all_to_all | solution.py:114
  13.1 21.0 %all-to-all-done.1 = bf16[384,16,128]{0,2,1:T(8,128)(2,1)S(1)} async-done(((bf16[384,16,128]{0,2,1:T(8,128)(2,1)}), bf16[384,16,128]{0,2,1:T(8,128)(2,1)S(1)}, u32[]{:S(2)}, u32[]{:S(2)}) %all-to-all-start.1) | async-done | bytes 1572896 | tf_op jit(solution)/shard_map/all_to_all | solution.py:113
  34.1 0.0 copy-start
  34.1 3.7 %all-to-all-start.2 = ((bf16[384,16,128]{2,0,1:T(8,128)(2,1)}), bf16[384,16,128]{2,0,1:T(8,128)(2,1)S(1)}, u32[]{:S(2)}, u32[]{:S(2)}) async-start(bf16[384,16,128]{2,0,1:T(8,128)(2,1)} %copy.24), calls=%async_computation.2 | async-start | bytes 3145728 | tf_op jit(solution)/shard_map/all_to_all | solution.py:114
  37.9 2.6 %copy.20 = bf16[384,2048]{0,1:T(8,128)(2,1)} copy(bf16[384,2048]{1,0:T(8,128)(2,1)} %param.4) | data formatting | bytes 3145728 | tf_op args[0]
  40.4 0.0 copy-start.2
  40.4 2.6 %copy.21 = bf16[384,16,128]{2,0,1:T(8,128)(2,1)} copy(bf16[384,16,128]{0,2,1:T(8,128)(2,1)} %bitcast.27) | data formatting | bytes 3145728 | tf_op jit(solution)/shard_map/all_to_all | solution.py:158
  43.1 0.0 copy-done.2
  43.1 18.0 %all-to-all-done.2 = bf16[384,16,128]{2,0,1:T(8,128)(2,1)S(1)} async-done(((bf16[384,16,128]{2,0,1:T(8,128)(2,1)}), bf16[384,16,128]{2,0,1:T(8,128)(2,1)S(1)}, u32[]{:S(2)}, u32[]{:S(2)}) %all-to-all-start.2) | async-done | bytes 1572896 | tf_op jit(solution)/shard_map/all_to_all | solution.py:114
  61.1 0.0 copy-start.1
  61.1 4.4 %all-to-all-start = ((bf16[384,16,128]{2,0,1:T(8,128)(2,1)}), bf16[384,16,128]{2,0,1:T(8,128)(2,1)}, u32[]{:S(2)}, u32[]{:S(2)}) async-start(bf16[384,16,128]{2,0,1:T(8,128)(2,1)} %copy.21), calls=%async_computation | async-start | bytes 3145728 | tf_op jit(solution)/shard_map/all_to_all | solution.py:158
  65.5 0.2 select_reduce_fusion.1
  65.8 0.7 fusion.5
  67.7 0.6 fusion.6
  70.8 0.0 copy-done.1
  70.8 1.4 dynamic-slice_bitcast_fusion
  72.2 1.9 %collective-permute-start.3 = (bf16[8,384,128]{2,1,0:T(8,128)(2,1)}, bf16[8,384,128]{2,1,0:T(8,128)(2,1)}, u32[]{:S(2)}, u32[]{:S(2)}) collective-permute-start(bf16[8,384,128]{2,1,0:T(8,128)(2,1)} %get-tuple-element.9), channel_id=1, source_target_pairs={{1,0},{2,1},{3,2},{4,3},{5,4},{6,5},{7,6},{8,7},{9,8},{10,9},{11,1... | collective-permute-start | bytes 2359304 | tf_op jit(solution)/shard_map/ppermute | solution.py:21
  74.1 2.4 %collective-permute-start.2 = (bf16[8,384,128]{2,1,0:T(8,128)(2,1)}, bf16[8,384,128]{2,1,0:T(8,128)(2,1)}, u32[]{:S(2)}, u32[]{:S(2)}) collective-permute-start(bf16[8,384,128]{2,1,0:T(8,128)(2,1)} %get-tuple-element.10), channel_id=1, source_target_pairs={{0,1},{1,2},{2,3},{3,4},{4,5},{5,6},{6,7},{7,8},{8,9},{9,10},{10,1... | collective-permute-start | bytes 2359304 | tf_op jit(solution)/shard_map/ppermute | solution.py:21
  76.5 0.0 copy-done
  76.5 0.2 dynamic-slice_bitcast_fusion.2
  76.7 3.2 %collective-permute-start.1 = (bf16[8,128,384]{2,1,0:T(8,128)(2,1)S(1)}, bf16[8,128,384]{2,1,0:T(8,128)(2,1)S(1)}, u32[]{:S(2)}, u32[]{:S(2)}) collective-permute-start(bf16[8,128,384]{2,1,0:T(8,128)(2,1)S(1)} %get-tuple-element.11), channel_id=1, source_target_pairs={{1,0},{2,1},{3,2},{4,3},{5,4},{6,5},{7,6},{8,7},{9,8},{10,9},{11,1... | collective-permute-start | bytes 2359304 | tf_op jit(solution)/shard_map/ppermute | solution.py:21
  79.9 1.9 %collective-permute-start = (bf16[8,128,384]{2,1,0:T(8,128)(2,1)S(1)}, bf16[8,128,384]{2,1,0:T(8,128)(2,1)}, u32[]{:S(2)}, u32[]{:S(2)}) collective-permute-start(bf16[8,128,384]{2,1,0:T(8,128)(2,1)S(1)} %get-tuple-element.12), channel_id=1, source_target_pairs={{0,1},{1,2},{2,3},{3,4},{4,5},{5,6},{6,7},{7,8},{8,9},{9,10},{10,1... | collective-permute-start | bytes 2359304 | tf_op jit(solution)/shard_map/ppermute | solution.py:21
  81.8 0.1 copy.19
  82.0 0.6 gather_fusion
  82.6 0.7 convert_reduce_fusion
  83.2 0.1 select_n.122
  83.3 1.8 %compare_select_fusion.9 = (s32[96]{0:T(128)}, s32[96]{0:T(128)}) fusion(s32[96]{0:T(128)S(1)} %select_n.122, s32[]{:T(128)} %bitcast.2, s32[]{:T(128)} %bitcast.1, s32[]{:T(128)S(6)} %axis_index.12), kind=kLoop, calls=%fused_computation.33 | loop fusion | flops 2976 | bytes 1164 | tf_op jit(solution)/shard_map/jit(_where)/select_n | solution.py:152
  85.1 3.1 %all-to-all-done = bf16[384,16,128]{2,0,1:T(8,128)(2,1)} async-done(((bf16[384,16,128]{2,0,1:T(8,128)(2,1)}), bf16[384,16,128]{2,0,1:T(8,128)(2,1)}, u32[]{:S(2)}, u32[]{:S(2)}) %all-to-all-start) | async-done | bytes 1572896 | tf_op jit(solution)/shard_map/all_to_all | solution.py:158
  88.2 0.0 collective-permute-done.3.vr_ref
  88.2 0.0 collective-permute-done.2.vl_ref
  88.2 4.1 %collective-permute-done.1.kr_ref = bf16[8,128,384]{2,1,0:T(8,128)(2,1)S(1)} collective-permute-done((bf16[8,128,384]{2,1,0:T(8,128)(2,1)S(1)}, bf16[8,128,384]{2,1,0:T(8,128)(2,1)S(1)}, u32[]{:S(2)}, u32[]{:S(2)}) %collective-permute-start.1) | collective-permute-done | bytes 786464 | tf_op jit(solution)/shard_map/ppermute | solution.py:21
  92.2 0.0 copy-start.3
  92.2 3.9 %collective-permute-done.kl_ref = bf16[8,128,384]{2,1,0:T(8,128)(2,1)} collective-permute-done((bf16[8,128,384]{2,1,0:T(8,128)(2,1)S(1)}, bf16[8,128,384]{2,1,0:T(8,128)(2,1)}, u32[]{:S(2)}, u32[]{:S(2)}) %collective-permute-start) | collective-permute-done | bytes 786464 | tf_op jit(solution)/shard_map/ppermute | solution.py:21
  96.2 0.0 copy-done.3
  96.2 32.8 %shard_map.46 = bf16[16,384,128]{2,1,0:T(8,128)(2,1)} custom-call(s32[96]{0:T(128)} %get-tuple-element.20.which_ref, s32[96]{0:T(128)} %get-tuple-element.19.index_ref, s32[16]{0:T(128)} %get-tuple-element.7.count_ref, bf16[16,384,128]{2,1,0:T(8,128)(2,1)} %bitcast.4.q_ref, bf16[8,128,384]{2,1,0:T(8,128)(2,1)} %collective-permute-done.kl_ref, ...), custom_call_target="tpu_custom_call" | custom-call | flops 7247757312 | bytes 9437184 | tf_op jit(solution)/shard_map/pallas_call | solution.py:102
  129.0 29.1 %all_to_all.61 = bf16[16,384,128]{2,1,0:T(8,128)(2,1)S(1)} all-to-all(bf16[16,384,128]{2,1,0:T(8,128)(2,1)} %shard_map.46), channel_id=1, replica_groups=mesh['uly'=16,'blk'=16] {'uly'}, dimensions={0} | all-to-all | bytes 3145728 | tf_op jit(solution)/shard_map/all_to_all | solution.py:166
  158.1 0.9 copy.25
  159.0 1.6 %copy.26 = bf16[384,2048]{1,0:T(8,128)(2,1)} copy(bf16[384,2048]{0,1:T(8,128)(2,1)S(1)} %bitcast.25) | data formatting | bytes 3145728 | tf_op jit(solution)/shard_map/all_to_all | solution.py:166
  (9 shorter events, 0.1 us)
Async XLA Ops:
  2.6 31.6 %all-to-all-start.1 = ((bf16[384,16,128]{0,2,1:T(8,128)(2,1)}), bf16[384,16,128]{0,2,1:T(8,128)(2,1)S(1)}, u32[]{:S(2)}, u32[]{:S(2)}) async-start(bf16[384,16,128]{0,2,1:T(8,128)(2,1)} %bitcast.5), calls=%async_computation.1 | async-start | bytes 3145728 | tf_op jit(solution)/shard_map/all_to_all | solution.py:113
  34.1 42.4 %copy-start = (bf16[384,16,128]{0,2,1:T(8,128)(2,1)}, bf16[384,16,128]{0,2,1:T(8,128)(2,1)S(1)}, u32[]{:S(2)}) copy-start(bf16[384,16,128]{0,2,1:T(8,128)(2,1)S(1)} %all-to-all-done.1) | copy-start | bytes 4718596
  34.1 27.0 %all-to-all-start.2 = ((bf16[384,16,128]{2,0,1:T(8,128)(2,1)}), bf16[384,16,128]{2,0,1:T(8,128)(2,1)S(1)}, u32[]{:S(2)}, u32[]{:S(2)}) async-start(bf16[384,16,128]{2,0,1:T(8,128)(2,1)} %copy.24), calls=%async_computation.2 | async-start | bytes 3145728 | tf_op jit(solution)/shard_map/all_to_all | solution.py:114
  40.4 2.6 %copy-start.2 = (s32[256,6]{0,1:T(8,128)S(1)}, s32[256,6]{0,1:T(8,128)}, u32[]{:S(2)}) copy-start(s32[256,6]{0,1:T(8,128)} %param.7) | copy-start | bytes 18436
  61.1 9.7 %copy-start.1 = (bf16[384,16,128]{2,0,1:T(8,128)(2,1)}, bf16[384,16,128]{2,0,1:T(8,128)(2,1)S(1)}, u32[]{:S(2)}) copy-start(bf16[384,16,128]{2,0,1:T(8,128)(2,1)S(1)} %all-to-all-done.2) | copy-start | bytes 4718596
  61.1 27.0 %all-to-all-start = ((bf16[384,16,128]{2,0,1:T(8,128)(2,1)}), bf16[384,16,128]{2,0,1:T(8,128)(2,1)}, u32[]{:S(2)}, u32[]{:S(2)}) async-start(bf16[384,16,128]{2,0,1:T(8,128)(2,1)} %copy.21), calls=%async_computation | async-start | bytes 3145728 | tf_op jit(solution)/shard_map/all_to_all | solution.py:158
  72.2 16.0 %collective-permute-start.3 = (bf16[8,384,128]{2,1,0:T(8,128)(2,1)}, bf16[8,384,128]{2,1,0:T(8,128)(2,1)}, u32[]{:S(2)}, u32[]{:S(2)}) collective-permute-start(bf16[8,384,128]{2,1,0:T(8,128)(2,1)} %get-tuple-element.9), channel_id=1, source_target_pairs={{1,0},{2,1},{3,2},{4,3},{5,4},{6,5},{7,6},{8,7},{9,8},{10,9},{11,1... | collective-permute-start | bytes 2359304 | tf_op jit(solution)/shard_map/ppermute | solution.py:21
  74.1 14.1 %collective-permute-start.2 = (bf16[8,384,128]{2,1,0:T(8,128)(2,1)}, bf16[8,384,128]{2,1,0:T(8,128)(2,1)}, u32[]{:S(2)}, u32[]{:S(2)}) collective-permute-start(bf16[8,384,128]{2,1,0:T(8,128)(2,1)} %get-tuple-element.10), channel_id=1, source_target_pairs={{0,1},{1,2},{2,3},{3,4},{4,5},{5,6},{6,7},{7,8},{8,9},{9,10},{10,1... | collective-permute-start | bytes 2359304 | tf_op jit(solution)/shard_map/ppermute | solution.py:21
  76.7 15.5 %collective-permute-start.1 = (bf16[8,128,384]{2,1,0:T(8,128)(2,1)S(1)}, bf16[8,128,384]{2,1,0:T(8,128)(2,1)S(1)}, u32[]{:S(2)}, u32[]{:S(2)}) collective-permute-start(bf16[8,128,384]{2,1,0:T(8,128)(2,1)S(1)} %get-tuple-element.11), channel_id=1, source_target_pairs={{1,0},{2,1},{3,2},{4,3},{5,4},{6,5},{7,6},{8,7},{9,8},{10,9},{11,1... | collective-permute-start | bytes 2359304 | tf_op jit(solution)/shard_map/ppermute | solution.py:21
  79.9 16.3 %collective-permute-start = (bf16[8,128,384]{2,1,0:T(8,128)(2,1)S(1)}, bf16[8,128,384]{2,1,0:T(8,128)(2,1)}, u32[]{:S(2)}, u32[]{:S(2)}) collective-permute-start(bf16[8,128,384]{2,1,0:T(8,128)(2,1)S(1)} %get-tuple-element.12), channel_id=1, source_target_pairs={{0,1},{1,2},{2,3},{3,4},{4,5},{5,6},{6,7},{7,8},{8,9},{9,10},{10,1... | collective-permute-start | bytes 2359304 | tf_op jit(solution)/shard_map/ppermute | solution.py:21
  92.2 3.9 %copy-start.3 = (bf16[8,128,384]{2,1,0:T(8,128)(2,1)}, bf16[8,128,384]{2,1,0:T(8,128)(2,1)S(1)}, u32[]{:S(2)}) copy-start(bf16[8,128,384]{2,1,0:T(8,128)(2,1)S(1)} %collective-permute-done.1.kr_ref) | copy-start | bytes 2359300

commit v4 on v3

--- a/solution.py
+++ b/solution.py
@@ -109,15 +109,20 @@
 
 
 def body(query_rows, key_rows, value_rows, kept_tiles):
-    key_local, value_local = (
-        lax.all_to_all(key_rows, "uly", split_axis=1, concat_axis=0, tiled=True),
-        lax.all_to_all(value_rows, "uly", split_axis=1, concat_axis=0, tiled=True),
-    )
     n_uly = lax.axis_size("uly")
     n_blk = lax.axis_size("blk")
-    feat_width = key_local.shape[1]
+    rows, width = query_rows.shape
+    feat_width = width // n_uly
+    stacked = jnp.stack(
+        [x.reshape(rows, n_uly, feat_width) for x in (query_rows, key_rows, value_rows)]
+    )
+    stacked = lax.all_to_all(stacked, "uly", split_axis=2, concat_axis=1, tiled=True)
+    query_local, key_local, value_local = (
+        stacked[0].reshape(n_uly * rows, feat_width),
+        stacked[1].reshape(n_uly * rows, feat_width),
+        stacked[2].reshape(n_uly * rows, feat_width),
+    )
     slab_now = lax.axis_index("blk")
-    rows = query_rows.shape[0]
     chunk = rows // CHUNKS
 
     from_left, from_right = run_starts(kept_tiles, n_blk, n_uly)
@@ -153,11 +158,10 @@
     which = jnp.where(is_live, which, 1)
     count = jnp.sum(is_live.astype(jnp.int32), axis=1)
 
+    query_tiles = query_local.reshape(n_uly, rows, feat_width)
     pieces = []
     for c in range(CHUNKS):
-        query_part = lax.all_to_all(
-            query_rows[c * chunk:(c + 1) * chunk], "uly", split_axis=1, concat_axis=0, tiled=True
-        ).reshape(n_uly, chunk, feat_width)
+        query_part = query_tiles[:, c * chunk:(c + 1) * chunk]
         attended = attend(
             which.reshape(-1), index.reshape(-1), count,
             query_part, left_key, key_tiles, right_key, left_value, value_tiles, right_value,

time: 163 us -> 194 us (1.19)
  waiting for transfers between devices: 50.1 us -> 72.8 us
  local copies, waits for them, and re-layouts: 17.4 us -> 28.3 us
  starting transfers between devices: 24.5 us -> 18.3 us
  other arithmetic: 2.74 us -> 6.44 us
    all_to_all x3 -> x1, waiting for transfers between devices: 42.1 us -> 65.2 us  [body(): lax.all_to_all(stacked, 'uly', split_axis=2, concat_axis=1, tiled=True)]
    another operation x0 -> x5, local copies, waits for them, and re-layouts: none -> 12 us  [the longest x1 6.63 us: body(): jnp.stack([x.reshape(rows, n_uly, feat_width) for x in (query_rows, key_r...]
    all_to_all x3 -> x1, starting transfers between devices: 15.1 us -> 7.21 us  [body(): lax.all_to_all(stacked, 'uly', split_axis=2, concat_axis=1, tiled=True)]
    another operation x0 -> x1, other arithmetic: none -> 3.59 us  [body(): jnp.stack([x.reshape(rows, n_uly, feat_width) for x in (query_rows, key_r...]
    all_to_all x2 -> x1, local copies, waits for them, and re-layouts: 4.22 us -> 2.64 us  [body(): lax.all_to_all(stacked, 'uly', split_axis=2, concat_axis=1, tiled=True)]
    unnamed x12 -> x8, local copies, waits for them, and re-layouts: 7.18 us -> 6.47 us
  transfers between devices with their start and end apart: 7 -> 5, of which waited for: 5 -> 3; matrix products, arithmetic and copies ran while one was open for 9% -> 3% of each run, Pallas kernels for 0% -> 0%
where the time goes in v4:
time: 194 us; the launch traced here: 193 us
  waiting for transfers between devices  72.8 us (38%)
  Pallas kernels  32.8 us (17%)
  blocking collectives  29.9 us (15%)
  local copies, waits for them, and re-layouts  28.3 us (15%)
  starting transfers between devices  18.3 us (9%)
  other arithmetic  6.44 us (3%)
  between operations  4.17 us (2%)
    all_to_all x1, waiting for transfers between devices, body(): lax.all_to_all(stacked, 'uly', split_axis=2, concat_axis=1, tiled=True)  65.2 us
    pallas_call x1, Pallas kernels, attend(): pl.pallas_call(attend_kernel, grid_spec=grid_spec, out_shape=jax.ShapeDty...  32.8 us
    all_to_all x1, blocking collectives, body(): lax.all_to_all(attended, 'uly', split_axis=0, concat_axis=1, tiled=True)  29.9 us
    ppermute x4, starting transfers between devices, passed_along(): return lax.ppermute(block, axis, route)  11.1 us
    ppermute x4, waiting for transfers between devices, passed_along(): return lax.ppermute(block, axis, route)  7.58 us
    all_to_all x1, starting transfers between devices, body(): lax.all_to_all(stacked, 'uly', split_axis=2, concat_axis=1, tiled=True)  7.21 us
    another operation x1, local copies, waits for them, and re-layouts, body(): jnp.stack([x.reshape(rows, n_uly, feat_width) for x in (query_rows, key_r...  6.63 us
    unnamed x8, local copies, waits for them, and re-layouts  6.47 us
  transfers between devices with their start and end apart: 5, of which 3 were waited for; matrix products, arithmetic and copies ran while one was open for 3% of the time, Pallas kernels for 0%

profile of v4, /device:TPU:192, one launch (start us, length us, event | category | flops | bytes accessed | tf_op | source)
XLA Modules:
  0.0 192.8 jit_solution(10422694938466761391)
XLA Ops:
  0.0 1.9 copy.37
  1.9 1.9 copy.38
  3.8 2.6 %copy.39 = bf16[384,2048]{0,1:T(8,128)(2,1)} copy(bf16[384,2048]{1,0:T(8,128)(2,1)} %param.6) | data formatting | bytes 3145728 | tf_op args[2]
  6.3 3.6 %pad_maximum_fusion = bf16[3,384,16,128]{1,3,2,0:T(8,128)(2,1)} fusion(bf16[1,384,16,128]{1,3,2,0:T(8,128)(2,1)} %bitcast.37, bf16[1,384,16,128]{1,3,2,0:T(8,128)(2,1)S(1)} %bitcast.36, bf16[1,384,16,128]{1,3,2,0:T(8,128)(2,1)S(1)} %bitcast.35), kind=kLoop, calls=%fused_computation.1 | loop fusion | flops 4718592 | bytes 9437184 | tf_op jit(solution)/shard_map/stack | solution.py:116
  9.9 6.6 %copy.40 = bf16[3,384,16,128]{3,1,0,2:T(8,128)(2,1)} copy(bf16[3,384,16,128]{1,3,2,0:T(8,128)(2,1)} %pad_maximum_fusion) | data formatting | bytes 9437184 | tf_op jit(solution)/shard_map/stack | solution.py:116
  16.6 0.0 copy-start.1
  16.6 7.2 %all-to-all-start = ((bf16[3,384,16,128]{3,1,0,2:T(8,128)(2,1)}), bf16[3,384,16,128]{3,1,0,2:T(8,128)(2,1)}, u32[]{:S(2)}, u32[]{:S(2)}) async-start(bf16[3,384,16,128]{3,1,0,2:T(8,128)(2,1)} %copy.40), calls=%async_computation | async-start | bytes 9437184 | tf_op jit(solution)/shard_map/all_to_all | solution.py:119
  23.8 0.0 copy-done.1
  23.9 0.2 select_reduce_fusion.1
  24.1 0.6 fusion.5
  26.0 0.7 fusion.6
  29.4 65.2 %all-to-all-done = bf16[3,384,16,128]{3,1,0,2:T(8,128)(2,1)} async-done(((bf16[3,384,16,128]{3,1,0,2:T(8,128)(2,1)}), bf16[3,384,16,128]{3,1,0,2:T(8,128)(2,1)}, u32[]{:S(2)}, u32[]{:S(2)}) %all-to-all-start) | async-done | bytes 4718624 | tf_op jit(solution)/shard_map/all_to_all | solution.py:119
  94.6 2.6 %copy.48 = bf16[3,384,16,128]{3,1,2,0:T(8,128)(2,1)S(1)} copy(bf16[3,384,16,128]{3,1,0,2:T(8,128)(2,1)} %all-to-all-done) | data formatting | bytes 9437184 | tf_op jit(solution)/shard_map/all_to_all | solution.py:119
  97.2 2.8 %slice_bitcast_fusion.1 = (bf16[16,384,128]{2,1,0:T(8,128)(2,1)}, bf16[16,128,384]{1,2,0:T(8,128)(2,1)S(1)}, bf16[1,16,384,1,128]{4,2,1,3,0:T(8,128)(2,1)S(1)}, ...) fusion(bf16[3,16,384,1,128]{4,2,1,3,0:T(8,128)(2,1)S(1)} %bitcast.34), kind=kLoop, calls=%fused_computation.43 | loop fusion | bytes 12582912 | tf_op jit(solution)/shard_map/reshape;reshape;squeeze | solution.py:130
  100.0 1.3 dynamic-slice_bitcast_fusion
  101.3 0.1 dynamic-slice_bitcast_fusion.2
  101.4 1.2 copy.43
  102.6 0.0 copy-start
  102.6 1.3 copy.42
  103.8 1.9 collective-permute-start
  105.8 3.6 %collective-permute-start.3 = (bf16[8,384,128]{2,1,0:T(8,128)(2,1)}, bf16[8,384,128]{2,1,0:T(8,128)(2,1)}, u32[]{:S(2)}, u32[]{:S(2)}) collective-permute-start(bf16[8,384,128]{2,1,0:T(8,128)(2,1)} %get-tuple-element.14), channel_id=1, source_target_pairs={{1,0},{2,1},{3,2},{4,3},{5,4},{6,5},{7,6},{8,7},{9,8},{10,9},{11,1... | collective-permute-start | bytes 2359304 | tf_op jit(solution)/shard_map/ppermute | solution.py:21
  109.4 1.9 collective-permute-start.2
  111.3 0.0 copy-done
  111.3 3.6 %collective-permute-start.1 = (bf16[8,128,384]{2,1,0:T(8,128)(2,1)S(1)}, bf16[8,128,384]{2,1,0:T(8,128)(2,1)}, u32[]{:S(2)}, u32[]{:S(2)}) collective-permute-start(bf16[8,128,384]{2,1,0:T(8,128)(2,1)S(1)} %bitcast.40), channel_id=1, source_target_pairs={{1,0},{2,1},{3,2},{4,3},{5,4},{6,5},{7,6},{8,7},{9,8},{10,9},{11,1... | collective-permute-start | bytes 2359304 | tf_op jit(solution)/shard_map/ppermute | solution.py:21
  115.0 0.1 copy.36
  115.2 0.6 gather_fusion
  115.7 0.8 convert_reduce_fusion
  116.5 0.1 select_n.122
  116.6 1.8 compare_select_fusion.9
  118.4 1.6 copy.44.kc_ref
  119.9 0.0 collective-permute-done.kl_ref
  119.9 0.0 collective-permute-done.3.vr_ref
  119.9 5.9 %collective-permute-done.2.vl_ref = bf16[8,384,128]{2,1,0:T(8,128)(2,1)} collective-permute-done((bf16[8,384,128]{2,1,0:T(8,128)(2,1)}, bf16[8,384,128]{2,1,0:T(8,128)(2,1)}, u32[]{:S(2)}, u32[]{:S(2)}) %collective-permute-start.2) | collective-permute-done | bytes 786464 | tf_op jit(solution)/shard_map/ppermute | solution.py:21
  125.9 1.7 collective-permute-done.1.kr_ref
  127.5 32.8 %shard_map.46 = bf16[16,384,128]{2,1,0:T(8,128)(2,1)} custom-call(s32[96]{0:T(128)} %get-tuple-element.25.which_ref, s32[96]{0:T(128)} %get-tuple-element.24.index_ref, s32[16]{0:T(128)} %get-tuple-element.7.count_ref, bf16[16,384,128]{2,1,0:T(8,128)(2,1)} %get-tuple-element.13.q_ref, bf16[8,128,384]{2,1,0:T(8,128)(2,1)} %collective-permute-done.kl_ref, ...), custom_call_target="tpu_custom_call" | custom-call | flops 7247757312 | bytes 9437184 | tf_op jit(solution)/shard_map/pallas_call | solution.py:102
  160.4 29.9 %all_to_all.31 = bf16[16,384,128]{2,1,0:T(8,128)(2,1)S(1)} all-to-all(bf16[16,384,128]{2,1,0:T(8,128)(2,1)} %shard_map.46), channel_id=1, replica_groups=mesh['uly'=16,'blk'=16] {'uly'}, dimensions={0} | all-to-all | bytes 3145728 | tf_op jit(solution)/shard_map/all_to_all | solution.py:170
  190.3 0.9 copy.45
  191.1 1.6 copy.46
  (9 shorter events, 0.1 us)
Async XLA Ops:
  16.6 7.3 %copy-start.1 = (s32[256,6]{0,1:T(8,128)S(1)}, s32[256,6]{0,1:T(8,128)}, u32[]{:S(2)}) copy-start(s32[256,6]{0,1:T(8,128)} %param.7) | copy-start | bytes 18436
  16.6 78.0 %all-to-all-start = ((bf16[3,384,16,128]{3,1,0,2:T(8,128)(2,1)}), bf16[3,384,16,128]{3,1,0,2:T(8,128)(2,1)}, u32[]{:S(2)}, u32[]{:S(2)}) async-start(bf16[3,384,16,128]{3,1,0,2:T(8,128)(2,1)} %copy.40), calls=%async_computation | async-start | bytes 9437184 | tf_op jit(solution)/shard_map/all_to_all | solution.py:119
  102.6 8.8 %copy-start = (bf16[8,384,128]{1,2,0:T(8,128)(2,1)S(1)}, bf16[8,384,128]{1,2,0:T(8,128)(2,1)}, u32[]{:S(2)}) copy-start(bf16[8,384,128]{1,2,0:T(8,128)(2,1)} %copy.43) | copy-start | bytes 2359300
  103.8 16.1 %collective-permute-start = (bf16[8,128,384]{2,1,0:T(8,128)(2,1)}, bf16[8,128,384]{2,1,0:T(8,128)(2,1)}, u32[]{:S(2)}, u32[]{:S(2)}) collective-permute-start(bf16[8,128,384]{2,1,0:T(8,128)(2,1)} %bitcast.41), channel_id=1, source_target_pairs={{0,1},{1,2},{2,3},{3,4},{4,5},{5,6},{6,7},{7,8},{8,9},{9,10},{10,1... | collective-permute-start | bytes 2359304 | tf_op jit(solution)/shard_map/ppermute | solution.py:21
  105.8 14.2 %collective-permute-start.3 = (bf16[8,384,128]{2,1,0:T(8,128)(2,1)}, bf16[8,384,128]{2,1,0:T(8,128)(2,1)}, u32[]{:S(2)}, u32[]{:S(2)}) collective-permute-start(bf16[8,384,128]{2,1,0:T(8,128)(2,1)} %get-tuple-element.14), channel_id=1, source_target_pairs={{1,0},{2,1},{3,2},{4,3},{5,4},{6,5},{7,6},{8,7},{9,8},{10,9},{11,1... | collective-permute-start | bytes 2359304 | tf_op jit(solution)/shard_map/ppermute | solution.py:21
  109.4 16.5 %collective-permute-start.2 = (bf16[8,384,128]{2,1,0:T(8,128)(2,1)}, bf16[8,384,128]{2,1,0:T(8,128)(2,1)}, u32[]{:S(2)}, u32[]{:S(2)}) collective-permute-start(bf16[8,384,128]{2,1,0:T(8,128)(2,1)} %get-tuple-element.15), channel_id=1, source_target_pairs={{0,1},{1,2},{2,3},{3,4},{4,5},{5,6},{6,7},{7,8},{8,9},{9,10},{10,1... | collective-permute-start | bytes 2359304 | tf_op jit(solution)/shard_map/ppermute | solution.py:21
  111.3 16.2 %collective-permute-start.1 = (bf16[8,128,384]{2,1,0:T(8,128)(2,1)S(1)}, bf16[8,128,384]{2,1,0:T(8,128)(2,1)}, u32[]{:S(2)}, u32[]{:S(2)}) collective-permute-start(bf16[8,128,384]{2,1,0:T(8,128)(2,1)S(1)} %bitcast.40), channel_id=1, source_target_pairs={{1,0},{2,1},{3,2},{4,3},{5,4},{6,5},{7,6},{8,7},{9,8},{10,9},{11,1... | collective-permute-start | bytes 2359304 | tf_op jit(solution)/shard_map/ppermute | solution.py:21

commit v5 on v3

--- a/solution.py
+++ b/solution.py
@@ -12,6 +12,7 @@
 KEEP = 6
 USED = 8
 CHUNKS = 1
+GROUP = 4
 LOG2_E = 1.4426950408889634
 
 
@@ -42,10 +43,16 @@
 
 def attend_kernel(which_ref, index_ref, count_ref, q_ref, kl_ref, kc_ref, kr_ref,
                   vl_ref, vc_ref, vr_ref, o_ref):
-    i = pl.program_id(0)
+    for g in range(q_ref.shape[0]):
+        attend_one(g, pl.program_id(0) * q_ref.shape[0] + g, which_ref, index_ref, count_ref,
+                   q_ref, kl_ref, kc_ref, kr_ref, vl_ref, vc_ref, vr_ref, o_ref)
+
+
+def attend_one(g, i, which_ref, index_ref, count_ref, q_ref, kl_ref, kc_ref, kr_ref,
+               vl_ref, vc_ref, vr_ref, o_ref):
     n = count_ref[i]
     score_scale = (HEAD_DIM ** (-0.5)) * LOG2_E
-    q = q_ref[0]
+    q = q_ref[g]
 
     def pick(l_ref, c_ref, r_ref, j):
         w = which_ref[i * KEEP + j]
@@ -77,7 +84,7 @@
         spread = p if spread is None else spread + p
         acc = pv if acc is None else acc + pv
     total = jnp.sum(spread, axis=1, keepdims=True)
-    o_ref[0] = (acc / total).astype(o_ref.dtype)
+    o_ref[g] = (acc / total).astype(o_ref.dtype)
 
 
 def attend(which, index, count, q, kl, kc, kr, vl, vc, vr):
@@ -87,10 +94,11 @@
     def whole(x):
         return pl.BlockSpec(x.shape, lambda i, *_: (0, 0, 0))
 
-    one = pl.BlockSpec((1, tile, width), lambda i, *_: (i, 0, 0))
+    group = GROUP if n_q % GROUP == 0 else 1
+    one = pl.BlockSpec((group, tile, width), lambda i, *_: (i, 0, 0))
     grid_spec = pltpu.PrefetchScalarGridSpec(
         num_scalar_prefetch=3,
-        grid=(n_q,),
+        grid=(n_q // group,),
         in_specs=[one] + [whole(x) for x in (kl, kc, kr, vl, vc, vr)],
         out_specs=one,
     )

time: 163 us -> 158 us (0.969)
  Pallas kernels: 32.8 us -> 28.3 us
    pallas_call x1, Pallas kernels: 32.8 us -> 28.3 us  [attend(): pl.pallas_call(attend_kernel, grid_spec=grid_spec, out_shape=jax.ShapeDty...]
  transfers between devices with their start and end apart: 7 -> 7, of which waited for: 5 -> 5; matrix products, arithmetic and copies ran while one was open for 9% -> 10% of each run, Pallas kernels for 0% -> 0%
where the time goes in v5:
time: 158 us; the launch traced here: 156 us
  waiting for transfers between devices  50.1 us (32%)
  blocking collectives  29.1 us (18%)
  Pallas kernels  28.3 us (18%)
  starting transfers between devices  24.5 us (16%)
  local copies, waits for them, and re-layouts  17.4 us (11%)
  between operations  3.93 us (2%)
  other arithmetic  2.74 us (2%)
    all_to_all x1, blocking collectives, body(): lax.all_to_all(attended, 'uly', split_axis=0, concat_axis=1, tiled=True)  29.1 us
    pallas_call x1, Pallas kernels, attend(): pl.pallas_call(attend_kernel, grid_spec=grid_spec, out_shape=jax.ShapeDty...  28.3 us
    all_to_all x1, waiting for transfers between devices, body(): lax.all_to_all(key_rows, 'uly', split_axis=1, concat_axis=0, tiled=True)  21 us
    all_to_all x1, waiting for transfers between devices, body(): lax.all_to_all(value_rows, 'uly', split_axis=1, concat_axis=0, tiled=True)  18 us
    ppermute x4, starting transfers between devices, passed_along(): return lax.ppermute(block, axis, route)  9.39 us
    ppermute x4, waiting for transfers between devices, passed_along(): return lax.ppermute(block, axis, route)  7.99 us
    unnamed x12, local copies, waits for them, and re-layouts  7.18 us
    all_to_all x1, starting transfers between devices, body(): lax.all_to_all(key_rows, 'uly', split_axis=1, concat_axis=0, tiled=True)  7.03 us
  transfers between devices with their start and end apart: 7, of which 5 were waited for; matrix products, arithmetic and copies ran while one was open for 10% of the time, Pallas kernels for 0%

profile of v5, /device:TPU:192, one launch (start us, length us, event | category | flops | bytes accessed | tf_op | source)
XLA Modules:
  0.0 156.1 jit_solution(10214451479130778271)
XLA Ops:
  0.0 2.6 %copy.22 = bf16[384,2048]{0,1:T(8,128)(2,1)} copy(bf16[384,2048]{1,0:T(8,128)(2,1)} %param.5) | data formatting | bytes 3145728 | tf_op args[1]
  2.6 7.0 %all-to-all-start.1 = ((bf16[384,16,128]{0,2,1:T(8,128)(2,1)}), bf16[384,16,128]{0,2,1:T(8,128)(2,1)S(1)}, u32[]{:S(2)}, u32[]{:S(2)}) async-start(bf16[384,16,128]{0,2,1:T(8,128)(2,1)} %bitcast.5), calls=%async_computation.1 | async-start | bytes 3145728 | tf_op jit(solution)/shard_map/all_to_all | solution.py:121
  9.6 1.9 %copy.23 = bf16[384,2048]{0,1:T(8,128)(2,1)S(1)} copy(bf16[384,2048]{1,0:T(8,128)(2,1)} %param.6) | data formatting | bytes 3145728 | tf_op args[2]
  11.5 1.6 %copy.24 = bf16[384,16,128]{2,0,1:T(8,128)(2,1)} copy(bf16[384,16,128]{0,2,1:T(8,128)(2,1)S(1)} %bitcast.26) | data formatting | bytes 3145728 | tf_op jit(solution)/shard_map/all_to_all | solution.py:122
  13.1 21.0 %all-to-all-done.1 = bf16[384,16,128]{0,2,1:T(8,128)(2,1)S(1)} async-done(((bf16[384,16,128]{0,2,1:T(8,128)(2,1)}), bf16[384,16,128]{0,2,1:T(8,128)(2,1)S(1)}, u32[]{:S(2)}, u32[]{:S(2)}) %all-to-all-start.1) | async-done | bytes 1572896 | tf_op jit(solution)/shard_map/all_to_all | solution.py:121
  34.1 0.0 copy-start
  34.1 3.7 %all-to-all-start.2 = ((bf16[384,16,128]{2,0,1:T(8,128)(2,1)}), bf16[384,16,128]{2,0,1:T(8,128)(2,1)S(1)}, u32[]{:S(2)}, u32[]{:S(2)}) async-start(bf16[384,16,128]{2,0,1:T(8,128)(2,1)} %copy.24), calls=%async_computation.2 | async-start | bytes 3145728 | tf_op jit(solution)/shard_map/all_to_all | solution.py:122
  37.9 2.6 %copy.20 = bf16[384,2048]{0,1:T(8,128)(2,1)} copy(bf16[384,2048]{1,0:T(8,128)(2,1)} %param.4) | data formatting | bytes 3145728 | tf_op args[0]
  40.4 0.0 copy-start.2
  40.4 2.6 %copy.21 = bf16[384,16,128]{2,0,1:T(8,128)(2,1)} copy(bf16[384,16,128]{0,2,1:T(8,128)(2,1)} %bitcast.27) | data formatting | bytes 3145728 | tf_op jit(solution)/shard_map/all_to_all | solution.py:166
  43.1 0.0 copy-done.2
  43.1 18.0 %all-to-all-done.2 = bf16[384,16,128]{2,0,1:T(8,128)(2,1)S(1)} async-done(((bf16[384,16,128]{2,0,1:T(8,128)(2,1)}), bf16[384,16,128]{2,0,1:T(8,128)(2,1)S(1)}, u32[]{:S(2)}, u32[]{:S(2)}) %all-to-all-start.2) | async-done | bytes 1572896 | tf_op jit(solution)/shard_map/all_to_all | solution.py:122
  61.1 0.0 copy-start.1
  61.1 4.4 %all-to-all-start = ((bf16[384,16,128]{2,0,1:T(8,128)(2,1)}), bf16[384,16,128]{2,0,1:T(8,128)(2,1)}, u32[]{:S(2)}, u32[]{:S(2)}) async-start(bf16[384,16,128]{2,0,1:T(8,128)(2,1)} %copy.21), calls=%async_computation | async-start | bytes 3145728 | tf_op jit(solution)/shard_map/all_to_all | solution.py:166
  65.5 0.2 select_reduce_fusion.1
  65.8 0.7 fusion.5
  67.7 0.6 fusion.6
  70.8 0.0 copy-done.1
  70.8 1.4 dynamic-slice_bitcast_fusion
  72.2 1.9 %collective-permute-start.3 = (bf16[8,384,128]{2,1,0:T(8,128)(2,1)}, bf16[8,384,128]{2,1,0:T(8,128)(2,1)}, u32[]{:S(2)}, u32[]{:S(2)}) collective-permute-start(bf16[8,384,128]{2,1,0:T(8,128)(2,1)} %get-tuple-element.9), channel_id=1, source_target_pairs={{1,0},{2,1},{3,2},{4,3},{5,4},{6,5},{7,6},{8,7},{9,8},{10,9},{11,1... | collective-permute-start | bytes 2359304 | tf_op jit(solution)/shard_map/ppermute | solution.py:22
  74.1 2.4 %collective-permute-start.2 = (bf16[8,384,128]{2,1,0:T(8,128)(2,1)}, bf16[8,384,128]{2,1,0:T(8,128)(2,1)}, u32[]{:S(2)}, u32[]{:S(2)}) collective-permute-start(bf16[8,384,128]{2,1,0:T(8,128)(2,1)} %get-tuple-element.10), channel_id=1, source_target_pairs={{0,1},{1,2},{2,3},{3,4},{4,5},{5,6},{6,7},{7,8},{8,9},{9,10},{10,1... | collective-permute-start | bytes 2359304 | tf_op jit(solution)/shard_map/ppermute | solution.py:22
  76.5 0.0 copy-done
  76.5 0.2 dynamic-slice_bitcast_fusion.2
  76.7 3.2 %collective-permute-start.1 = (bf16[8,128,384]{2,1,0:T(8,128)(2,1)S(1)}, bf16[8,128,384]{2,1,0:T(8,128)(2,1)S(1)}, u32[]{:S(2)}, u32[]{:S(2)}) collective-permute-start(bf16[8,128,384]{2,1,0:T(8,128)(2,1)S(1)} %get-tuple-element.11), channel_id=1, source_target_pairs={{1,0},{2,1},{3,2},{4,3},{5,4},{6,5},{7,6},{8,7},{9,8},{10,9},{11,1... | collective-permute-start | bytes 2359304 | tf_op jit(solution)/shard_map/ppermute | solution.py:22
  79.9 1.9 %collective-permute-start = (bf16[8,128,384]{2,1,0:T(8,128)(2,1)S(1)}, bf16[8,128,384]{2,1,0:T(8,128)(2,1)}, u32[]{:S(2)}, u32[]{:S(2)}) collective-permute-start(bf16[8,128,384]{2,1,0:T(8,128)(2,1)S(1)} %get-tuple-element.12), channel_id=1, source_target_pairs={{0,1},{1,2},{2,3},{3,4},{4,5},{5,6},{6,7},{7,8},{8,9},{9,10},{10,1... | collective-permute-start | bytes 2359304 | tf_op jit(solution)/shard_map/ppermute | solution.py:22
  81.8 0.1 copy.19
  82.0 0.6 gather_fusion
  82.6 0.7 convert_reduce_fusion
  83.2 0.1 select_n.122
  83.3 1.8 %compare_select_fusion.9 = (s32[96]{0:T(128)}, s32[96]{0:T(128)}) fusion(s32[96]{0:T(128)S(1)} %select_n.122, s32[]{:T(128)} %bitcast.2, s32[]{:T(128)} %bitcast.1, s32[]{:T(128)S(6)} %axis_index.12), kind=kLoop, calls=%fused_computation.33 | loop fusion | flops 2976 | bytes 1164 | tf_op jit(solution)/shard_map/jit(_where)/select_n | solution.py:160
  85.1 3.1 %all-to-all-done = bf16[384,16,128]{2,0,1:T(8,128)(2,1)} async-done(((bf16[384,16,128]{2,0,1:T(8,128)(2,1)}), bf16[384,16,128]{2,0,1:T(8,128)(2,1)}, u32[]{:S(2)}, u32[]{:S(2)}) %all-to-all-start) | async-done | bytes 1572896 | tf_op jit(solution)/shard_map/all_to_all | solution.py:166
  88.2 0.0 collective-permute-done.3.vr_ref
  88.2 0.0 collective-permute-done.2.vl_ref
  88.2 4.1 %collective-permute-done.1.kr_ref = bf16[8,128,384]{2,1,0:T(8,128)(2,1)S(1)} collective-permute-done((bf16[8,128,384]{2,1,0:T(8,128)(2,1)S(1)}, bf16[8,128,384]{2,1,0:T(8,128)(2,1)S(1)}, u32[]{:S(2)}, u32[]{:S(2)}) %collective-permute-start.1) | collective-permute-done | bytes 786464 | tf_op jit(solution)/shard_map/ppermute | solution.py:22
  92.2 0.0 copy-start.3
  92.2 3.9 %collective-permute-done.kl_ref = bf16[8,128,384]{2,1,0:T(8,128)(2,1)} collective-permute-done((bf16[8,128,384]{2,1,0:T(8,128)(2,1)S(1)}, bf16[8,128,384]{2,1,0:T(8,128)(2,1)}, u32[]{:S(2)}, u32[]{:S(2)}) %collective-permute-start) | collective-permute-done | bytes 786464 | tf_op jit(solution)/shard_map/ppermute | solution.py:22
  96.2 0.0 copy-done.3
  96.2 28.3 %shard_map.46 = bf16[16,384,128]{2,1,0:T(8,128)(2,1)} custom-call(s32[96]{0:T(128)} %get-tuple-element.20.which_ref, s32[96]{0:T(128)} %get-tuple-element.19.index_ref, s32[16]{0:T(128)} %get-tuple-element.7.count_ref, bf16[16,384,128]{2,1,0:T(8,128)(2,1)} %bitcast.4.q_ref, bf16[8,128,384]{2,1,0:T(8,128)(2,1)} %collective-permute-done.kl_ref, ...), custom_call_target="tpu_custom_call" | custom-call | flops 7247757312 | bytes 9437184 | tf_op jit(solution)/shard_map/pallas_call | solution.py:110
  124.5 29.1 %all_to_all.61 = bf16[16,384,128]{2,1,0:T(8,128)(2,1)S(1)} all-to-all(bf16[16,384,128]{2,1,0:T(8,128)(2,1)} %shard_map.46), channel_id=1, replica_groups=mesh['uly'=16,'blk'=16] {'uly'}, dimensions={0} | all-to-all | bytes 3145728 | tf_op jit(solution)/shard_map/all_to_all | solution.py:174
  153.6 0.9 copy.25
  154.5 1.6 %copy.26 = bf16[384,2048]{1,0:T(8,128)(2,1)} copy(bf16[384,2048]{0,1:T(8,128)(2,1)S(1)} %bitcast.25) | data formatting | bytes 3145728 | tf_op jit(solution)/shard_map/all_to_all | solution.py:174
  (9 shorter events, 0.1 us)
Async XLA Ops:
  2.6 31.6 %all-to-all-start.1 = ((bf16[384,16,128]{0,2,1:T(8,128)(2,1)}), bf16[384,16,128]{0,2,1:T(8,128)(2,1)S(1)}, u32[]{:S(2)}, u32[]{:S(2)}) async-start(bf16[384,16,128]{0,2,1:T(8,128)(2,1)} %bitcast.5), calls=%async_computation.1 | async-start | bytes 3145728 | tf_op jit(solution)/shard_map/all_to_all | solution.py:121
  34.1 42.4 %copy-start = (bf16[384,16,128]{0,2,1:T(8,128)(2,1)}, bf16[384,16,128]{0,2,1:T(8,128)(2,1)S(1)}, u32[]{:S(2)}) copy-start(bf16[384,16,128]{0,2,1:T(8,128)(2,1)S(1)} %all-to-all-done.1) | copy-start | bytes 4718596
  34.1 27.0 %all-to-all-start.2 = ((bf16[384,16,128]{2,0,1:T(8,128)(2,1)}), bf16[384,16,128]{2,0,1:T(8,128)(2,1)S(1)}, u32[]{:S(2)}, u32[]{:S(2)}) async-start(bf16[384,16,128]{2,0,1:T(8,128)(2,1)} %copy.24), calls=%async_computation.2 | async-start | bytes 3145728 | tf_op jit(solution)/shard_map/all_to_all | solution.py:122
  40.4 2.6 %copy-start.2 = (s32[256,6]{0,1:T(8,128)S(1)}, s32[256,6]{0,1:T(8,128)}, u32[]{:S(2)}) copy-start(s32[256,6]{0,1:T(8,128)} %param.7) | copy-start | bytes 18436
  61.1 9.7 %copy-start.1 = (bf16[384,16,128]{2,0,1:T(8,128)(2,1)}, bf16[384,16,128]{2,0,1:T(8,128)(2,1)S(1)}, u32[]{:S(2)}) copy-start(bf16[384,16,128]{2,0,1:T(8,128)(2,1)S(1)} %all-to-all-done.2) | copy-start | bytes 4718596
  61.1 27.0 %all-to-all-start = ((bf16[384,16,128]{2,0,1:T(8,128)(2,1)}), bf16[384,16,128]{2,0,1:T(8,128)(2,1)}, u32[]{:S(2)}, u32[]{:S(2)}) async-start(bf16[384,16,128]{2,0,1:T(8,128)(2,1)} %copy.21), calls=%async_computation | async-start | bytes 3145728 | tf_op jit(solution)/shard_map/all_to_all | solution.py:166
  72.2 16.0 %collective-permute-start.3 = (bf16[8,384,128]{2,1,0:T(8,128)(2,1)}, bf16[8,384,128]{2,1,0:T(8,128)(2,1)}, u32[]{:S(2)}, u32[]{:S(2)}) collective-permute-start(bf16[8,384,128]{2,1,0:T(8,128)(2,1)} %get-tuple-element.9), channel_id=1, source_target_pairs={{1,0},{2,1},{3,2},{4,3},{5,4},{6,5},{7,6},{8,7},{9,8},{10,9},{11,1... | collective-permute-start | bytes 2359304 | tf_op jit(solution)/shard_map/ppermute | solution.py:22
  74.1 14.1 %collective-permute-start.2 = (bf16[8,384,128]{2,1,0:T(8,128)(2,1)}, bf16[8,384,128]{2,1,0:T(8,128)(2,1)}, u32[]{:S(2)}, u32[]{:S(2)}) collective-permute-start(bf16[8,384,128]{2,1,0:T(8,128)(2,1)} %get-tuple-element.10), channel_id=1, source_target_pairs={{0,1},{1,2},{2,3},{3,4},{4,5},{5,6},{6,7},{7,8},{8,9},{9,10},{10,1... | collective-permute-start | bytes 2359304 | tf_op jit(solution)/shard_map/ppermute | solution.py:22
  76.7 15.5 %collective-permute-start.1 = (bf16[8,128,384]{2,1,0:T(8,128)(2,1)S(1)}, bf16[8,128,384]{2,1,0:T(8,128)(2,1)S(1)}, u32[]{:S(2)}, u32[]{:S(2)}) collective-permute-start(bf16[8,128,384]{2,1,0:T(8,128)(2,1)S(1)} %get-tuple-element.11), channel_id=1, source_target_pairs={{1,0},{2,1},{3,2},{4,3},{5,4},{6,5},{7,6},{8,7},{9,8},{10,9},{11,1... | collective-permute-start | bytes 2359304 | tf_op jit(solution)/shard_map/ppermute | solution.py:22
  79.9 16.3 %collective-permute-start = (bf16[8,128,384]{2,1,0:T(8,128)(2,1)S(1)}, bf16[8,128,384]{2,1,0:T(8,128)(2,1)}, u32[]{:S(2)}, u32[]{:S(2)}) collective-permute-start(bf16[8,128,384]{2,1,0:T(8,128)(2,1)S(1)} %get-tuple-element.12), channel_id=1, source_target_pairs={{0,1},{1,2},{2,3},{3,4},{4,5},{5,6},{6,7},{7,8},{8,9},{9,10},{10,1... | collective-permute-start | bytes 2359304 | tf_op jit(solution)/shard_map/ppermute | solution.py:22
  92.2 3.9 %copy-start.3 = (bf16[8,128,384]{2,1,0:T(8,128)(2,1)}, bf16[8,128,384]{2,1,0:T(8,128)(2,1)S(1)}, u32[]{:S(2)}) copy-start(bf16[8,128,384]{2,1,0:T(8,128)(2,1)S(1)} %collective-permute-done.1.kr_ref) | copy-start | bytes 2359300

commit v6 on v5

--- a/solution.py
+++ b/solution.py
@@ -42,14 +42,30 @@
 
 
 def attend_kernel(which_ref, index_ref, count_ref, q_ref, kl_ref, kc_ref, kr_ref,
-                  vl_ref, vc_ref, vr_ref, o_ref):
+                  vl_hbm, vc_hbm, vr_hbm, o_ref, vl_ref, vc_ref, vr_ref, sems):
+    first = pl.program_id(0) == 0
+    loads = [pltpu.make_async_copy(src, dst, sems.at[k])
+             for k, (src, dst) in enumerate(((vl_hbm, vl_ref), (vc_hbm, vc_ref), (vr_hbm, vr_ref)))]
+
+    @pl.when(first)
+    def _():
+        for load in loads:
+            load.start()
+
+    def values_ready():
+        @pl.when(first)
+        def _():
+            for load in loads:
+                load.wait()
+
     for g in range(q_ref.shape[0]):
         attend_one(g, pl.program_id(0) * q_ref.shape[0] + g, which_ref, index_ref, count_ref,
-                   q_ref, kl_ref, kc_ref, kr_ref, vl_ref, vc_ref, vr_ref, o_ref)
+                   q_ref, kl_ref, kc_ref, kr_ref, vl_ref, vc_ref, vr_ref, o_ref,
+                   values_ready if g == 0 else None)
 
 
 def attend_one(g, i, which_ref, index_ref, count_ref, q_ref, kl_ref, kc_ref, kr_ref,
-               vl_ref, vc_ref, vr_ref, o_ref):
+               vl_ref, vc_ref, vr_ref, o_ref, before_values=None):
     n = count_ref[i]
     score_scale = (HEAD_DIM ** (-0.5)) * LOG2_E
     q = q_ref[g]
@@ -74,6 +90,8 @@
         scores.append(s)
         top = s if top is None else jnp.maximum(top, s)
     m = jnp.max(top, axis=1, keepdims=True)
+    if before_values is not None:
+        before_values()
 
     spread = None
     acc = None
@@ -99,8 +117,11 @@
     grid_spec = pltpu.PrefetchScalarGridSpec(
         num_scalar_prefetch=3,
         grid=(n_q // group,),
-        in_specs=[one] + [whole(x) for x in (kl, kc, kr, vl, vc, vr)],
+        in_specs=[one] + [whole(x) for x in (kl, kc, kr)]
+        + [pl.BlockSpec(memory_space=pl.ANY)] * 3,
         out_specs=one,
+        scratch_shapes=[pltpu.VMEM(x.shape, x.dtype) for x in (vl, vc, vr)]
+        + [pltpu.SemaphoreType.DMA((3,))],
     )
     cost = pl.CostEstimate(
         flops=n_q * KEEP * tile * key_tile * width * 4,

time: 158 us -> 159 us (level)
  no operation moved by 1% of the time
where the time goes in v6:
time: 159 us; the launch traced here: 157 us
  waiting for transfers between devices  50.1 us (32%)
  Pallas kernels  29.2 us (18%)
  blocking collectives  29.1 us (18%)
  starting transfers between devices  24.5 us (15%)
  local copies, waits for them, and re-layouts  17.4 us (11%)
  between operations  3.94 us (2%)
  other arithmetic  2.74 us (2%)
    pallas_call x1, Pallas kernels, attend(): pl.pallas_call(attend_kernel, grid_spec=grid_spec, out_shape=jax.ShapeDty...  29.2 us
    all_to_all x1, blocking collectives, body(): lax.all_to_all(attended, 'uly', split_axis=0, concat_axis=1, tiled=True)  29.1 us
    all_to_all x1, waiting for transfers between devices, body(): lax.all_to_all(key_rows, 'uly', split_axis=1, concat_axis=0, tiled=True)  21 us
    all_to_all x1, waiting for transfers between devices, body(): lax.all_to_all(value_rows, 'uly', split_axis=1, concat_axis=0, tiled=True)  18 us
    ppermute x4, starting transfers between devices, passed_along(): return lax.ppermute(block, axis, route)  9.39 us
    ppermute x4, waiting for transfers between devices, passed_along(): return lax.ppermute(block, axis, route)  7.99 us
    unnamed x12, local copies, waits for them, and re-layouts  7.18 us
    all_to_all x1, starting transfers between devices, body(): lax.all_to_all(key_rows, 'uly', split_axis=1, concat_axis=0, tiled=True)  7.03 us
  transfers between devices with their start and end apart: 7, of which 5 were waited for; matrix products, arithmetic and copies ran while one was open for 10% of the time, Pallas kernels for 0%

profile of v6, /device:TPU:192, one launch (start us, length us, event | category | flops | bytes accessed | tf_op | source)
XLA Modules:
  0.0 156.9 jit_solution(132991947455512466)
XLA Ops:
  0.0 2.6 %copy.22 = bf16[384,2048]{0,1:T(8,128)(2,1)} copy(bf16[384,2048]{1,0:T(8,128)(2,1)} %param.5) | data formatting | bytes 3145728 | tf_op args[1]
  2.6 7.0 %all-to-all-start.1 = ((bf16[384,16,128]{0,2,1:T(8,128)(2,1)}), bf16[384,16,128]{0,2,1:T(8,128)(2,1)S(1)}, u32[]{:S(2)}, u32[]{:S(2)}) async-start(bf16[384,16,128]{0,2,1:T(8,128)(2,1)} %bitcast.5), calls=%async_computation.1 | async-start | bytes 3145728 | tf_op jit(solution)/shard_map/all_to_all | solution.py:142
  9.6 1.9 %copy.23 = bf16[384,2048]{0,1:T(8,128)(2,1)S(1)} copy(bf16[384,2048]{1,0:T(8,128)(2,1)} %param.6) | data formatting | bytes 3145728 | tf_op args[2]
  11.5 1.6 %copy.24 = bf16[384,16,128]{2,0,1:T(8,128)(2,1)} copy(bf16[384,16,128]{0,2,1:T(8,128)(2,1)S(1)} %bitcast.26) | data formatting | bytes 3145728 | tf_op jit(solution)/shard_map/all_to_all | solution.py:143
  13.1 21.0 %all-to-all-done.1 = bf16[384,16,128]{0,2,1:T(8,128)(2,1)S(1)} async-done(((bf16[384,16,128]{0,2,1:T(8,128)(2,1)}), bf16[384,16,128]{0,2,1:T(8,128)(2,1)S(1)}, u32[]{:S(2)}, u32[]{:S(2)}) %all-to-all-start.1) | async-done | bytes 1572896 | tf_op jit(solution)/shard_map/all_to_all | solution.py:142
  34.1 0.0 copy-start
  34.1 3.7 %all-to-all-start.2 = ((bf16[384,16,128]{2,0,1:T(8,128)(2,1)}), bf16[384,16,128]{2,0,1:T(8,128)(2,1)S(1)}, u32[]{:S(2)}, u32[]{:S(2)}) async-start(bf16[384,16,128]{2,0,1:T(8,128)(2,1)} %copy.24), calls=%async_computation.2 | async-start | bytes 3145728 | tf_op jit(solution)/shard_map/all_to_all | solution.py:143
  37.9 2.6 %copy.20 = bf16[384,2048]{0,1:T(8,128)(2,1)} copy(bf16[384,2048]{1,0:T(8,128)(2,1)} %param.4) | data formatting | bytes 3145728 | tf_op args[0]
  40.4 0.0 copy-start.2
  40.4 2.6 %copy.21 = bf16[384,16,128]{2,0,1:T(8,128)(2,1)} copy(bf16[384,16,128]{0,2,1:T(8,128)(2,1)} %bitcast.27) | data formatting | bytes 3145728 | tf_op jit(solution)/shard_map/all_to_all | solution.py:187
  43.1 0.0 copy-done.2
  43.1 18.0 %all-to-all-done.2 = bf16[384,16,128]{2,0,1:T(8,128)(2,1)S(1)} async-done(((bf16[384,16,128]{2,0,1:T(8,128)(2,1)}), bf16[384,16,128]{2,0,1:T(8,128)(2,1)S(1)}, u32[]{:S(2)}, u32[]{:S(2)}) %all-to-all-start.2) | async-done | bytes 1572896 | tf_op jit(solution)/shard_map/all_to_all | solution.py:143
  61.1 0.0 copy-start.1
  61.1 4.4 %all-to-all-start = ((bf16[384,16,128]{2,0,1:T(8,128)(2,1)}), bf16[384,16,128]{2,0,1:T(8,128)(2,1)}, u32[]{:S(2)}, u32[]{:S(2)}) async-start(bf16[384,16,128]{2,0,1:T(8,128)(2,1)} %copy.21), calls=%async_computation | async-start | bytes 3145728 | tf_op jit(solution)/shard_map/all_to_all | solution.py:187
  65.5 0.2 select_reduce_fusion.1
  65.8 0.7 fusion.5
  67.7 0.6 fusion.6
  70.8 0.0 copy-done.1
  70.8 1.4 dynamic-slice_bitcast_fusion
  72.2 1.9 %collective-permute-start.3 = (bf16[8,384,128]{2,1,0:T(8,128)(2,1)}, bf16[8,384,128]{2,1,0:T(8,128)(2,1)}, u32[]{:S(2)}, u32[]{:S(2)}) collective-permute-start(bf16[8,384,128]{2,1,0:T(8,128)(2,1)} %get-tuple-element.9), channel_id=1, source_target_pairs={{1,0},{2,1},{3,2},{4,3},{5,4},{6,5},{7,6},{8,7},{9,8},{10,9},{11,1... | collective-permute-start | bytes 2359304 | tf_op jit(solution)/shard_map/ppermute | solution.py:22
  74.1 2.4 %collective-permute-start.2 = (bf16[8,384,128]{2,1,0:T(8,128)(2,1)}, bf16[8,384,128]{2,1,0:T(8,128)(2,1)}, u32[]{:S(2)}, u32[]{:S(2)}) collective-permute-start(bf16[8,384,128]{2,1,0:T(8,128)(2,1)} %get-tuple-element.10), channel_id=1, source_target_pairs={{0,1},{1,2},{2,3},{3,4},{4,5},{5,6},{6,7},{7,8},{8,9},{9,10},{10,1... | collective-permute-start | bytes 2359304 | tf_op jit(solution)/shard_map/ppermute | solution.py:22
  76.5 0.0 copy-done
  76.5 0.2 dynamic-slice_bitcast_fusion.2
  76.7 3.2 %collective-permute-start.1 = (bf16[8,128,384]{2,1,0:T(8,128)(2,1)S(1)}, bf16[8,128,384]{2,1,0:T(8,128)(2,1)S(1)}, u32[]{:S(2)}, u32[]{:S(2)}) collective-permute-start(bf16[8,128,384]{2,1,0:T(8,128)(2,1)S(1)} %get-tuple-element.11), channel_id=1, source_target_pairs={{1,0},{2,1},{3,2},{4,3},{5,4},{6,5},{7,6},{8,7},{9,8},{10,9},{11,1... | collective-permute-start | bytes 2359304 | tf_op jit(solution)/shard_map/ppermute | solution.py:22
  79.9 1.9 %collective-permute-start = (bf16[8,128,384]{2,1,0:T(8,128)(2,1)S(1)}, bf16[8,128,384]{2,1,0:T(8,128)(2,1)}, u32[]{:S(2)}, u32[]{:S(2)}) collective-permute-start(bf16[8,128,384]{2,1,0:T(8,128)(2,1)S(1)} %get-tuple-element.12), channel_id=1, source_target_pairs={{0,1},{1,2},{2,3},{3,4},{4,5},{5,6},{6,7},{7,8},{8,9},{9,10},{10,1... | collective-permute-start | bytes 2359304 | tf_op jit(solution)/shard_map/ppermute | solution.py:22
  81.8 0.1 copy.19
  82.0 0.6 gather_fusion
  82.6 0.7 convert_reduce_fusion
  83.2 0.1 select_n.122
  83.3 1.8 %compare_select_fusion.9 = (s32[96]{0:T(128)}, s32[96]{0:T(128)}) fusion(s32[96]{0:T(128)S(1)} %select_n.122, s32[]{:T(128)} %bitcast.2, s32[]{:T(128)} %bitcast.1, s32[]{:T(128)S(6)} %axis_index.12), kind=kLoop, calls=%fused_computation.33 | loop fusion | flops 2976 | bytes 1164 | tf_op jit(solution)/shard_map/jit(_where)/select_n | solution.py:181
  85.1 3.1 %all-to-all-done = bf16[384,16,128]{2,0,1:T(8,128)(2,1)} async-done(((bf16[384,16,128]{2,0,1:T(8,128)(2,1)}), bf16[384,16,128]{2,0,1:T(8,128)(2,1)}, u32[]{:S(2)}, u32[]{:S(2)}) %all-to-all-start) | async-done | bytes 1572896 | tf_op jit(solution)/shard_map/all_to_all | solution.py:187
  88.2 0.0 collective-permute-done.3.vr_hbm
  88.2 0.0 collective-permute-done.2.vl_hbm
  88.2 4.1 %collective-permute-done.1.kr_ref = bf16[8,128,384]{2,1,0:T(8,128)(2,1)S(1)} collective-permute-done((bf16[8,128,384]{2,1,0:T(8,128)(2,1)S(1)}, bf16[8,128,384]{2,1,0:T(8,128)(2,1)S(1)}, u32[]{:S(2)}, u32[]{:S(2)}) %collective-permute-start.1) | collective-permute-done | bytes 786464 | tf_op jit(solution)/shard_map/ppermute | solution.py:22
  92.2 0.0 copy-start.3
  92.2 3.9 %collective-permute-done.kl_ref = bf16[8,128,384]{2,1,0:T(8,128)(2,1)} collective-permute-done((bf16[8,128,384]{2,1,0:T(8,128)(2,1)S(1)}, bf16[8,128,384]{2,1,0:T(8,128)(2,1)}, u32[]{:S(2)}, u32[]{:S(2)}) %collective-permute-start) | collective-permute-done | bytes 786464 | tf_op jit(solution)/shard_map/ppermute | solution.py:22
  96.2 0.0 copy-done.3
  96.2 29.2 %shard_map.46 = bf16[16,384,128]{2,1,0:T(8,128)(2,1)} custom-call(s32[96]{0:T(128)} %get-tuple-element.20.which_ref, s32[96]{0:T(128)} %get-tuple-element.19.index_ref, s32[16]{0:T(128)} %get-tuple-element.7.count_ref, bf16[16,384,128]{2,1,0:T(8,128)(2,1)} %bitcast.4.q_ref, bf16[8,128,384]{2,1,0:T(8,128)(2,1)} %collective-permute-done.kl_ref, ...), custom_call_target="tpu_custom_call" | custom-call | flops 7247757312 | bytes 9437184 | tf_op jit(solution)/shard_map/pallas_call | solution.py:131
  125.3 29.1 %all_to_all.61 = bf16[16,384,128]{2,1,0:T(8,128)(2,1)S(1)} all-to-all(bf16[16,384,128]{2,1,0:T(8,128)(2,1)} %shard_map.46), channel_id=1, replica_groups=mesh['uly'=16,'blk'=16] {'uly'}, dimensions={0} | all-to-all | bytes 3145728 | tf_op jit(solution)/shard_map/all_to_all | solution.py:195
  154.4 0.9 copy.25
  155.3 1.6 %copy.26 = bf16[384,2048]{1,0:T(8,128)(2,1)} copy(bf16[384,2048]{0,1:T(8,128)(2,1)S(1)} %bitcast.25) | data formatting | bytes 3145728 | tf_op jit(solution)/shard_map/all_to_all | solution.py:195
  (9 shorter events, 0.1 us)
Async XLA Ops:
  2.6 31.6 %all-to-all-start.1 = ((bf16[384,16,128]{0,2,1:T(8,128)(2,1)}), bf16[384,16,128]{0,2,1:T(8,128)(2,1)S(1)}, u32[]{:S(2)}, u32[]{:S(2)}) async-start(bf16[384,16,128]{0,2,1:T(8,128)(2,1)} %bitcast.5), calls=%async_computation.1 | async-start | bytes 3145728 | tf_op jit(solution)/shard_map/all_to_all | solution.py:142
  34.1 42.4 %copy-start = (bf16[384,16,128]{0,2,1:T(8,128)(2,1)}, bf16[384,16,128]{0,2,1:T(8,128)(2,1)S(1)}, u32[]{:S(2)}) copy-start(bf16[384,16,128]{0,2,1:T(8,128)(2,1)S(1)} %all-to-all-done.1) | copy-start | bytes 4718596
  34.1 27.0 %all-to-all-start.2 = ((bf16[384,16,128]{2,0,1:T(8,128)(2,1)}), bf16[384,16,128]{2,0,1:T(8,128)(2,1)S(1)}, u32[]{:S(2)}, u32[]{:S(2)}) async-start(bf16[384,16,128]{2,0,1:T(8,128)(2,1)} %copy.24), calls=%async_computation.2 | async-start | bytes 3145728 | tf_op jit(solution)/shard_map/all_to_all | solution.py:143
  40.4 2.6 %copy-start.2 = (s32[256,6]{0,1:T(8,128)S(1)}, s32[256,6]{0,1:T(8,128)}, u32[]{:S(2)}) copy-start(s32[256,6]{0,1:T(8,128)} %param.7) | copy-start | bytes 18436
  61.1 9.7 %copy-start.1 = (bf16[384,16,128]{2,0,1:T(8,128)(2,1)}, bf16[384,16,128]{2,0,1:T(8,128)(2,1)S(1)}, u32[]{:S(2)}) copy-start(bf16[384,16,128]{2,0,1:T(8,128)(2,1)S(1)} %all-to-all-done.2) | copy-start | bytes 4718596
  61.1 27.0 %all-to-all-start = ((bf16[384,16,128]{2,0,1:T(8,128)(2,1)}), bf16[384,16,128]{2,0,1:T(8,128)(2,1)}, u32[]{:S(2)}, u32[]{:S(2)}) async-start(bf16[384,16,128]{2,0,1:T(8,128)(2,1)} %copy.21), calls=%async_computation | async-start | bytes 3145728 | tf_op jit(solution)/shard_map/all_to_all | solution.py:187
  72.2 16.0 %collective-permute-start.3 = (bf16[8,384,128]{2,1,0:T(8,128)(2,1)}, bf16[8,384,128]{2,1,0:T(8,128)(2,1)}, u32[]{:S(2)}, u32[]{:S(2)}) collective-permute-start(bf16[8,384,128]{2,1,0:T(8,128)(2,1)} %get-tuple-element.9), channel_id=1, source_target_pairs={{1,0},{2,1},{3,2},{4,3},{5,4},{6,5},{7,6},{8,7},{9,8},{10,9},{11,1... | collective-permute-start | bytes 2359304 | tf_op jit(solution)/shard_map/ppermute | solution.py:22
  74.1 14.1 %collective-permute-start.2 = (bf16[8,384,128]{2,1,0:T(8,128)(2,1)}, bf16[8,384,128]{2,1,0:T(8,128)(2,1)}, u32[]{:S(2)}, u32[]{:S(2)}) collective-permute-start(bf16[8,384,128]{2,1,0:T(8,128)(2,1)} %get-tuple-element.10), channel_id=1, source_target_pairs={{0,1},{1,2},{2,3},{3,4},{4,5},{5,6},{6,7},{7,8},{8,9},{9,10},{10,1... | collective-permute-start | bytes 2359304 | tf_op jit(solution)/shard_map/ppermute | solution.py:22
  76.7 15.5 %collective-permute-start.1 = (bf16[8,128,384]{2,1,0:T(8,128)(2,1)S(1)}, bf16[8,128,384]{2,1,0:T(8,128)(2,1)S(1)}, u32[]{:S(2)}, u32[]{:S(2)}) collective-permute-start(bf16[8,128,384]{2,1,0:T(8,128)(2,1)S(1)} %get-tuple-element.11), channel_id=1, source_target_pairs={{1,0},{2,1},{3,2},{4,3},{5,4},{6,5},{7,6},{8,7},{9,8},{10,9},{11,1... | collective-permute-start | bytes 2359304 | tf_op jit(solution)/shard_map/ppermute | solution.py:22
  79.9 16.3 %collective-permute-start = (bf16[8,128,384]{2,1,0:T(8,128)(2,1)S(1)}, bf16[8,128,384]{2,1,0:T(8,128)(2,1)}, u32[]{:S(2)}, u32[]{:S(2)}) collective-permute-start(bf16[8,128,384]{2,1,0:T(8,128)(2,1)S(1)} %get-tuple-element.12), channel_id=1, source_target_pairs={{0,1},{1,2},{2,3},{3,4},{4,5},{5,6},{6,7},{7,8},{8,9},{9,10},{10,1... | collective-permute-start | bytes 2359304 | tf_op jit(solution)/shard_map/ppermute | solution.py:22
  92.2 3.9 %copy-start.3 = (bf16[8,128,384]{2,1,0:T(8,128)(2,1)}, bf16[8,128,384]{2,1,0:T(8,128)(2,1)S(1)}, u32[]{:S(2)}) copy-start(bf16[8,128,384]{2,1,0:T(8,128)(2,1)S(1)} %collective-permute-done.1.kr_ref) | copy-start | bytes 2359300

commit v7 on v5

--- a/solution.py
+++ b/solution.py
@@ -161,6 +161,7 @@
     which = jnp.where(is_live, which, 1)
     count = jnp.sum(is_live.astype(jnp.int32), axis=1)
 
+    query_rows, left_key, right_key = lax.optimization_barrier((query_rows, left_key, right_key))
     pieces = []
     for c in range(CHUNKS):
         query_part = lax.all_to_all(

time: 158 us -> 157 us (level)
  starting transfers between devices: 24.5 us -> 29 us
  waiting for transfers between devices: 50.1 us -> 47.2 us
  blocking collectives: 29.1 us -> 27.1 us
    all_to_all x1, waiting for transfers between devices: 18 us -> 0.01 us  [body(): lax.all_to_all(value_rows, 'uly', split_axis=1, concat_axis=0, tiled=True)]
    all_to_all x1, waiting for transfers between devices: 3.06 us -> 11.2 us  [body(): lax.all_to_all(query_rows[c * chunk:(c + 1) * chunk], 'uly', split_axis=1...]
    ppermute x4, waiting for transfers between devices: 7.99 us -> 15.1 us  [passed_along(): return lax.ppermute(block, axis, route)]
    all_to_all x1, starting transfers between devices: 4.4 us -> 7.15 us  [body(): lax.all_to_all(query_rows[c * chunk:(c + 1) * chunk], 'uly', split_axis=1...]
    all_to_all x1, blocking collectives: 29.1 us -> 27.1 us  [body(): lax.all_to_all(attended, 'uly', split_axis=0, concat_axis=1, tiled=True)]
    optimization_barrier x0 -> x1, local copies, waits for them, and re-layouts: none -> 1.87 us  [body(): lax.optimization_barrier((query_rows, left_key, right_key))]
    ppermute x4, starting transfers between devices: 9.39 us -> 11.1 us  [passed_along(): return lax.ppermute(block, axis, route)]
    unnamed x12 -> x15, local copies, waits for them, and re-layouts: 7.18 us -> 6.64 us
  transfers between devices with their start and end apart: 7 -> 7, of which waited for: 5 -> 6; matrix products, arithmetic and copies ran while one was open for 10% -> 8% of each run, Pallas kernels for 0% -> 0%
where the time goes in v7:
time: 157 us; the launch traced here: 156 us
  waiting for transfers between devices  47.2 us (30%)
  starting transfers between devices  29 us (18%)
  Pallas kernels  28.3 us (18%)
  blocking collectives  27.1 us (17%)
  local copies, waits for them, and re-layouts  17.6 us (11%)
  between operations  4.21 us (3%)
  other arithmetic  2.77 us (2%)
    pallas_call x1, Pallas kernels, attend(): pl.pallas_call(attend_kernel, grid_spec=grid_spec, out_shape=jax.ShapeDty...  28.3 us
    all_to_all x1, blocking collectives, body(): lax.all_to_all(attended, 'uly', split_axis=0, concat_axis=1, tiled=True)  27.1 us
    all_to_all x1, waiting for transfers between devices, body(): lax.all_to_all(key_rows, 'uly', split_axis=1, concat_axis=0, tiled=True)  20.9 us
    ppermute x4, waiting for transfers between devices, passed_along(): return lax.ppermute(block, axis, route)  15.1 us
    all_to_all x1, waiting for transfers between devices, body(): lax.all_to_all(query_rows[c * chunk:(c + 1) * chunk], 'uly', split_axis=1...  11.2 us
    ppermute x4, starting transfers between devices, passed_along(): return lax.ppermute(block, axis, route)  11.1 us
    all_to_all x1, starting transfers between devices, body(): lax.all_to_all(query_rows[c * chunk:(c + 1) * chunk], 'uly', split_axis=1...  7.15 us
    all_to_all x1, starting transfers between devices, body(): lax.all_to_all(key_rows, 'uly', split_axis=1, concat_axis=0, tiled=True)  7.03 us
  transfers between devices with their start and end apart: 7, of which 6 were waited for; matrix products, arithmetic and copies ran while one was open for 8% of the time, Pallas kernels for 0%

profile of v7, /device:TPU:192, one launch (start us, length us, event | category | flops | bytes accessed | tf_op | source)
XLA Modules:
  0.0 156.3 jit_solution(3829467480398020322)
XLA Ops:
  0.0 2.6 %copy.20 = bf16[384,2048]{0,1:T(8,128)(2,1)} copy(bf16[384,2048]{1,0:T(8,128)(2,1)} %param.5) | data formatting | bytes 3145728 | tf_op args[1]
  2.6 7.0 %all-to-all-start = ((bf16[384,16,128]{0,2,1:T(8,128)(2,1)}), bf16[384,16,128]{0,2,1:T(8,128)(2,1)S(1)}, u32[]{:S(2)}, u32[]{:S(2)}) async-start(bf16[384,16,128]{0,2,1:T(8,128)(2,1)} %bitcast.3), calls=%async_computation | async-start | bytes 3145728 | tf_op jit(solution)/shard_map/all_to_all | solution.py:121
  9.6 1.9 %copy.23 = bf16[384,2048]{0,1:T(8,128)(2,1)S(1)} copy(bf16[384,2048]{1,0:T(8,128)(2,1)} %param.6) | data formatting | bytes 3145728 | tf_op args[2]
  11.5 0.0 copy-start.3
  11.5 1.6 %copy.24 = bf16[384,16,128]{2,0,1:T(8,128)(2,1)} copy(bf16[384,16,128]{0,2,1:T(8,128)(2,1)S(1)} %bitcast.26) | data formatting | bytes 3145728 | tf_op jit(solution)/shard_map/all_to_all | solution.py:122
  13.2 0.0 copy-done.3
  13.2 20.9 %all-to-all-done = bf16[384,16,128]{0,2,1:T(8,128)(2,1)S(1)} async-done(((bf16[384,16,128]{0,2,1:T(8,128)(2,1)}), bf16[384,16,128]{0,2,1:T(8,128)(2,1)S(1)}, u32[]{:S(2)}, u32[]{:S(2)}) %all-to-all-start) | async-done | bytes 1572896 | tf_op jit(solution)/shard_map/all_to_all | solution.py:121
  34.1 0.0 copy-start
  34.1 3.7 %all-to-all-start.2 = ((bf16[384,16,128]{2,0,1:T(8,128)(2,1)}), bf16[384,16,128]{2,0,1:T(8,128)(2,1)S(1)}, u32[]{:S(2)}, u32[]{:S(2)}) async-start(bf16[384,16,128]{2,0,1:T(8,128)(2,1)} %copy.24), calls=%async_computation.2 | async-start | bytes 3145728 | tf_op jit(solution)/shard_map/all_to_all | solution.py:122
  37.9 0.2 select_reduce_fusion.1
  38.1 0.7 fusion.6
  40.2 0.6 fusion.5
  43.4 0.0 copy-done
  43.4 0.2 dynamic-slice_bitcast_fusion.2
  43.6 1.9 %collective-permute-start = (bf16[8,128,384]{2,1,0:T(8,128)(2,1)S(1)}, bf16[8,128,384]{2,1,0:T(8,128)(2,1)S(1)}, u32[]{:S(2)}, u32[]{:S(2)}) collective-permute-start(bf16[8,128,384]{2,1,0:T(8,128)(2,1)S(1)} %get-tuple-element.18), channel_id=1, source_target_pairs={{0,1},{1,2},{2,3},{3,4},{4,5},{5,6},{6,7},{7,8},{8,9},{9,10},{10,1... | collective-permute-start | bytes 2359304 | tf_op jit(solution)/shard_map/ppermute | solution.py:22
  45.5 3.6 %collective-permute-start.1 = (bf16[8,128,384]{2,1,0:T(8,128)(2,1)S(1)}, bf16[8,128,384]{2,1,0:T(8,128)(2,1)}, u32[]{:S(2)}, u32[]{:S(2)}) collective-permute-start(bf16[8,128,384]{2,1,0:T(8,128)(2,1)S(1)} %get-tuple-element.17), channel_id=1, source_target_pairs={{1,0},{2,1},{3,2},{4,3},{5,4},{6,5},{7,6},{8,7},{9,8},{10,9},{11,1... | collective-permute-start | bytes 2359304 | tf_op jit(solution)/shard_map/ppermute | solution.py:22
  49.2 7.7 %collective-permute-done.kl_ref = bf16[8,128,384]{2,1,0:T(8,128)(2,1)S(1)} collective-permute-done((bf16[8,128,384]{2,1,0:T(8,128)(2,1)S(1)}, bf16[8,128,384]{2,1,0:T(8,128)(2,1)S(1)}, u32[]{:S(2)}, u32[]{:S(2)}) %collective-permute-start) | collective-permute-done | bytes 786464 | tf_op jit(solution)/shard_map/ppermute | solution.py:22
  56.9 0.0 copy-start.4
  56.9 0.9 copy-done.4
  57.8 0.9 collective-permute-done.1.kr_ref
  58.7 1.9 %copy.21 = bf16[384,2048]{0,1:T(8,128)(2,1)S(1)} copy(bf16[384,2048]{1,0:T(8,128)(2,1)} %param.4) | data formatting | bytes 3145728 | tf_op jit(solution)/shard_map/optimization_barrier | solution.py:164
  60.6 1.6 %copy.22 = bf16[384,16,128]{2,0,1:T(8,128)(2,1)} copy(bf16[384,16,128]{0,2,1:T(8,128)(2,1)S(1)} %bitcast.27) | data formatting | bytes 3145728 | tf_op jit(solution)/shard_map/all_to_all | solution.py:167
  62.2 0.0 all-to-all-done.2
  62.2 0.0 copy-start.1
  62.2 7.2 %all-to-all-start.1 = ((bf16[384,16,128]{2,0,1:T(8,128)(2,1)}), bf16[384,16,128]{2,0,1:T(8,128)(2,1)S(1)}, u32[]{:S(2)}, u32[]{:S(2)}) async-start(bf16[384,16,128]{2,0,1:T(8,128)(2,1)} %copy.22), calls=%async_computation.1 | async-start | bytes 3145728 | tf_op jit(solution)/shard_map/all_to_all | solution.py:167
  69.3 0.0 copy-done.1
  69.4 1.3 dynamic-slice_bitcast_fusion
  70.6 3.0 %collective-permute-start.2 = (bf16[8,384,128]{2,1,0:T(8,128)(2,1)}, bf16[8,384,128]{2,1,0:T(8,128)(2,1)S(1)}, u32[]{:S(2)}, u32[]{:S(2)}) collective-permute-start(bf16[8,384,128]{2,1,0:T(8,128)(2,1)} %get-tuple-element.16), channel_id=1, source_target_pairs={{0,1},{1,2},{2,3},{3,4},{4,5},{5,6},{6,7},{7,8},{8,9},{9,10},{10,1... | collective-permute-start | bytes 2359304 | tf_op jit(solution)/shard_map/ppermute | solution.py:22
  73.7 2.5 %collective-permute-start.3 = (bf16[8,384,128]{2,1,0:T(8,128)(2,1)}, bf16[8,384,128]{2,1,0:T(8,128)(2,1)}, u32[]{:S(2)}, u32[]{:S(2)}) collective-permute-start(bf16[8,384,128]{2,1,0:T(8,128)(2,1)} %get-tuple-element.15), channel_id=1, source_target_pairs={{1,0},{2,1},{3,2},{4,3},{5,4},{6,5},{7,6},{8,7},{9,8},{10,9},{11,1... | collective-permute-start | bytes 2359304 | tf_op jit(solution)/shard_map/ppermute | solution.py:22
  76.2 0.1 copy.19
  76.4 0.6 gather_fusion
  76.9 0.7 convert_reduce_fusion
  77.6 0.1 select_n.122
  77.7 1.8 %compare_select_fusion.9 = (s32[96]{0:T(128)}, s32[96]{0:T(128)}) fusion(s32[96]{0:T(128)S(1)} %select_n.122, s32[]{:T(128)} %bitcast.2, s32[]{:T(128)} %bitcast.1, s32[]{:T(128)S(6)} %axis_index.12), kind=kLoop, calls=%fused_computation.33 | loop fusion | flops 2976 | bytes 1164 | tf_op jit(solution)/shard_map/jit(_where)/select_n | solution.py:160
  79.5 4.6 %collective-permute-done.2.vl_ref = bf16[8,384,128]{2,1,0:T(8,128)(2,1)S(1)} collective-permute-done((bf16[8,384,128]{2,1,0:T(8,128)(2,1)}, bf16[8,384,128]{2,1,0:T(8,128)(2,1)S(1)}, u32[]{:S(2)}, u32[]{:S(2)}) %collective-permute-start.2) | collective-permute-done | bytes 786464 | tf_op jit(solution)/shard_map/ppermute | solution.py:22
  84.1 0.0 copy-start.5
  84.1 1.9 %collective-permute-done.3.vr_ref = bf16[8,384,128]{2,1,0:T(8,128)(2,1)} collective-permute-done((bf16[8,384,128]{2,1,0:T(8,128)(2,1)}, bf16[8,384,128]{2,1,0:T(8,128)(2,1)}, u32[]{:S(2)}, u32[]{:S(2)}) %collective-permute-start.3) | collective-permute-done | bytes 786464 | tf_op jit(solution)/shard_map/ppermute | solution.py:22
  86.0 11.2 %all-to-all-done.1 = bf16[384,16,128]{2,0,1:T(8,128)(2,1)S(1)} async-done(((bf16[384,16,128]{2,0,1:T(8,128)(2,1)}), bf16[384,16,128]{2,0,1:T(8,128)(2,1)S(1)}, u32[]{:S(2)}, u32[]{:S(2)}) %all-to-all-start.1) | async-done | bytes 1572896 | tf_op jit(solution)/shard_map/all_to_all | solution.py:167
  97.2 0.0 copy-start.2
  97.2 0.0 copy-done.5
  97.2 1.1 copy-done.2
  98.3 28.3 %shard_map.46 = bf16[16,384,128]{2,1,0:T(8,128)(2,1)} custom-call(s32[96]{0:T(128)} %get-tuple-element.26.which_ref, s32[96]{0:T(128)} %get-tuple-element.25.index_ref, s32[16]{0:T(128)} %get-tuple-element.13.count_ref, bf16[16,384,128]{2,1,0:T(8,128)(2,1)} %bitcast.28, bf16[8,128,384]{2,1,0:T(8,128)(2,1)} %copy-done.4, bf16[16,128,384]{2,1,0:T(8,128)(2,1)} %bitcast.22, ...), custom_call_target="tpu_custom_call" | custom-call | flops 7247757312 | bytes 9437184 | tf_op jit(solution)/shard_map/pallas_call | solution.py:110
  126.7 27.1 %all_to_all.61 = bf16[16,384,128]{2,1,0:T(8,128)(2,1)S(1)} all-to-all(bf16[16,384,128]{2,1,0:T(8,128)(2,1)} %shard_map.46), channel_id=1, replica_groups=mesh['uly'=16,'blk'=16] {'uly'}, dimensions={0} | all-to-all | bytes 3145728 | tf_op jit(solution)/shard_map/all_to_all | solution.py:175
  153.8 0.9 copy.25
  154.6 1.6 %copy.26 = bf16[384,2048]{1,0:T(8,128)(2,1)} copy(bf16[384,2048]{0,1:T(8,128)(2,1)S(1)} %bitcast.25) | data formatting | bytes 3145728 | tf_op jit(solution)/shard_map/all_to_all | solution.py:175
  (9 shorter events, 0.1 us)
Async XLA Ops:
  2.6 31.6 %all-to-all-start = ((bf16[384,16,128]{0,2,1:T(8,128)(2,1)}), bf16[384,16,128]{0,2,1:T(8,128)(2,1)S(1)}, u32[]{:S(2)}, u32[]{:S(2)}) async-start(bf16[384,16,128]{0,2,1:T(8,128)(2,1)} %bitcast.3), calls=%async_computation | async-start | bytes 3145728 | tf_op jit(solution)/shard_map/all_to_all | solution.py:121
  11.5 1.7 %copy-start.3 = (s32[256,6]{0,1:T(8,128)S(1)}, s32[256,6]{0,1:T(8,128)}, u32[]{:S(2)}) copy-start(s32[256,6]{0,1:T(8,128)} %param.7) | copy-start | bytes 18436
  34.1 9.3 %copy-start = (bf16[384,16,128]{0,2,1:T(8,128)(2,1)}, bf16[384,16,128]{0,2,1:T(8,128)(2,1)S(1)}, u32[]{:S(2)}) copy-start(bf16[384,16,128]{0,2,1:T(8,128)(2,1)S(1)} %all-to-all-done) | copy-start | bytes 4718596
  34.1 28.0 %all-to-all-start.2 = ((bf16[384,16,128]{2,0,1:T(8,128)(2,1)}), bf16[384,16,128]{2,0,1:T(8,128)(2,1)S(1)}, u32[]{:S(2)}, u32[]{:S(2)}) async-start(bf16[384,16,128]{2,0,1:T(8,128)(2,1)} %copy.24), calls=%async_computation.2 | async-start | bytes 3145728 | tf_op jit(solution)/shard_map/all_to_all | solution.py:122
  43.6 13.3 %collective-permute-start = (bf16[8,128,384]{2,1,0:T(8,128)(2,1)S(1)}, bf16[8,128,384]{2,1,0:T(8,128)(2,1)S(1)}, u32[]{:S(2)}, u32[]{:S(2)}) collective-permute-start(bf16[8,128,384]{2,1,0:T(8,128)(2,1)S(1)} %get-tuple-element.18), channel_id=1, source_target_pairs={{0,1},{1,2},{2,3},{3,4},{4,5},{5,6},{6,7},{7,8},{8,9},{9,10},{10,1... | collective-permute-start | bytes 2359304 | tf_op jit(solution)/shard_map/ppermute | solution.py:22
  45.5 13.1 %collective-permute-start.1 = (bf16[8,128,384]{2,1,0:T(8,128)(2,1)S(1)}, bf16[8,128,384]{2,1,0:T(8,128)(2,1)}, u32[]{:S(2)}, u32[]{:S(2)}) collective-permute-start(bf16[8,128,384]{2,1,0:T(8,128)(2,1)S(1)} %get-tuple-element.17), channel_id=1, source_target_pairs={{1,0},{2,1},{3,2},{4,3},{5,4},{6,5},{7,6},{8,7},{9,8},{10,9},{11,1... | collective-permute-start | bytes 2359304 | tf_op jit(solution)/shard_map/ppermute | solution.py:22
  56.9 0.9 copy-start.4
  62.2 7.2 %copy-start.1 = (bf16[384,16,128]{2,0,1:T(8,128)(2,1)}, bf16[384,16,128]{2,0,1:T(8,128)(2,1)S(1)}, u32[]{:S(2)}) copy-start(bf16[384,16,128]{2,0,1:T(8,128)(2,1)S(1)} %all-to-all-done.2) | copy-start | bytes 4718596
  62.2 35.0 %all-to-all-start.1 = ((bf16[384,16,128]{2,0,1:T(8,128)(2,1)}), bf16[384,16,128]{2,0,1:T(8,128)(2,1)S(1)}, u32[]{:S(2)}, u32[]{:S(2)}) async-start(bf16[384,16,128]{2,0,1:T(8,128)(2,1)} %copy.22), calls=%async_computation.1 | async-start | bytes 3145728 | tf_op jit(solution)/shard_map/all_to_all | solution.py:167
  70.6 13.5 %collective-permute-start.2 = (bf16[8,384,128]{2,1,0:T(8,128)(2,1)}, bf16[8,384,128]{2,1,0:T(8,128)(2,1)S(1)}, u32[]{:S(2)}, u32[]{:S(2)}) collective-permute-start(bf16[8,384,128]{2,1,0:T(8,128)(2,1)} %get-tuple-element.16), channel_id=1, source_target_pairs={{0,1},{1,2},{2,3},{3,4},{4,5},{5,6},{6,7},{7,8},{8,9},{9,10},{10,1... | collective-permute-start | bytes 2359304 | tf_op jit(solution)/shard_map/ppermute | solution.py:22
  73.7 12.3 %collective-permute-start.3 = (bf16[8,384,128]{2,1,0:T(8,128)(2,1)}, bf16[8,384,128]{2,1,0:T(8,128)(2,1)}, u32[]{:S(2)}, u32[]{:S(2)}) collective-permute-start(bf16[8,384,128]{2,1,0:T(8,128)(2,1)} %get-tuple-element.15), channel_id=1, source_target_pairs={{1,0},{2,1},{3,2},{4,3},{5,4},{6,5},{7,6},{8,7},{9,8},{10,9},{11,1... | collective-permute-start | bytes 2359304 | tf_op jit(solution)/shard_map/ppermute | solution.py:22
  84.1 13.1 %copy-start.5 = (bf16[8,384,128]{2,1,0:T(8,128)(2,1)}, bf16[8,384,128]{2,1,0:T(8,128)(2,1)S(1)}, u32[]{:S(2)}) copy-start(bf16[8,384,128]{2,1,0:T(8,128)(2,1)S(1)} %collective-permute-done.2.vl_ref) | copy-start | bytes 2359300
  97.2 1.1 copy-start.2

commit v8 on v5

--- a/solution.py
+++ b/solution.py
@@ -161,11 +161,13 @@
     which = jnp.where(is_live, which, 1)
     count = jnp.sum(is_live.astype(jnp.int32), axis=1)
 
+    query_heads = jnp.transpose(query_rows.reshape(rows, n_uly, feat_width), (1, 0, 2))
+    query_heads, left_key, right_key = lax.optimization_barrier((query_heads, left_key, right_key))
     pieces = []
     for c in range(CHUNKS):
         query_part = lax.all_to_all(
-            query_rows[c * chunk:(c + 1) * chunk], "uly", split_axis=1, concat_axis=0, tiled=True
-        ).reshape(n_uly, chunk, feat_width)
+            query_heads[:, c * chunk:(c + 1) * chunk], "uly", split_axis=0, concat_axis=0, tiled=True
+        )
         attended = attend(
             which.reshape(-1), index.reshape(-1), count,
             query_part, left_key, key_tiles, right_key, left_value, value_tiles, right_value,

time: 158 us -> 155 us (0.981)
  waiting for transfers between devices: 50.1 us -> 46.3 us
  starting transfers between devices: 24.5 us -> 27.6 us
  blocking collectives: 29.1 us -> 27.1 us
    all_to_all x1, waiting for transfers between devices: 18 us -> 1.37 us  [body(): lax.all_to_all(value_rows, 'uly', split_axis=1, concat_axis=0, tiled=True)]
    all_to_all x1, waiting for transfers between devices: 3.06 us -> 11.3 us  [body(): lax.all_to_all(query_heads[:, c * chunk:(c + 1) * chunk], 'uly', split_ax...]
    ppermute x4, waiting for transfers between devices: 7.99 us -> 12.6 us  [passed_along(): return lax.ppermute(block, axis, route)]
    all_to_all x1 -> x0, local copies, waits for them, and re-layouts: 2.59 us -> none  [body(): lax.all_to_all(query_rows[c * chunk:(c + 1) * chunk], 'uly', split_axis=1...]
    all_to_all x1, blocking collectives: 29.1 us -> 27.1 us  [body(): lax.all_to_all(attended, 'uly', split_axis=0, concat_axis=1, tiled=True)]
    ppermute x4, starting transfers between devices: 9.39 us -> 11.1 us  [passed_along(): return lax.ppermute(block, axis, route)]
    reshape x0 -> x1, local copies, waits for them, and re-layouts: none -> 1.62 us  [body(): query_rows.reshape(rows, n_uly, feat_width)]
    unnamed x12 -> x14, local copies, waits for them, and re-layouts: 7.18 us -> 7.62 us
  transfers between devices with their start and end apart: 7 -> 7, of which waited for: 5 -> 7; matrix products, arithmetic and copies ran while one was open for 10% -> 9% of each run, Pallas kernels for 0% -> 0%
where the time goes in v8:
time: 155 us; the launch traced here: 154 us
  waiting for transfers between devices  46.3 us (30%)
  Pallas kernels  28.3 us (18%)
  starting transfers between devices  27.6 us (18%)
  blocking collectives  27.1 us (17%)
  local copies, waits for them, and re-layouts  17.9 us (12%)
  between operations  3.8 us (2%)
  other arithmetic  2.91 us (2%)
    pallas_call x1, Pallas kernels, attend(): pl.pallas_call(attend_kernel, grid_spec=grid_spec, out_shape=jax.ShapeDty...  28.3 us
    all_to_all x1, blocking collectives, body(): lax.all_to_all(attended, 'uly', split_axis=0, concat_axis=1, tiled=True)  27.1 us
    all_to_all x1, waiting for transfers between devices, body(): lax.all_to_all(key_rows, 'uly', split_axis=1, concat_axis=0, tiled=True)  20.9 us
    ppermute x4, waiting for transfers between devices, passed_along(): return lax.ppermute(block, axis, route)  12.6 us
    all_to_all x1, waiting for transfers between devices, body(): lax.all_to_all(query_heads[:, c * chunk:(c + 1) * chunk], 'uly', split_ax...  11.3 us
    ppermute x4, starting transfers between devices, passed_along(): return lax.ppermute(block, axis, route)  11.1 us
    unnamed x14, local copies, waits for them, and re-layouts  7.62 us
    all_to_all x1, starting transfers between devices, body(): lax.all_to_all(key_rows, 'uly', split_axis=1, concat_axis=0, tiled=True)  7.03 us
  transfers between devices with their start and end apart: 7, of which 7 were waited for; matrix products, arithmetic and copies ran while one was open for 9% of the time, Pallas kernels for 0%

profile of v8, /device:TPU:192, one launch (start us, length us, event | category | flops | bytes accessed | tf_op | source)
XLA Modules:
  0.0 153.9 jit_solution(3409424620090136572)
XLA Ops:
  0.0 2.6 %copy.22 = bf16[384,2048]{0,1:T(8,128)(2,1)} copy(bf16[384,2048]{1,0:T(8,128)(2,1)} %param.5) | data formatting | bytes 3145728 | tf_op args[1]
  2.6 7.0 %all-to-all-start = ((bf16[384,16,128]{0,2,1:T(8,128)(2,1)}), bf16[384,16,128]{0,2,1:T(8,128)(2,1)S(1)}, u32[]{:S(2)}, u32[]{:S(2)}) async-start(bf16[384,16,128]{0,2,1:T(8,128)(2,1)} %bitcast.5), calls=%async_computation | async-start | bytes 3145728 | tf_op jit(solution)/shard_map/all_to_all | solution.py:121
  9.6 1.9 %copy.23 = bf16[384,2048]{0,1:T(8,128)(2,1)S(1)} copy(bf16[384,2048]{1,0:T(8,128)(2,1)} %param.6) | data formatting | bytes 3145728 | tf_op args[2]
  11.5 0.0 copy-start.3
  11.5 1.6 %copy.24 = bf16[384,16,128]{2,0,1:T(8,128)(2,1)} copy(bf16[384,16,128]{0,2,1:T(8,128)(2,1)S(1)} %bitcast.26) | data formatting | bytes 3145728 | tf_op jit(solution)/shard_map/all_to_all | solution.py:122
  13.2 0.0 copy-done.3
  13.2 20.9 %all-to-all-done = bf16[384,16,128]{0,2,1:T(8,128)(2,1)S(1)} async-done(((bf16[384,16,128]{0,2,1:T(8,128)(2,1)}), bf16[384,16,128]{0,2,1:T(8,128)(2,1)S(1)}, u32[]{:S(2)}, u32[]{:S(2)}) %all-to-all-start) | async-done | bytes 1572896 | tf_op jit(solution)/shard_map/all_to_all | solution.py:121
  34.1 0.0 copy-start
  34.1 3.7 %all-to-all-start.2 = ((bf16[384,16,128]{2,0,1:T(8,128)(2,1)}), bf16[384,16,128]{2,0,1:T(8,128)(2,1)S(1)}, u32[]{:S(2)}, u32[]{:S(2)}) async-start(bf16[384,16,128]{2,0,1:T(8,128)(2,1)} %copy.24), calls=%async_computation.2 | async-start | bytes 3145728 | tf_op jit(solution)/shard_map/all_to_all | solution.py:122
  37.9 0.2 select_reduce_fusion.1
  38.1 0.6 fusion.6
  39.8 0.7 fusion.5
  43.0 0.0 copy-done
  43.0 1.3 dynamic-slice_bitcast_fusion.2
  44.4 1.9 %collective-permute-start = (bf16[8,128,384]{2,1,0:T(8,128)(2,1)}, bf16[8,128,384]{2,1,0:T(8,128)(2,1)}, u32[]{:S(2)}, u32[]{:S(2)}) collective-permute-start(bf16[8,128,384]{2,1,0:T(8,128)(2,1)} %get-tuple-element.18), channel_id=1, source_target_pairs={{0,1},{1,2},{2,3},{3,4},{4,5},{5,6},{6,7},{7,8},{8,9},{9,10},{10,1... | collective-permute-start | bytes 2359304 | tf_op jit(solution)/shard_map/ppermute | solution.py:22
  46.3 3.6 %collective-permute-start.1 = (bf16[8,128,384]{2,1,0:T(8,128)(2,1)}, bf16[8,128,384]{2,1,0:T(8,128)(2,1)}, u32[]{:S(2)}, u32[]{:S(2)}) collective-permute-start(bf16[8,128,384]{2,1,0:T(8,128)(2,1)} %get-tuple-element.17), channel_id=1, source_target_pairs={{1,0},{2,1},{3,2},{4,3},{5,4},{6,5},{7,6},{8,7},{9,8},{10,9},{11,1... | collective-permute-start | bytes 2359304 | tf_op jit(solution)/shard_map/ppermute | solution.py:22
  49.9 1.9 %copy.20 = bf16[384,2048]{0,1:T(8,128)(2,1)S(1)} copy(bf16[384,2048]{1,0:T(8,128)(2,1)} %param.4) | data formatting | bytes 3145728 | tf_op args[0]
  51.8 1.6 %copy.21 = bf16[384,16,128]{2,0,1:T(8,128)(2,1)} copy(bf16[384,16,128]{0,2,1:T(8,128)(2,1)S(1)} %bitcast.27) | data formatting | bytes 3145728 | tf_op jit(solution)/shard_map/reshape | solution.py:164
  53.4 4.5 %collective-permute-done.kl_ref = bf16[8,128,384]{2,1,0:T(8,128)(2,1)} collective-permute-done((bf16[8,128,384]{2,1,0:T(8,128)(2,1)}, bf16[8,128,384]{2,1,0:T(8,128)(2,1)}, u32[]{:S(2)}, u32[]{:S(2)}) %collective-permute-start) | collective-permute-done | bytes 786464 | tf_op jit(solution)/shard_map/ppermute | solution.py:22
  58.0 1.8 %collective-permute-done.1.kr_ref = bf16[8,128,384]{2,1,0:T(8,128)(2,1)} collective-permute-done((bf16[8,128,384]{2,1,0:T(8,128)(2,1)}, bf16[8,128,384]{2,1,0:T(8,128)(2,1)}, u32[]{:S(2)}, u32[]{:S(2)}) %collective-permute-start.1) | collective-permute-done | bytes 786464 | tf_op jit(solution)/shard_map/ppermute | solution.py:22
  59.7 1.4 all-to-all-done.2
  61.1 0.0 copy-start.1
  61.1 5.8 %all-to-all-start.1 = ((bf16[16,384,128]{2,1,0:T(8,128)(2,1)}), bf16[16,384,128]{2,1,0:T(8,128)(2,1)S(1)}, u32[]{:S(2)}, u32[]{:S(2)}) async-start(bf16[16,384,128]{2,1,0:T(8,128)(2,1)} %bitcast.4), calls=%async_computation.1 | async-start | bytes 3145728 | tf_op jit(solution)/shard_map/all_to_all | solution.py:168
  66.9 1.3 dynamic-slice_bitcast_fusion
  68.2 0.0 copy-done.1
  68.2 2.9 %collective-permute-start.2 = (bf16[8,384,128]{2,1,0:T(8,128)(2,1)}, bf16[8,384,128]{2,1,0:T(8,128)(2,1)S(1)}, u32[]{:S(2)}, u32[]{:S(2)}) collective-permute-start(bf16[8,384,128]{2,1,0:T(8,128)(2,1)} %get-tuple-element.16), channel_id=1, source_target_pairs={{0,1},{1,2},{2,3},{3,4},{4,5},{5,6},{6,7},{7,8},{8,9},{9,10},{10,1... | collective-permute-start | bytes 2359304 | tf_op jit(solution)/shard_map/ppermute | solution.py:22
  71.1 2.6 %collective-permute-start.3 = (bf16[8,384,128]{2,1,0:T(8,128)(2,1)}, bf16[8,384,128]{2,1,0:T(8,128)(2,1)}, u32[]{:S(2)}, u32[]{:S(2)}) collective-permute-start(bf16[8,384,128]{2,1,0:T(8,128)(2,1)} %get-tuple-element.15), channel_id=1, source_target_pairs={{1,0},{2,1},{3,2},{4,3},{5,4},{6,5},{7,6},{8,7},{9,8},{10,9},{11,1... | collective-permute-start | bytes 2359304 | tf_op jit(solution)/shard_map/ppermute | solution.py:22
  73.7 0.1 copy.19
  73.9 0.6 gather_fusion
  74.5 0.8 convert_reduce_fusion
  75.2 0.1 select_n.122
  75.3 1.9 %compare_select_fusion.9 = (s32[96]{0:T(128)}, s32[96]{0:T(128)}) fusion(s32[96]{0:T(128)S(1)} %select_n.122, s32[]{:T(128)} %bitcast.2, s32[]{:T(128)} %bitcast.1, s32[]{:T(128)S(6)} %axis_index.12), kind=kLoop, calls=%fused_computation.33 | loop fusion | flops 2976 | bytes 1164 | tf_op jit(solution)/shard_map/jit(_where)/select_n | solution.py:160
  77.2 4.5 %collective-permute-done.2.vl_ref = bf16[8,384,128]{2,1,0:T(8,128)(2,1)S(1)} collective-permute-done((bf16[8,384,128]{2,1,0:T(8,128)(2,1)}, bf16[8,384,128]{2,1,0:T(8,128)(2,1)S(1)}, u32[]{:S(2)}, u32[]{:S(2)}) %collective-permute-start.2) | collective-permute-done | bytes 786464 | tf_op jit(solution)/shard_map/ppermute | solution.py:22
  81.7 0.0 copy-start.4
  81.7 1.9 %collective-permute-done.3.vr_ref = bf16[8,384,128]{2,1,0:T(8,128)(2,1)} collective-permute-done((bf16[8,384,128]{2,1,0:T(8,128)(2,1)}, bf16[8,384,128]{2,1,0:T(8,128)(2,1)}, u32[]{:S(2)}, u32[]{:S(2)}) %collective-permute-start.3) | collective-permute-done | bytes 786464 | tf_op jit(solution)/shard_map/ppermute | solution.py:22
  83.5 11.3 %all-to-all-done.1.q_ref = bf16[16,384,128]{2,1,0:T(8,128)(2,1)S(1)} async-done(((bf16[16,384,128]{2,1,0:T(8,128)(2,1)}), bf16[16,384,128]{2,1,0:T(8,128)(2,1)S(1)}, u32[]{:S(2)}, u32[]{:S(2)}) %all-to-all-start.1) | async-done | bytes 1572896 | tf_op jit(solution)/shard_map/all_to_all | solution.py:168
  94.9 0.0 copy-start.2
  94.9 0.0 copy-done.4
  94.9 1.1 copy-done.2
  96.0 28.3 %shard_map.46 = bf16[16,384,128]{2,1,0:T(8,128)(2,1)} custom-call(s32[96]{0:T(128)} %get-tuple-element.26.which_ref, s32[96]{0:T(128)} %get-tuple-element.25.index_ref, s32[16]{0:T(128)} %get-tuple-element.13.count_ref, bf16[16,384,128]{2,1,0:T(8,128)(2,1)} %copy-done.2, bf16[8,128,384]{2,1,0:T(8,128)(2,1)} %collective-permute-done.kl_ref, ...), custom_call_target="tpu_custom_call" | custom-call | flops 7247757312 | bytes 9437184 | tf_op jit(solution)/shard_map/pallas_call | solution.py:110
  124.3 27.1 %all_to_all.50 = bf16[16,384,128]{2,1,0:T(8,128)(2,1)S(1)} all-to-all(bf16[16,384,128]{2,1,0:T(8,128)(2,1)} %shard_map.46), channel_id=1, replica_groups=mesh['uly'=16,'blk'=16] {'uly'}, dimensions={0} | all-to-all | bytes 3145728 | tf_op jit(solution)/shard_map/all_to_all | solution.py:176
  151.4 0.9 copy.25
  152.3 1.6 %copy.26 = bf16[384,2048]{1,0:T(8,128)(2,1)} copy(bf16[384,2048]{0,1:T(8,128)(2,1)S(1)} %bitcast.25) | data formatting | bytes 3145728 | tf_op jit(solution)/shard_map/all_to_all | solution.py:176
  (9 shorter events, 0.1 us)
Async XLA Ops:
  2.6 31.6 %all-to-all-start = ((bf16[384,16,128]{0,2,1:T(8,128)(2,1)}), bf16[384,16,128]{0,2,1:T(8,128)(2,1)S(1)}, u32[]{:S(2)}, u32[]{:S(2)}) async-start(bf16[384,16,128]{0,2,1:T(8,128)(2,1)} %bitcast.5), calls=%async_computation | async-start | bytes 3145728 | tf_op jit(solution)/shard_map/all_to_all | solution.py:121
  11.5 1.7 %copy-start.3 = (s32[256,6]{0,1:T(8,128)S(1)}, s32[256,6]{0,1:T(8,128)}, u32[]{:S(2)}) copy-start(s32[256,6]{0,1:T(8,128)} %param.7) | copy-start | bytes 18436
  34.1 8.9 %copy-start = (bf16[384,16,128]{0,2,1:T(8,128)(2,1)}, bf16[384,16,128]{0,2,1:T(8,128)(2,1)S(1)}, u32[]{:S(2)}) copy-start(bf16[384,16,128]{0,2,1:T(8,128)(2,1)S(1)} %all-to-all-done) | copy-start | bytes 4718596
  34.1 27.0 %all-to-all-start.2 = ((bf16[384,16,128]{2,0,1:T(8,128)(2,1)}), bf16[384,16,128]{2,0,1:T(8,128)(2,1)S(1)}, u32[]{:S(2)}, u32[]{:S(2)}) async-start(bf16[384,16,128]{2,0,1:T(8,128)(2,1)} %copy.24), calls=%async_computation.2 | async-start | bytes 3145728 | tf_op jit(solution)/shard_map/all_to_all | solution.py:122
  44.4 13.6 %collective-permute-start = (bf16[8,128,384]{2,1,0:T(8,128)(2,1)}, bf16[8,128,384]{2,1,0:T(8,128)(2,1)}, u32[]{:S(2)}, u32[]{:S(2)}) collective-permute-start(bf16[8,128,384]{2,1,0:T(8,128)(2,1)} %get-tuple-element.18), channel_id=1, source_target_pairs={{0,1},{1,2},{2,3},{3,4},{4,5},{5,6},{6,7},{7,8},{8,9},{9,10},{10,1... | collective-permute-start | bytes 2359304 | tf_op jit(solution)/shard_map/ppermute | solution.py:22
  46.3 13.5 %collective-permute-start.1 = (bf16[8,128,384]{2,1,0:T(8,128)(2,1)}, bf16[8,128,384]{2,1,0:T(8,128)(2,1)}, u32[]{:S(2)}, u32[]{:S(2)}) collective-permute-start(bf16[8,128,384]{2,1,0:T(8,128)(2,1)} %get-tuple-element.17), channel_id=1, source_target_pairs={{1,0},{2,1},{3,2},{4,3},{5,4},{6,5},{7,6},{8,7},{9,8},{10,9},{11,1... | collective-permute-start | bytes 2359304 | tf_op jit(solution)/shard_map/ppermute | solution.py:22
  61.1 7.1 %copy-start.1 = (bf16[384,16,128]{2,0,1:T(8,128)(2,1)}, bf16[384,16,128]{2,0,1:T(8,128)(2,1)S(1)}, u32[]{:S(2)}) copy-start(bf16[384,16,128]{2,0,1:T(8,128)(2,1)S(1)} %all-to-all-done.2) | copy-start | bytes 4718596
  61.1 33.7 %all-to-all-start.1 = ((bf16[16,384,128]{2,1,0:T(8,128)(2,1)}), bf16[16,384,128]{2,1,0:T(8,128)(2,1)S(1)}, u32[]{:S(2)}, u32[]{:S(2)}) async-start(bf16[16,384,128]{2,1,0:T(8,128)(2,1)} %bitcast.4), calls=%async_computation.1 | async-start | bytes 3145728 | tf_op jit(solution)/shard_map/all_to_all | solution.py:168
  68.2 13.5 %collective-permute-start.2 = (bf16[8,384,128]{2,1,0:T(8,128)(2,1)}, bf16[8,384,128]{2,1,0:T(8,128)(2,1)S(1)}, u32[]{:S(2)}, u32[]{:S(2)}) collective-permute-start(bf16[8,384,128]{2,1,0:T(8,128)(2,1)} %get-tuple-element.16), channel_id=1, source_target_pairs={{0,1},{1,2},{2,3},{3,4},{4,5},{5,6},{6,7},{7,8},{8,9},{9,10},{10,1... | collective-permute-start | bytes 2359304 | tf_op jit(solution)/shard_map/ppermute | solution.py:22
  71.1 12.5 %collective-permute-start.3 = (bf16[8,384,128]{2,1,0:T(8,128)(2,1)}, bf16[8,384,128]{2,1,0:T(8,128)(2,1)}, u32[]{:S(2)}, u32[]{:S(2)}) collective-permute-start(bf16[8,384,128]{2,1,0:T(8,128)(2,1)} %get-tuple-element.15), channel_id=1, source_target_pairs={{1,0},{2,1},{3,2},{4,3},{5,4},{6,5},{7,6},{8,7},{9,8},{10,9},{11,1... | collective-permute-start | bytes 2359304 | tf_op jit(solution)/shard_map/ppermute | solution.py:22
  81.7 13.2 %copy-start.4 = (bf16[8,384,128]{2,1,0:T(8,128)(2,1)}, bf16[8,384,128]{2,1,0:T(8,128)(2,1)S(1)}, u32[]{:S(2)}) copy-start(bf16[8,384,128]{2,1,0:T(8,128)(2,1)S(1)} %collective-permute-done.2.vl_ref) | copy-start | bytes 2359300
  94.9 1.1 copy-start.2
